TPU v7x, 32 devices: a whole 2x2x4 slice. The times are simulated.
32 devices in a mesh: rows: 8 (over y, x, core), cols: 4 (over z).
Axes of the slice: x: 2, y: 2, z: 4, core: 2. Of those that a mesh axis runs over, the one named last changes fastest.
Arguments:
- fields: bfloat16 [12, 64, 128, 4096], P(None, 'rows', 'cols'), may hold values from -110 to 110
- front_cells: int32 [32, 32, 4], P(('rows', 'cols')), may hold values from -1 to 2047, as said below
Outputs:
- front_tensors: bfloat16 [32, 33, 128], P(('rows', 'cols'))
Inputs may be any that keep to these rules, and one draw needn't show every extreme that they name: front_cells[s, d, n] is a cell number of device s's slab or -1 for an empty slot; the live slots of each (s, d) come first; in every draw some owner receives 4 cells from every device; a cell may go to several owners.
All inputs are finite; a program needn't handle non-finite values.
Results may differ from a plain program's by a relative error of at most 0.01.
Values may be sent and summed in bfloat16 or wider, within the bound.
No kernel may reach another device: no remote copies, remote signals or barrier semaphores. Data moves between devices by JAX's collectives and lax.ppermute only.
A program may use at most 192 MiB of HBM per device.

v0:
```python
import numpy as np
import jax
import jax.numpy as jnp
import ml_dtypes
from jax import lax
from jax.sharding import PartitionSpec as P
from jax.experimental import pallas as pl
from jax.experimental.pallas import tpu as pltpu

first_tap = -20
last_tap = 27
sigma_sq = 256.0 / 12.0
coarse_step = 8.0
model_coeff = 1.0 / 3.0
upper_pairs = ((0, 0), (0, 1), (0, 2), (1, 1), (1, 2), (2, 2))
block_len = 1024
halo = 128


def tap_weights(offsets):
    f32 = np.float32
    every_tap = np.arange(first_tap, last_tap + 1).astype(f32)
    weight_sum = np.sum(np.exp(-(every_tap - f32(3.5)) * (every_tap - f32(3.5)) / f32(2.0 * sigma_sq)), dtype=f32)
    shifted = offsets.astype(f32) - f32(3.5)
    inside = (offsets >= first_tap) & (offsets <= last_tap)
    gauss = np.where(inside, np.exp(-shifted * shifted / f32(2.0 * sigma_sq)), f32(0.0)).astype(f32) / weight_sum
    slope = (f32(-coarse_step) * shifted / f32(sigma_sq) * gauss).astype(f32)
    bf = ml_dtypes.bfloat16
    return gauss.astype(bf).astype(f32), slope.astype(bf).astype(f32)


def line_matrices(length):
    fine_pos = np.arange(length)[:, None]
    coarse_pos = np.arange(length // 8)[None, :]
    offsets = np.mod(fine_pos - 8 * coarse_pos, length)
    offsets = np.where(offsets >= length // 2, offsets - length, offsets)
    return tap_weights(offsets)


def z_tables(length):
    coarse = np.arange(length // 8)[None, :]
    main = np.arange(length)[:, None] - 8 * coarse
    prev = np.arange(halo)[:, None] - halo - 8 * coarse
    nxt = np.arange(halo)[:, None] + length - 8 * coarse
    return [tap_weights(o) for o in (main, prev, nxt)]


def filter_kernel(block_count, coarse_block, value_rows, slope_rows):
    def body(x_ref, main_ref, prev_ref, next_ref, wv_ref, ws_ref, o_ref, zv_ref, zs_ref):
        length = x_ref.shape[2]
        blen = length // block_count
        for b in range(block_count):
            main = x_ref[0, :, b * blen:(b + 1) * blen]
            start = (b * blen - halo) % length
            tail = x_ref[0, :, start:start + halo]
            start = ((b + 1) * blen) % length
            head = x_ref[0, :, start:start + halo]
            acc = jnp.dot(main, main_ref[...], preferred_element_type=jnp.float32)
            acc = acc + jnp.dot(tail, prev_ref[...], preferred_element_type=jnp.float32)
            acc = acc + jnp.dot(head, next_ref[...], preferred_element_type=jnp.float32)
            lanes = slice(b * coarse_block, (b + 1) * coarse_block)
            zv_ref[:, lanes] = acc[:, :coarse_block].astype(jnp.bfloat16)
            zs_ref[:, lanes] = acc[:, coarse_block:].astype(jnp.bfloat16)
        zv = zv_ref[...]
        zs = zs_ref[...]
        pv = jnp.dot(wv_ref[0], zv, preferred_element_type=jnp.float32)
        pv = pv + jnp.dot(wv_ref[1], zv, preferred_element_type=jnp.float32)
        ps = jnp.dot(ws_ref[0], zs, preferred_element_type=jnp.float32)
        ps = ps + jnp.dot(ws_ref[1], zs, preferred_element_type=jnp.float32)
        o_ref[0, :value_rows, :] = pv
        o_ref[0, value_rows:, :] = ps

    return body


def split_hi_lo(w):
    hi = w.astype(jnp.bfloat16)
    lo = (w - hi.astype(jnp.float32)).astype(jnp.bfloat16)
    return jnp.stack([hi, lo], axis=0)


def filtered_partials(fields3, value_w, slope_w):
    field_count, rows, length = fields3.shape
    blen = block_len if (length % block_len == 0 and length > block_len) else length
    block_count = length // blen
    coarse_block = blen // 8
    tables = z_tables(blen)
    joined = [np.concatenate([t[0], t[1]], axis=1) for t in tables]
    main, prev, nxt = [jnp.asarray(t, jnp.bfloat16) for t in joined]
    wv = split_hi_lo(value_w)
    ws = split_hi_lo(slope_w)
    value_rows = wv.shape[1]
    slope_rows = ws.shape[1]
    total_rows = value_rows + slope_rows
    coarse = length // 8
    const = lambda f: (0, 0)
    const3 = lambda f: (0, 0, 0)
    return pl.pallas_call(
        filter_kernel(block_count, coarse_block, value_rows, slope_rows),
        out_shape=jax.ShapeDtypeStruct((field_count, total_rows, coarse), jnp.float32),
        grid=(field_count,),
        in_specs=[
            pl.BlockSpec((1, rows, length), lambda f: (f, 0, 0)),
            pl.BlockSpec(main.shape, const),
            pl.BlockSpec(prev.shape, const),
            pl.BlockSpec(nxt.shape, const),
            pl.BlockSpec(wv.shape, const3),
            pl.BlockSpec(ws.shape, const3),
        ],
        out_specs=pl.BlockSpec((1, total_rows, coarse), lambda f: (f, 0, 0)),
        scratch_shapes=[pltpu.VMEM((rows, coarse), jnp.bfloat16), pltpu.VMEM((rows, coarse), jnp.bfloat16)],
    )(fields3, main, prev, nxt, wv, ws)


def model_tensors(coarse):
    values = coarse.astype(jnp.float32)
    points = values.shape[-1]
    values = values.reshape(values.shape[0] // 3, 3, points)
    velocity = values[:3]
    species = values[3:]
    stress = [
        jnp.sum(velocity[first_comp] * velocity[second_comp], axis=0)
        for first_comp, second_comp in upper_pairs
    ]
    species_flux = jnp.sum(species[:, None, :, :] * velocity[None, :, :, :], axis=2)
    joined = jnp.concatenate([jnp.stack(stress, axis=0), species_flux.reshape(-1, points)], axis=0)
    return (model_coeff * joined).astype(jnp.bfloat16)


def window(at, count, coarse):
    reach = (count + 19) // 8 + 4
    if count % 8 or reach >= coarse:
        return 0, coarse
    return at * (count // 8) - 3, reach


def make_shards(row_count, col_count):
    def shards(fields, front_cells):
        field_count, local_x, local_y, z_length = fields.shape
        devices = row_count * col_count
        full_x = local_x * row_count
        full_y = local_y * col_count
        coarse_x = full_x // 8
        coarse_y = full_y // 8
        coarse_z = z_length // 8
        slab = coarse_z // devices
        slots = front_cells.shape[2]
        row = lax.axis_index("rows")
        col = lax.axis_index("cols")
        me = row * col_count + col

        every_cell = lax.all_gather(front_cells, ("rows", "cols"), axis=0, tiled=True)

        smooth_x, deriv_x = line_matrices(full_x)
        smooth_y, deriv_y = line_matrices(full_y)
        x_base, x_count = window(row, local_x, coarse_x)
        y_base, y_count = window(col, local_y, coarse_y)

        def local_rows(table, at, count, base, width, full):
            rows = lax.dynamic_slice_in_dim(jnp.asarray(table), at * count, count)
            picks = (base + jnp.arange(width)) % full
            return jnp.take(rows, picks, axis=1)

        ax = local_rows(smooth_x, row, local_x, x_base, x_count, coarse_x)
        bx = local_rows(deriv_x, row, local_x, x_base, x_count, coarse_x)
        ay = local_rows(smooth_y, col, local_y, y_base, y_count, coarse_y)
        by = local_rows(deriv_y, col, local_y, y_base, y_count, coarse_y)
        group = x_count * y_count
        padded = -(-group // 8) * 8

        def kron(wx, wy):
            joined = (wx[:, None, :, None] * wy[None, :, None, :]).reshape(local_x * local_y, group)
            return jnp.pad(joined, ((0, 0), (0, padded - group))).T

        value_w = jnp.concatenate([kron(bx, ay), kron(ax, by)], axis=0)
        slope_w = kron(ax, ay)
        fields3 = fields.reshape(field_count, local_x * local_y, z_length)
        partials = filtered_partials(fields3, value_w, slope_w)
        partials = partials.reshape(field_count, 3, padded, coarse_z)

        by_owner = jnp.transpose(every_cell, (1, 0, 2))
        holder = lax.broadcasted_iota(jnp.int32, by_owner.shape, 1)
        clipped = jnp.clip(by_owner, 0, coarse_x * coarse_y * slab - 1)
        cell_pq = clipped // slab
        at_z = holder * slab + clipped % slab
        at_x = (cell_pq // coarse_y - x_base) % coarse_x
        at_y = (cell_pq % coarse_y - y_base) % coarse_y
        inside = (at_x < x_count) & (at_y < y_count) & (by_owner >= 0)
        at_group = jnp.where(inside, at_x * y_count + at_y, 0)
        flat = (at_group * coarse_z + at_z).reshape(-1)
        table = jnp.transpose(partials, (2, 3, 0, 1)).reshape(padded * coarse_z, field_count * 3)
        taken = jnp.take(table, flat, axis=0)
        taken = jnp.where(inside.reshape(-1, 1), taken, jnp.zeros_like(taken))
        taken = taken.reshape(devices, -1, field_count * 3)
        arrived = lax.all_to_all(taken, ("rows", "cols"), split_axis=0, concat_axis=0, tiled=True)
        summed = jnp.sum(arrived.reshape(devices, -1, field_count * 3), axis=0).T
        rounded = lax.reduce_precision(summed, exponent_bits=8, mantissa_bits=7)
        mine = lax.dynamic_index_in_dim(by_owner, me, axis=0, keepdims=False).reshape(-1)
        picked = jnp.where(mine[None, :] >= 0, rounded, jnp.zeros_like(rounded))
        return model_tensors(picked)[None]

    return shards


def solution(mesh):
    in_specs = (P(None, "rows", "cols", None), P(("rows", "cols"), None, None))
    out_specs = P(("rows", "cols"), None, None)
    shards = make_shards(mesh.shape["rows"], mesh.shape["cols"])
    return jax.shard_map(shards, mesh=mesh, in_specs=in_specs, out_specs=out_specs, check_vma=False)
```

profile of v0, /device:TPU:1, one launch (start us, length us, event | category | flops | bytes accessed | tf_op | source)
XLA Modules:
  0.0 160.0 jit_solution(15797829803033889457)
XLA Ops:
  0.1 0.8 constant_dynamic-slice_fusion
  0.9 0.6 gather_fusion.2
  1.4 0.6 gather_fusion.4
  2.0 0.8 constant_dynamic-slice_fusion.1
  2.8 0.6 gather_fusion.3
  3.4 0.6 gather_fusion.1
  4.1 0.1 broadcast_multiply_fusion.1
  4.2 0.1 mul.140
  4.4 0.1 mul.138
  4.5 0.1 mul.134
  4.7 0.6 pad_maximum_fusion.2.ws_ref
  5.3 0.7 pad_maximum_fusion.1.wv_ref
  6.0 20.6 %shard_map.91 = f32[12,216,512]{2,1,0:T(8,128)} custom-call(bf16[12,256,4096]{2,1,0:T(8,128)(2,1)} %bitcast.96, bf16[1024,256]{1,0:T(8,128)(2,1)} %constant.173.clone.main_ref, bf16[128,256]{1,0:T(8,128)(2,1)} %constant.174.clone.prev_ref, bf16[128,256]{1,0:T(8,128)(2,1)} %constant.175.clone.next_ref, bf16[2,144,256]{2,1,0:T(8,128)(2,1)} %pad_maximum_fusion.1.wv_ref, ...), custom_call_target="tpu_custom_call" | custom-call | tf_op jit(solution)/shard_map/pallas_call | solution.py:98
  26.6 3.2 %pad.24 = f32[40,72,512]{2,1,0:T(8,128)S(1)} pad(f32[36,72,512]{2,1,0:T(8,128)} %bitcast.99, f32[]{:T(128)} %constant.166.clone.1), padding=0_4x0_0x0_0 | pad | bytes 11206660
  29.7 5.8 %copy.62 = f32[5,8,72,512]{3,1,2,0:T(8,128)} copy(f32[5,8,72,512]{3,2,1,0:T(8,128)S(1)} %bitcast.97) | data formatting | bytes 11796480
  35.5 11.9 %copy.48 = f32[36864,36]{1,0:T(8,128)} copy(f32[36864,36]{0,1:T(8,128)} %bitcast.98) | data formatting | bytes 10616832 | tf_op jit(solution)/shard_map/reshape | solution.py:191
  47.5 64.9 %all_gather.3 = s32[32,32,4]{1,2,0:T(4,128)S(1)} all-gather(s32[1,32,4]{1,2,0:T(4,128)S(1)} %copy-done), channel_id=1, replica_groups=mesh['rows'=8,'cols'=4] {'rows','cols'}, dimensions={0}, use_global_device_ids=true | all-gather | bytes 16896 | tf_op jit(solution)/shard_map/all_gather | solution.py:152
  112.4 0.4 fusion.7
  112.8 0.5 copy.47
  113.3 0.3 reshape.292
  113.7 17.1 %gather_fusion = f32[4096,36]{1,0:T(8,128)S(1)} fusion(f32[36864,36]{1,0:T(8,128)} %copy.48, s32[4096]{0:T(1024)S(1)} %broadcast_clamp_fusion), kind=kCustom, calls=%fused_computation.4 | custom fusion | bytes 1196032 | tf_op jit(solution)/shard_map/jit(_take)/gather | solution.py:192
  130.8 0.6 copy.49
  131.7 1.0 select_select_fusion
  132.7 7.5 %all-to-all-start = ((f32[32,128,36]{1,2,0:T(8,128)}), f32[32,128,36]{1,2,0:T(8,128)S(1)}, u32[]{:S(2)}, u32[]{:S(2)}) async-start(f32[32,128,36]{1,2,0:T(8,128)} %select_select_fusion), calls=%async_computation | async-start | bytes 1310720 | tf_op jit(solution)/shard_map/all_to_all | solution.py:195
  140.2 0.7 fusion.11
  140.9 0.1 ge.41
  141.0 17.4 %all-to-all-done = f32[32,128,36]{1,2,0:T(8,128)S(1)} async-done(((f32[32,128,36]{1,2,0:T(8,128)}), f32[32,128,36]{1,2,0:T(8,128)S(1)}, u32[]{:S(2)}, u32[]{:S(2)}) %all-to-all-start) | async-done | bytes 589856 | tf_op jit(solution)/shard_map/all_to_all | solution.py:195
  158.4 0.1 copy.53
  158.5 0.1 select_bitcast_fusion
  158.7 0.3 multiply_reduce_fusion
  159.2 0.2 concatenate.58
  159.4 0.6 multiply_convert_fusion
  (30 shorter events, 0.9 us)
Async XLA Ops:
  35.5 11.9 %copy-start = (s32[1,32,4]{1,2,0:T(4,128)S(1)}, s32[1,32,4]{1,2,0:T(4,128)}, u32[]{:S(2)}) copy-start(s32[1,32,4]{1,2,0:T(4,128)} %param.14) | copy-start | bytes 1540
  132.7 25.7 %all-to-all-start = ((f32[32,128,36]{1,2,0:T(8,128)}), f32[32,128,36]{1,2,0:T(8,128)S(1)}, u32[]{:S(2)}, u32[]{:S(2)}) async-start(f32[32,128,36]{1,2,0:T(8,128)} %select_select_fusion), calls=%async_computation | async-start | bytes 1310720 | tf_op jit(solution)/shard_map/all_to_all | solution.py:195
where the time goes:
time: 161 us; the launch traced here: 160 us
  blocking collectives  64.9 us (40%)
  local copies, waits for them, and re-layouts  44.5 us (28%)
  Pallas kernels  20.6 us (13%)
  waiting for transfers between devices  17.4 us (11%)
  starting transfers between devices  7.5 us (5%)
  other arithmetic  4.89 us (3%)
    all_gather x1, blocking collectives, shards(): lax.all_gather(front_cells, ('rows', 'cols'), axis=0, tiled=True)  64.9 us
    pallas_call x1, Pallas kernels, filtered_partials(): pl.pallas_call(filter_kernel(block_count, coarse_block, value_rows, slope...  20.6 us
    gather x2, local copies, waits for them, and re-layouts, shards(): taken = jnp.take(table, flat, axis=0)  17.8 us
    all_to_all x1, waiting for transfers between devices, shards(): lax.all_to_all(taken, ('rows', 'cols'), split_axis=0, concat_axis=0, tile...  17.4 us
    reshape x1, local copies, waits for them, and re-layouts, shards(): jnp.transpose(partials, (2, 3, 0, 1))  11.9 us
    unnamed x5, local copies, waits for them, and re-layouts  9.07 us
    all_to_all x1, starting transfers between devices, shards(): lax.all_to_all(taken, ('rows', 'cols'), split_axis=0, concat_axis=0, tile...  7.5 us
  transfers between devices with their start and end apart: 1, of which 1 were waited for; matrix products, arithmetic and copies ran while one was open for 1% of the time, Pallas kernels for 0%

commit v1 on v0

--- a/solution.py
+++ b/solution.py
@@ -149,7 +149,8 @@
         col = lax.axis_index("cols")
         me = row * col_count + col
 
-        every_cell = lax.all_gather(front_cells, ("rows", "cols"), axis=0, tiled=True)
+        copies = jnp.broadcast_to(front_cells, (devices,) + front_cells.shape[1:])
+        every_cell = lax.all_to_all(copies, ("rows", "cols"), split_axis=0, concat_axis=0, tiled=True)
 
         smooth_x, deriv_x = line_matrices(full_x)
         smooth_y, deriv_y = line_matrices(full_y)

time: 161 us -> 104 us (0.65)
  blocking collectives: 64.9 us -> 0 us
  starting transfers between devices: 7.5 us -> 12.9 us
  local copies, waits for them, and re-layouts: 44.5 us -> 46.5 us
    all_gather x1 -> x0, blocking collectives: 64.9 us -> none  [shards(): lax.all_gather(front_cells, ('rows', 'cols'), axis=0, tiled=True)]
    all_to_all x0 -> x1, starting transfers between devices: none -> 7.1 us  [shards(): lax.all_to_all(copies, ('rows', 'cols'), split_axis=0, concat_axis=0, til...]
    all_to_all x1, starting transfers between devices: 7.5 us -> 5.84 us  [shards(): lax.all_to_all(taken, ('rows', 'cols'), split_axis=0, concat_axis=0, tile...]
    unnamed x5 -> x10, local copies, waits for them, and re-layouts: 9.07 us -> 10.6 us
  transfers between devices with their start and end apart: 1 -> 2, of which waited for: 1 -> 1; matrix products, arithmetic and copies ran while one was open for 1% -> 27% of each run, Pallas kernels for 0% -> 20%
where the time goes in v1:
time: 104 us; the launch traced here: 103 us
  local copies, waits for them, and re-layouts  46.5 us (45%)
  Pallas kernels  20.6 us (20%)
  waiting for transfers between devices  17.2 us (17%)
  starting transfers between devices  12.9 us (12%)
  other arithmetic  5.57 us (5%)
    pallas_call x1, Pallas kernels, filtered_partials(): pl.pallas_call(filter_kernel(block_count, coarse_block, value_rows, slope...  20.6 us
    gather x2, local copies, waits for them, and re-layouts, shards(): taken = jnp.take(table, flat, axis=0)  17.8 us
    all_to_all x1, waiting for transfers between devices, shards(): lax.all_to_all(taken, ('rows', 'cols'), split_axis=0, concat_axis=0, tile...  17.2 us
    reshape x1, local copies, waits for them, and re-layouts, shards(): jnp.transpose(partials, (2, 3, 0, 1))  11.9 us
    unnamed x10, local copies, waits for them, and re-layouts  10.6 us
    all_to_all x1, starting transfers between devices, shards(): lax.all_to_all(copies, ('rows', 'cols'), split_axis=0, concat_axis=0, til...  7.1 us
    all_to_all x1, starting transfers between devices, shards(): lax.all_to_all(taken, ('rows', 'cols'), split_axis=0, concat_axis=0, tile...  5.84 us
    gather x4, local copies, waits for them, and re-layouts, local_rows(): return jnp.take(rows, picks, axis=1)  2.22 us
  transfers between devices with their start and end apart: 2, of which 1 were waited for; matrix products, arithmetic and copies ran while one was open for 27% of the time, Pallas kernels for 20%

profile of v1, /device:TPU:1, one launch (start us, length us, event | category | flops | bytes accessed | tf_op | source)
XLA Modules:
  0.0 103.1 jit_solution(10058017746338965030)
XLA Ops:
  0.0 0.7 copy-done
  0.7 0.7 reshape.346
  1.4 7.1 %all-to-all-start = ((s32[32,1,128]{2,1,0:T(1,128)}), s32[32,1,128]{2,1,0:T(1,128)S(1)}, u32[]{:S(2)}, u32[]{:S(2)}) async-start(s32[32,1,128]{2,1,0:T(1,128)} %reshape.346), calls=%async_computation | async-start | bytes 32768 | tf_op jit(solution)/shard_map/all_to_all | solution.py:153
  8.6 0.8 constant_dynamic-slice_fusion
  9.4 0.6 gather_fusion.2
  10.0 0.6 gather_fusion.4
  10.5 0.8 constant_dynamic-slice_fusion.1
  11.3 0.6 gather_fusion.3
  11.9 0.6 gather_fusion.1
  12.7 0.1 mul.140
  12.9 0.1 mul.138
  13.0 0.1 mul.134
  13.2 0.6 pad_maximum_fusion.2.ws_ref
  13.8 0.7 pad_maximum_fusion.1.wv_ref
  14.5 20.6 %shard_map.91 = f32[12,216,512]{2,1,0:T(8,128)} custom-call(bf16[12,256,4096]{2,1,0:T(8,128)(2,1)} %bitcast.102, bf16[1024,256]{1,0:T(8,128)(2,1)} %constant.173.clone.main_ref, bf16[128,256]{1,0:T(8,128)(2,1)} %constant.174.clone.prev_ref, bf16[128,256]{1,0:T(8,128)(2,1)} %constant.175.clone.next_ref, bf16[2,144,256]{2,1,0:T(8,128)(2,1)} %pad_maximum_fusion.1.wv_ref, ...), custom_call_target="tpu_custom_call" | custom-call | tf_op jit(solution)/shard_map/pallas_call | solution.py:98
  35.1 3.2 %pad.24 = f32[40,72,512]{2,1,0:T(8,128)S(1)} pad(f32[36,72,512]{2,1,0:T(8,128)} %bitcast.105, f32[]{:T(128)} %constant.166.clone.1), padding=0_4x0_0x0_0 | pad | bytes 11206660
  38.2 5.8 %copy.63 = f32[5,8,72,512]{3,1,2,0:T(8,128)} copy(f32[5,8,72,512]{3,2,1,0:T(8,128)S(1)} %bitcast.103) | data formatting | bytes 11796480
  44.0 11.9 %copy.49 = f32[36864,36]{1,0:T(8,128)} copy(f32[36864,36]{0,1:T(8,128)} %bitcast.104) | data formatting | bytes 10616832 | tf_op jit(solution)/shard_map/reshape | solution.py:192
  55.9 0.5 broadcast.217
  56.5 0.7 reduce.2
  57.2 0.4 fusion.7
  57.7 0.5 copy.48
  58.2 0.3 reshape.292
  58.6 17.1 %gather_fusion = f32[4096,36]{1,0:T(8,128)S(1)} fusion(f32[36864,36]{1,0:T(8,128)} %copy.49, s32[4096]{0:T(1024)S(1)} %broadcast_clamp_fusion), kind=kCustom, calls=%fused_computation.4 | custom fusion | bytes 1196032 | tf_op jit(solution)/shard_map/jit(_take)/gather | solution.py:193
  75.7 0.6 copy.50
  76.6 1.0 select_select_fusion
  77.6 5.8 %all-to-all-start.1 = ((f32[32,128,36]{1,2,0:T(8,128)}), f32[32,128,36]{1,2,0:T(8,128)S(1)}, u32[]{:S(2)}, u32[]{:S(2)}) async-start(f32[32,128,36]{1,2,0:T(8,128)} %select_select_fusion), calls=%async_computation.1 | async-start | bytes 1310720 | tf_op jit(solution)/shard_map/all_to_all | solution.py:196
  83.4 0.7 fusion.11
  84.2 17.2 %all-to-all-done.1 = f32[32,128,36]{1,2,0:T(8,128)S(1)} async-done(((f32[32,128,36]{1,2,0:T(8,128)}), f32[32,128,36]{1,2,0:T(8,128)S(1)}, u32[]{:S(2)}, u32[]{:S(2)}) %all-to-all-start.1) | async-done | bytes 589856 | tf_op jit(solution)/shard_map/all_to_all | solution.py:196
  101.8 0.3 multiply_reduce_fusion
  102.3 0.2 concatenate.58
  102.5 0.6 multiply_convert_fusion
  (38 shorter events, 1.4 us)
Async XLA Ops:
  0.0 0.7 copy-start
  1.4 54.5 %all-to-all-start = ((s32[32,1,128]{2,1,0:T(1,128)}), s32[32,1,128]{2,1,0:T(1,128)S(1)}, u32[]{:S(2)}, u32[]{:S(2)}) async-start(s32[32,1,128]{2,1,0:T(1,128)} %reshape.346), calls=%async_computation | async-start | bytes 32768 | tf_op jit(solution)/shard_map/all_to_all | solution.py:153
  58.6 44.6 %copy-start.1 = (s32[1,32,4]{1,2,0:T(4,128)S(1)}, s32[1,32,4]{1,2,0:T(4,128)}, u32[]{:S(2)}) copy-start(s32[1,32,4]{1,2,0:T(4,128)} %param.14) | copy-start | bytes 1540
  77.6 23.9 %all-to-all-start.1 = ((f32[32,128,36]{1,2,0:T(8,128)}), f32[32,128,36]{1,2,0:T(8,128)S(1)}, u32[]{:S(2)}, u32[]{:S(2)}) async-start(f32[32,128,36]{1,2,0:T(8,128)} %select_select_fusion), calls=%async_computation.1 | async-start | bytes 1310720 | tf_op jit(solution)/shard_map/all_to_all | solution.py:196

commit v2 on v1

--- a/solution.py
+++ b/solution.py
@@ -189,8 +189,8 @@
         inside = (at_x < x_count) & (at_y < y_count) & (by_owner >= 0)
         at_group = jnp.where(inside, at_x * y_count + at_y, 0)
         flat = (at_group * coarse_z + at_z).reshape(-1)
-        table = jnp.transpose(partials, (2, 3, 0, 1)).reshape(padded * coarse_z, field_count * 3)
-        taken = jnp.take(table, flat, axis=0)
+        table = partials.reshape(field_count * 3, padded * coarse_z)
+        taken = jnp.take(table, flat, axis=1).T
         taken = jnp.where(inside.reshape(-1, 1), taken, jnp.zeros_like(taken))
         taken = taken.reshape(devices, -1, field_count * 3)
         arrived = lax.all_to_all(taken, ("rows", "cols"), split_axis=0, concat_axis=0, tiled=True)

time: 104 us -> 109 us (1.048)
  local copies, waits for them, and re-layouts: 46.5 us -> 48.9 us
  other arithmetic: 5.57 us -> 7.73 us
    another operation x0 -> x2, local copies, waits for them, and re-layouts: none -> 18.5 us  [shards(): table = partials.reshape(field_count * 3, padded * coarse_z)]
    reshape x1, local copies, waits for them, and re-layouts: 11.9 us -> 1.46 us  [shards(): taken = taken.reshape(devices, -1, field_count * 3)]
    unnamed x10 -> x6, local copies, waits for them, and re-layouts: 10.6 us -> 1.6 us
    gather x2 -> x1, local copies, waits for them, and re-layouts: 17.8 us -> 20.4 us  [shards(): taken = jnp.take(table, flat, axis=1).T]
    select_n x1, other arithmetic: 0.98 us -> 3.17 us  [shards(): taken = jnp.where(inside.reshape(-1, 1), taken, jnp.zeros_like(taken))]
  transfers between devices with their start and end apart: 2 -> 2, of which waited for: 1 -> 1; matrix products, arithmetic and copies ran while one was open for 27% -> 23% of each run, Pallas kernels for 20% -> 19%
where the time goes in v2:
time: 109 us; the launch traced here: 108 us
  local copies, waits for them, and re-layouts  48.9 us (45%)
  Pallas kernels  20.6 us (19%)
  waiting for transfers between devices  17.2 us (16%)
  starting transfers between devices  12.9 us (12%)
  other arithmetic  7.73 us (7%)
    pallas_call x1, Pallas kernels, filtered_partials(): pl.pallas_call(filter_kernel(block_count, coarse_block, value_rows, slope...  20.6 us
    gather x1, local copies, waits for them, and re-layouts, shards(): taken = jnp.take(table, flat, axis=1).T  20.4 us
    another operation x2, local copies, waits for them, and re-layouts, shards(): table = partials.reshape(field_count * 3, padded * coarse_z)  18.5 us
    all_to_all x1, waiting for transfers between devices, shards(): lax.all_to_all(taken, ('rows', 'cols'), split_axis=0, concat_axis=0, tile...  17.2 us
    all_to_all x1, starting transfers between devices, shards(): lax.all_to_all(copies, ('rows', 'cols'), split_axis=0, concat_axis=0, til...  7.1 us
    all_to_all x1, starting transfers between devices, shards(): lax.all_to_all(taken, ('rows', 'cols'), split_axis=0, concat_axis=0, tile...  5.84 us
    select_n x1, other arithmetic, shards(): taken = jnp.where(inside.reshape(-1, 1), taken, jnp.zeros_like(taken))  3.17 us
    gather x4, local copies, waits for them, and re-layouts, local_rows(): return jnp.take(rows, picks, axis=1)  2.22 us
  transfers between devices with their start and end apart: 2, of which 1 were waited for; matrix products, arithmetic and copies ran while one was open for 23% of the time, Pallas kernels for 19%

profile of v2, /device:TPU:1, one launch (start us, length us, event | category | flops | bytes accessed | tf_op | source)
XLA Modules:
  0.0 107.6 jit_solution(11776802280115782749)
XLA Ops:
  0.0 0.7 copy-done
  0.7 0.7 reshape.330
  1.4 7.1 %all-to-all-start = ((s32[32,1,128]{2,1,0:T(1,128)}), s32[32,1,128]{2,1,0:T(1,128)S(1)}, u32[]{:S(2)}, u32[]{:S(2)}) async-start(s32[32,1,128]{2,1,0:T(1,128)} %reshape.330), calls=%async_computation | async-start | bytes 32768 | tf_op jit(solution)/shard_map/all_to_all | solution.py:153
  8.6 0.8 constant_dynamic-slice_fusion
  9.4 0.6 gather_fusion.2
  10.0 0.6 gather_fusion.4
  10.5 0.8 constant_dynamic-slice_fusion.1
  11.3 0.6 gather_fusion.3
  11.9 0.6 gather_fusion.1
  13.2 0.6 pad_maximum_fusion.2.ws_ref
  13.8 0.7 pad_maximum_fusion.1.wv_ref
  14.5 20.6 %shard_map.91 = f32[12,216,512]{2,1,0:T(8,128)} custom-call(bf16[12,256,4096]{2,1,0:T(8,128)(2,1)} %bitcast.102, bf16[1024,256]{1,0:T(8,128)(2,1)} %constant.173.clone.main_ref, bf16[128,256]{1,0:T(8,128)(2,1)} %constant.174.clone.prev_ref, bf16[128,256]{1,0:T(8,128)(2,1)} %constant.175.clone.next_ref, bf16[2,144,256]{2,1,0:T(8,128)(2,1)} %pad_maximum_fusion.1.wv_ref, ...), custom_call_target="tpu_custom_call" | custom-call | tf_op jit(solution)/shard_map/pallas_call | solution.py:98
  35.1 6.6 %reshape_reshape.3 = f32[36,36864]{1,0:T(8,128)} reshape(f32[12,216,512]{2,1,0:T(8,128)} %shard_map.91) | data formatting | bytes 10616832 | tf_op jit(solution)/shard_map/reshape;reshape | solution.py:192
  41.7 11.9 %copy.57 = f32[36,36864]{0,1:T(8,128)} copy(f32[36,36864]{1,0:T(8,128)} %reshape_reshape.3) | data formatting | bytes 10616832 | tf_op jit(solution)/shard_map/reshape;reshape | solution.py:192
  53.6 0.5 broadcast.226
  54.1 0.7 reduce.2
  55.0 0.2 fusion.7
  55.2 0.3 copy.55
  55.5 0.3 reshape.275
  55.8 0.3 reshape.273
  56.1 0.2 bitcast_and_fusion
  56.3 0.3 copy.54
  56.6 0.3 broadcast_in_dim.73
  57.0 20.4 %gather_fusion = f32[4096,36]{1,0:T(8,128)} fusion(f32[36,36864]{0,1:T(8,128)} %copy.57, s32[4096]{0:T(1024)S(1)} %broadcast_clamp_fusion), kind=kCustom, calls=%fused_computation.4 | custom fusion | bytes 1196032 | tf_op jit(solution)/shard_map/jit(_take)/gather | solution.py:193
  77.4 3.2 %select_select_fusion = f32[4096,36]{1,0:T(8,128)S(1)} fusion(f32[4096,36]{1,0:T(8,128)} %gather_fusion, pred[4096]{0:T(1024)(128)(4,1)S(1)} %broadcast_in_dim.73, pred[4096]{0:T(1024)(128)(4,1)S(1)} %compare_and_fusion), kind=kLoop, calls=%fused_computation.5 | loop fusion | flops 294912 | bytes 1187840 | tf_op jit(solution)/shard_map/jit(_where)/select_n | solution.py:194
  80.6 1.5 %copy.58 = f32[32,128,36]{1,2,0:T(8,128)} copy(f32[32,128,36]{2,1,0:T(8,128)S(1)} %bitcast.103) | data formatting | bytes 1179648 | tf_op jit(solution)/shard_map/reshape | solution.py:195
  82.1 5.8 %all-to-all-start.1 = ((f32[32,128,36]{1,2,0:T(8,128)}), f32[32,128,36]{1,2,0:T(8,128)S(1)}, u32[]{:S(2)}, u32[]{:S(2)}) async-start(f32[32,128,36]{1,2,0:T(8,128)} %copy.58), calls=%async_computation.1 | async-start | bytes 1310720 | tf_op jit(solution)/shard_map/all_to_all | solution.py:196
  87.9 0.7 fusion.11
  88.7 17.2 %all-to-all-done.1 = f32[32,128,36]{1,2,0:T(8,128)S(1)} async-done(((f32[32,128,36]{1,2,0:T(8,128)}), f32[32,128,36]{1,2,0:T(8,128)S(1)}, u32[]{:S(2)}, u32[]{:S(2)}) %all-to-all-start.1) | async-done | bytes 589856 | tf_op jit(solution)/shard_map/all_to_all | solution.py:196
  106.3 0.3 multiply_reduce_fusion
  106.8 0.2 concatenate.58
  107.0 0.6 multiply_convert_fusion
  (38 shorter events, 1.7 us)
Async XLA Ops:
  0.0 0.7 copy-start
  1.4 52.2 %all-to-all-start = ((s32[32,1,128]{2,1,0:T(1,128)}), s32[32,1,128]{2,1,0:T(1,128)S(1)}, u32[]{:S(2)}, u32[]{:S(2)}) async-start(s32[32,1,128]{2,1,0:T(1,128)} %reshape.330), calls=%async_computation | async-start | bytes 32768 | tf_op jit(solution)/shard_map/all_to_all | solution.py:153
  82.1 23.9 %all-to-all-start.1 = ((f32[32,128,36]{1,2,0:T(8,128)}), f32[32,128,36]{1,2,0:T(8,128)S(1)}, u32[]{:S(2)}, u32[]{:S(2)}) async-start(f32[32,128,36]{1,2,0:T(8,128)} %copy.58), calls=%async_computation.1 | async-start | bytes 1310720 | tf_op jit(solution)/shard_map/all_to_all | solution.py:196

commit v3 on v2

--- a/solution.py
+++ b/solution.py
@@ -112,6 +112,28 @@
     )(fields3, main, prev, nxt, wv, ws)
 
 
+def transpose_body(x_ref, o_ref):
+    rows = x_ref.shape[0]
+    width = o_ref.shape[2]
+    for gi in range(x_ref.shape[1]):
+        slab = x_ref[:, gi, :]
+        slab = jnp.concatenate([slab, jnp.zeros((width - rows, slab.shape[1]), slab.dtype)], axis=0)
+        o_ref[gi] = slab.T
+
+
+def cells_by_row(x):
+    rows, groups, lanes = x.shape
+    step = 8
+    width = -(-rows // 128) * 128
+    return pl.pallas_call(
+        transpose_body,
+        out_shape=jax.ShapeDtypeStruct((groups, lanes, width), x.dtype),
+        grid=(groups // step,),
+        in_specs=[pl.BlockSpec((rows, step, lanes), lambda j: (0, j, 0))],
+        out_specs=pl.BlockSpec((step, lanes, width), lambda j: (j, 0, 0)),
+    )(x)
+
+
 def model_tensors(coarse):
     values = coarse.astype(jnp.float32)
     points = values.shape[-1]
@@ -189,8 +211,8 @@
         inside = (at_x < x_count) & (at_y < y_count) & (by_owner >= 0)
         at_group = jnp.where(inside, at_x * y_count + at_y, 0)
         flat = (at_group * coarse_z + at_z).reshape(-1)
-        table = partials.reshape(field_count * 3, padded * coarse_z)
-        taken = jnp.take(table, flat, axis=1).T
+        table = cells_by_row(partials.reshape(field_count * 3, padded, coarse_z))
+        taken = jnp.take(table.reshape(padded * coarse_z, -1), flat, axis=0)[:, :field_count * 3]
         taken = jnp.where(inside.reshape(-1, 1), taken, jnp.zeros_like(taken))
         taken = taken.reshape(devices, -1, field_count * 3)
         arrived = lax.all_to_all(taken, ("rows", "cols"), split_axis=0, concat_axis=0, tiled=True)

time: 109 us -> 102 us (0.936)
  local copies, waits for them, and re-layouts: 48.9 us -> 30.4 us
  Pallas kernels: 20.6 us -> 32.7 us
    another operation x2 -> x0, local copies, waits for them, and re-layouts: 18.5 us -> none  [shards(): table = partials.reshape(field_count * 3, padded * coarse_z)]
    pallas_call x0 -> x1, Pallas kernels: none -> 12.1 us  [cells_by_row(): pl.pallas_call(transpose_body, out_shape=jax.ShapeDtypeStruct((groups, la...]
  transfers between devices with their start and end apart: 2 -> 2, of which waited for: 1 -> 1; matrix products, arithmetic and copies ran while one was open for 23% -> 7% of each run, Pallas kernels for 19% -> 32%
where the time goes in v3:
time: 102 us; the launch traced here: 101 us
  Pallas kernels  32.7 us (32%)
  local copies, waits for them, and re-layouts  30.4 us (30%)
  waiting for transfers between devices  17.2 us (17%)
  starting transfers between devices  12.9 us (13%)
  other arithmetic  7.74 us (8%)
    pallas_call x1, Pallas kernels, filtered_partials(): pl.pallas_call(filter_kernel(block_count, coarse_block, value_rows, slope...  20.6 us
    gather x1, local copies, waits for them, and re-layouts, shards(): jnp.take(table.reshape(padded * coarse_z, -1), flat, axis=0)  20.4 us
    all_to_all x1, waiting for transfers between devices, shards(): lax.all_to_all(taken, ('rows', 'cols'), split_axis=0, concat_axis=0, tile...  17.2 us
    pallas_call x1, Pallas kernels, cells_by_row(): pl.pallas_call(transpose_body, out_shape=jax.ShapeDtypeStruct((groups, la...  12.1 us
    all_to_all x1, starting transfers between devices, shards(): lax.all_to_all(copies, ('rows', 'cols'), split_axis=0, concat_axis=0, til...  7.1 us
    all_to_all x1, starting transfers between devices, shards(): lax.all_to_all(taken, ('rows', 'cols'), split_axis=0, concat_axis=0, tile...  5.83 us
    select_n x1, other arithmetic, shards(): taken = jnp.where(inside.reshape(-1, 1), taken, jnp.zeros_like(taken))  3.17 us
    gather x4, local copies, waits for them, and re-layouts, local_rows(): return jnp.take(rows, picks, axis=1)  2.22 us
  transfers between devices with their start and end apart: 2, of which 1 were waited for; matrix products, arithmetic and copies ran while one was open for 7% of the time, Pallas kernels for 32%

profile of v3, /device:TPU:1, one launch (start us, length us, event | category | flops | bytes accessed | tf_op | source)
XLA Modules:
  0.0 101.2 jit_solution(14628447601649223984)
XLA Ops:
  0.0 0.7 copy-done
  0.7 0.7 reshape.334
  1.4 7.1 %all-to-all-start = ((s32[32,1,128]{2,1,0:T(1,128)}), s32[32,1,128]{2,1,0:T(1,128)S(1)}, u32[]{:S(2)}, u32[]{:S(2)}) async-start(s32[32,1,128]{2,1,0:T(1,128)} %reshape.334), calls=%async_computation | async-start | bytes 32768 | tf_op jit(solution)/shard_map/all_to_all | solution.py:175
  8.6 0.8 constant_dynamic-slice_fusion
  9.4 0.6 gather_fusion.2
  10.0 0.6 gather_fusion.4
  10.5 0.8 constant_dynamic-slice_fusion.1
  11.3 0.6 gather_fusion.3
  11.9 0.6 gather_fusion.1
  12.7 0.1 mul.140
  13.2 0.6 pad_maximum_fusion.2.ws_ref
  13.8 0.7 pad_maximum_fusion.1.wv_ref
  14.5 20.6 %shard_map.91 = f32[12,216,512]{2,1,0:T(8,128)} custom-call(bf16[12,256,4096]{2,1,0:T(8,128)(2,1)} %bitcast.105, bf16[1024,256]{1,0:T(8,128)(2,1)} %constant.173.clone.main_ref, bf16[128,256]{1,0:T(8,128)(2,1)} %constant.174.clone.prev_ref, bf16[128,256]{1,0:T(8,128)(2,1)} %constant.175.clone.next_ref, bf16[2,144,256]{2,1,0:T(8,128)(2,1)} %pad_maximum_fusion.1.wv_ref, ...), custom_call_target="tpu_custom_call" | custom-call | tf_op jit(solution)/shard_map/pallas_call | solution.py:98
  35.1 12.1 %shard_map.92 = f32[72,512,128]{2,1,0:T(8,128)} custom-call(f32[36,72,512]{2,1,0:T(8,128)} %bitcast.106), custom_call_target="tpu_custom_call" | custom-call | tf_op jit(solution)/shard_map/pallas_call | solution.py:128
  47.2 0.5 broadcast.208
  47.7 0.7 reduce.2
  48.6 0.2 fusion.8
  48.8 0.3 copy.50
  49.0 0.3 reshape.279
  49.4 0.3 reshape.276
  49.7 0.2 bitcast_and_fusion
  49.9 0.3 copy.49
  50.2 0.3 broadcast_in_dim.73
  50.6 20.4 %gather_fusion = f32[4096,128]{1,0:T(8,128)} fusion(f32[36864,128]{1,0:T(8,128)} %bitcast.104, s32[4096]{0:T(1024)S(1)} %broadcast_clamp_fusion), kind=kCustom, calls=%fused_computation.4 | custom fusion | bytes 4210688 | tf_op jit(solution)/shard_map/jit(_take)/gather | solution.py:215
  71.0 3.2 %fusion = f32[4096,36]{1,0:T(8,128)S(1)} fusion(f32[4096,128]{1,0:T(8,128)} %gather_fusion, pred[4096]{0:T(1024)(128)(4,1)S(1)} %compare_and_fusion, pred[4096]{0:T(1024)(128)(4,1)S(1)} %broadcast_in_dim.73), kind=kLoop, calls=%fused_computation.6 | loop fusion | flops 294912 | bytes 1187840 | tf_op jit(solution)/shard_map/jit(_where)/select_n | solution.py:216
  74.2 1.5 %copy.52 = f32[32,128,36]{1,2,0:T(8,128)} copy(f32[32,128,36]{2,1,0:T(8,128)S(1)} %bitcast.107) | data formatting | bytes 1179648 | tf_op jit(solution)/shard_map/reshape | solution.py:217
  75.6 5.8 %all-to-all-start.1 = ((f32[32,128,36]{1,2,0:T(8,128)}), f32[32,128,36]{1,2,0:T(8,128)S(1)}, u32[]{:S(2)}, u32[]{:S(2)}) async-start(f32[32,128,36]{1,2,0:T(8,128)} %copy.52), calls=%async_computation.1 | async-start | bytes 1310720 | tf_op jit(solution)/shard_map/all_to_all | solution.py:218
  81.5 0.7 fusion.12
  82.3 17.2 %all-to-all-done.1 = f32[32,128,36]{1,2,0:T(8,128)S(1)} async-done(((f32[32,128,36]{1,2,0:T(8,128)}), f32[32,128,36]{1,2,0:T(8,128)S(1)}, u32[]{:S(2)}, u32[]{:S(2)}) %all-to-all-start.1) | async-done | bytes 589856 | tf_op jit(solution)/shard_map/all_to_all | solution.py:218
  99.9 0.3 multiply_reduce_fusion
  100.4 0.2 concatenate.58
  100.6 0.6 multiply_convert_fusion
  (37 shorter events, 1.6 us)
Async XLA Ops:
  0.0 0.7 copy-start
  1.4 45.8 %all-to-all-start = ((s32[32,1,128]{2,1,0:T(1,128)}), s32[32,1,128]{2,1,0:T(1,128)S(1)}, u32[]{:S(2)}, u32[]{:S(2)}) async-start(s32[32,1,128]{2,1,0:T(1,128)} %reshape.334), calls=%async_computation | async-start | bytes 32768 | tf_op jit(solution)/shard_map/all_to_all | solution.py:175
  75.6 23.9 %all-to-all-start.1 = ((f32[32,128,36]{1,2,0:T(8,128)}), f32[32,128,36]{1,2,0:T(8,128)S(1)}, u32[]{:S(2)}, u32[]{:S(2)}) async-start(f32[32,128,36]{1,2,0:T(8,128)} %copy.52), calls=%async_computation.1 | async-start | bytes 1310720 | tf_op jit(solution)/shard_map/all_to_all | solution.py:218

commit v4 on v2

--- a/solution.py
+++ b/solution.py
@@ -112,6 +112,61 @@
     )(fields3, main, prev, nxt, wv, ws)
 
 
+def pick_kernel(group_steps, step, chunk):
+    def body(idx_ref, x_ref, o_ref, tab_ref):
+        j = pl.program_id(0)
+        rows = x_ref.shape[0]
+        lanes = x_ref.shape[2]
+        width = tab_ref.shape[1]
+
+        @pl.when(j < group_steps)
+        def _():
+            for gi in range(step):
+                slab = x_ref[:, gi, :]
+                slab = jnp.concatenate([slab, jnp.zeros((width - rows, lanes), slab.dtype)], axis=0)
+                at = pl.multiple_of((j * step + gi) * lanes, lanes)
+                tab_ref[pl.ds(at, lanes), :] = slab.T
+
+        @pl.when(j == group_steps - 1)
+        def _():
+            tail = tab_ref.shape[0] - 8
+            tab_ref[pl.ds(tail, 8), :] = jnp.zeros((8, width), tab_ref.dtype)
+
+        @pl.when(j >= group_steps)
+        def _():
+            base = (j - group_steps) * chunk
+
+            def one(e, carry):
+                at = idx_ref[base + e]
+                o_ref[pl.ds(e, 1), :] = tab_ref[pl.ds(at, 1), :][:, :rows]
+                return carry
+
+            lax.fori_loop(0, chunk, one, 0, unroll=8)
+
+    return body
+
+
+def pick_cells(x, flat, chunk=2048):
+    rows, groups, lanes = x.shape
+    step = 8
+    group_steps = groups // step
+    entries = flat.shape[0]
+    chunk = min(chunk, entries)
+    width = -(-rows // 128) * 128
+    grid_spec = pltpu.PrefetchScalarGridSpec(
+        num_scalar_prefetch=1,
+        grid=(group_steps + entries // chunk,),
+        in_specs=[pl.BlockSpec((rows, step, lanes), lambda j, idx: (0, jnp.minimum(j, group_steps - 1), 0))],
+        out_specs=pl.BlockSpec((chunk, rows), lambda j, idx: (jnp.maximum(j - group_steps, 0), 0)),
+        scratch_shapes=[pltpu.VMEM((groups * lanes + 8, width), x.dtype)],
+    )
+    return pl.pallas_call(
+        pick_kernel(group_steps, step, chunk),
+        out_shape=jax.ShapeDtypeStruct((entries, rows), x.dtype),
+        grid_spec=grid_spec,
+    )(flat, x)
+
+
 def model_tensors(coarse):
     values = coarse.astype(jnp.float32)
     points = values.shape[-1]
@@ -187,11 +242,8 @@
         at_x = (cell_pq // coarse_y - x_base) % coarse_x
         at_y = (cell_pq % coarse_y - y_base) % coarse_y
         inside = (at_x < x_count) & (at_y < y_count) & (by_owner >= 0)
-        at_group = jnp.where(inside, at_x * y_count + at_y, 0)
-        flat = (at_group * coarse_z + at_z).reshape(-1)
-        table = partials.reshape(field_count * 3, padded * coarse_z)
-        taken = jnp.take(table, flat, axis=1).T
-        taken = jnp.where(inside.reshape(-1, 1), taken, jnp.zeros_like(taken))
+        flat = jnp.where(inside, (at_x * y_count + at_y) * coarse_z + at_z, padded * coarse_z)
+        taken = pick_cells(partials.reshape(field_count * 3, padded, coarse_z), flat.reshape(-1))
         taken = taken.reshape(devices, -1, field_count * 3)
         arrived = lax.all_to_all(taken, ("rows", "cols"), split_axis=0, concat_axis=0, tiled=True)
         summed = jnp.sum(arrived.reshape(devices, -1, field_count * 3), axis=0).T

time: 109 us -> 85.1 us (0.78)
  local copies, waits for them, and re-layouts: 48.9 us -> 11.4 us
  Pallas kernels: 20.6 us -> 37.9 us
  other arithmetic: 7.73 us -> 4.5 us
    gather x1 -> x0, local copies, waits for them, and re-layouts: 20.4 us -> none  [shards(): taken = jnp.take(table, flat, axis=1).T]
    another operation x2 -> x0, local copies, waits for them, and re-layouts: 18.5 us -> none  [shards(): table = partials.reshape(field_count * 3, padded * coarse_z)]
    pallas_call x0 -> x1, Pallas kernels: none -> 17.4 us  [pick_cells(): pl.pallas_call(pick_kernel(group_steps, step, chunk), out_shape=jax.Shape...]
    select_n x2 -> x1, other arithmetic: 3.19 us -> 0.4 us  [shards(): jnp.where(inside, (at_x * y_count + at_y) * coarse_z + at_z, padded * coa...]
    reshape x1, local copies, waits for them, and re-layouts: 1.46 us -> 3.05 us  [shards(): taken = taken.reshape(devices, -1, field_count * 3)]
  transfers between devices with their start and end apart: 2 -> 2, of which waited for: 1 -> 1; matrix products, arithmetic and copies ran while one was open for 23% -> 8% of each run, Pallas kernels for 19% -> 24%
where the time goes in v4:
time: 85.1 us; the launch traced here: 84.2 us
  Pallas kernels  37.9 us (45%)
  waiting for transfers between devices  17.2 us (20%)
  starting transfers between devices  12.9 us (15%)
  local copies, waits for them, and re-layouts  11.4 us (13%)
  other arithmetic  4.5 us (5%)
    pallas_call x1, Pallas kernels, filtered_partials(): pl.pallas_call(filter_kernel(block_count, coarse_block, value_rows, slope...  20.6 us
    pallas_call x1, Pallas kernels, pick_cells(): pl.pallas_call(pick_kernel(group_steps, step, chunk), out_shape=jax.Shape...  17.4 us
    all_to_all x1, waiting for transfers between devices, shards(): lax.all_to_all(taken, ('rows', 'cols'), split_axis=0, concat_axis=0, tile...  17.2 us
    all_to_all x1, starting transfers between devices, shards(): lax.all_to_all(copies, ('rows', 'cols'), split_axis=0, concat_axis=0, til...  7.1 us
    all_to_all x1, starting transfers between devices, shards(): lax.all_to_all(taken, ('rows', 'cols'), split_axis=0, concat_axis=0, tile...  5.83 us
    reshape x1, local copies, waits for them, and re-layouts, shards(): taken = taken.reshape(devices, -1, field_count * 3)  3.05 us
    gather x4, local copies, waits for them, and re-layouts, local_rows(): return jnp.take(rows, picks, axis=1)  2.22 us
  transfers between devices with their start and end apart: 2, of which 1 were waited for; matrix products, arithmetic and copies ran while one was open for 8% of the time, Pallas kernels for 24%

profile of v4, /device:TPU:1, one launch (start us, length us, event | category | flops | bytes accessed | tf_op | source)
XLA Modules:
  0.0 84.2 jit_solution(17438864870215032310)
XLA Ops:
  0.0 0.7 copy-done
  0.7 0.7 reshape.283
  1.4 7.1 %all-to-all-start = ((s32[32,1,128]{2,1,0:T(1,128)}), s32[32,1,128]{2,1,0:T(1,128)S(1)}, u32[]{:S(2)}, u32[]{:S(2)}) async-start(s32[32,1,128]{2,1,0:T(1,128)} %reshape.283), calls=%async_computation | async-start | bytes 32768 | tf_op jit(solution)/shard_map/all_to_all | solution.py:208
  8.6 0.8 constant_dynamic-slice_fusion
  9.4 0.6 gather_fusion.2
  10.0 0.6 gather_fusion
  10.5 0.8 constant_dynamic-slice_fusion.1
  11.3 0.6 gather_fusion.1
  11.9 0.6 gather_fusion.3
  12.6 0.1 broadcast_multiply_fusion.1
  12.7 0.1 mul.140
  12.9 0.1 mul.134
  13.0 0.1 mul.138
  13.2 0.6 pad_maximum_fusion.2.ws_ref
  13.8 0.7 pad_maximum_fusion.1.wv_ref
  14.5 20.6 %shard_map.91 = f32[12,216,512]{2,1,0:T(8,128)} custom-call(bf16[12,256,4096]{2,1,0:T(8,128)(2,1)} %bitcast.83, bf16[1024,256]{1,0:T(8,128)(2,1)} %constant.159.clone.main_ref, bf16[128,256]{1,0:T(8,128)(2,1)} %constant.160.clone.prev_ref, bf16[128,256]{1,0:T(8,128)(2,1)} %constant.161.clone.next_ref, bf16[2,144,256]{2,1,0:T(8,128)(2,1)} %pad_maximum_fusion.1.wv_ref, ...), custom_call_target="tpu_custom_call" | custom-call | tf_op jit(solution)/shard_map/pallas_call | solution.py:98
  35.1 0.5 broadcast.177
  35.6 0.7 reduce.2
  36.3 0.1 reshape.284
  36.4 0.4 fusion.8
  36.8 0.6 copy.46
  37.3 0.9 %reshape.235.idx_ref = s32[4096]{0:T(1024)} reshape(s32[32,32,4]{2,1,0:T(8,128)S(1)} %copy.46) | data formatting | bytes 32768 | tf_op jit(solution)/shard_map/reshape | solution.py:246
  38.2 17.4 %shard_map.92 = f32[4096,36]{1,0:T(8,128)} custom-call(s32[4096]{0:T(1024)} %reshape.235.idx_ref, f32[36,72,512]{2,1,0:T(8,128)} %bitcast.84), custom_call_target="tpu_custom_call" | custom-call | tf_op jit(solution)/shard_map/pallas_call | solution.py:163
  55.6 3.0 %copy.47 = f32[32,128,36]{1,2,0:T(8,128)} copy(f32[32,128,36]{2,1,0:T(8,128)} %bitcast.85) | data formatting | bytes 1179648 | tf_op jit(solution)/shard_map/reshape | solution.py:247
  58.6 5.8 %all-to-all-start.1 = ((f32[32,128,36]{1,2,0:T(8,128)}), f32[32,128,36]{1,2,0:T(8,128)S(1)}, u32[]{:S(2)}, u32[]{:S(2)}) async-start(f32[32,128,36]{1,2,0:T(8,128)} %copy.47), calls=%async_computation.1 | async-start | bytes 1310720 | tf_op jit(solution)/shard_map/all_to_all | solution.py:248
  64.5 0.7 fusion.12
  65.2 0.1 ge.31
  65.3 17.2 %all-to-all-done.1 = f32[32,128,36]{1,2,0:T(8,128)S(1)} async-done(((f32[32,128,36]{1,2,0:T(8,128)}), f32[32,128,36]{1,2,0:T(8,128)S(1)}, u32[]{:S(2)}, u32[]{:S(2)}) %all-to-all-start.1) | async-done | bytes 589856 | tf_op jit(solution)/shard_map/all_to_all | solution.py:248
  82.6 0.1 copy.51
  82.8 0.3 multiply_reduce_fusion
  83.4 0.2 concatenate.58
  83.6 0.6 multiply_convert_fusion
  (27 shorter events, 0.8 us)
Async XLA Ops:
  0.0 0.7 copy-start
  1.4 33.7 %all-to-all-start = ((s32[32,1,128]{2,1,0:T(1,128)}), s32[32,1,128]{2,1,0:T(1,128)S(1)}, u32[]{:S(2)}, u32[]{:S(2)}) async-start(s32[32,1,128]{2,1,0:T(1,128)} %reshape.283), calls=%async_computation | async-start | bytes 32768 | tf_op jit(solution)/shard_map/all_to_all | solution.py:208
  58.6 23.9 %all-to-all-start.1 = ((f32[32,128,36]{1,2,0:T(8,128)}), f32[32,128,36]{1,2,0:T(8,128)S(1)}, u32[]{:S(2)}, u32[]{:S(2)}) async-start(f32[32,128,36]{1,2,0:T(8,128)} %copy.47), calls=%async_computation.1 | async-start | bytes 1310720 | tf_op jit(solution)/shard_map/all_to_all | solution.py:248

commit v5 on v4

--- a/solution.py
+++ b/solution.py
@@ -112,8 +112,8 @@
     )(fields3, main, prev, nxt, wv, ws)
 
 
-def pick_kernel(group_steps, step, chunk):
-    def body(idx_ref, x_ref, o_ref, tab_ref):
+def pick_kernel(group_steps, step, chunk, owner_len):
+    def body(idx_ref, x_ref, o_ref, tab_ref, buf_ref):
         j = pl.program_id(0)
         rows = x_ref.shape[0]
         lanes = x_ref.shape[2]
@@ -138,31 +138,35 @@
 
             def one(e, carry):
                 at = idx_ref[base + e]
-                o_ref[pl.ds(e, 1), :] = tab_ref[pl.ds(at, 1), :][:, :rows]
+                buf_ref[pl.ds(e, 1), :] = tab_ref[pl.ds(at, 1), :]
                 return carry
 
             lax.fori_loop(0, chunk, one, 0, unroll=8)
+            flipped = buf_ref[...].T
+            for owner in range(chunk // owner_len):
+                o_ref[owner] = flipped[:rows, owner * owner_len:(owner + 1) * owner_len]
 
     return body
 
 
-def pick_cells(x, flat, chunk=2048):
+def pick_cells(x, flat, owner_len, chunk=2048):
     rows, groups, lanes = x.shape
     step = 8
     group_steps = groups // step
     entries = flat.shape[0]
     chunk = min(chunk, entries)
     width = -(-rows // 128) * 128
+    per_chunk = chunk // owner_len
     grid_spec = pltpu.PrefetchScalarGridSpec(
         num_scalar_prefetch=1,
         grid=(group_steps + entries // chunk,),
         in_specs=[pl.BlockSpec((rows, step, lanes), lambda j, idx: (0, jnp.minimum(j, group_steps - 1), 0))],
-        out_specs=pl.BlockSpec((chunk, rows), lambda j, idx: (jnp.maximum(j - group_steps, 0), 0)),
-        scratch_shapes=[pltpu.VMEM((groups * lanes + 8, width), x.dtype)],
+        out_specs=pl.BlockSpec((per_chunk, rows, owner_len), lambda j, idx: (jnp.maximum(j - group_steps, 0), 0, 0)),
+        scratch_shapes=[pltpu.VMEM((groups * lanes + 8, width), x.dtype), pltpu.VMEM((chunk, width), x.dtype)],
     )
     return pl.pallas_call(
-        pick_kernel(group_steps, step, chunk),
-        out_shape=jax.ShapeDtypeStruct((entries, rows), x.dtype),
+        pick_kernel(group_steps, step, chunk, owner_len),
+        out_shape=jax.ShapeDtypeStruct((entries // owner_len, rows, owner_len), x.dtype),
         grid_spec=grid_spec,
     )(flat, x)
 
@@ -243,10 +247,10 @@
         at_y = (cell_pq % coarse_y - y_base) % coarse_y
         inside = (at_x < x_count) & (at_y < y_count) & (by_owner >= 0)
         flat = jnp.where(inside, (at_x * y_count + at_y) * coarse_z + at_z, padded * coarse_z)
-        taken = pick_cells(partials.reshape(field_count * 3, padded, coarse_z), flat.reshape(-1))
-        taken = taken.reshape(devices, -1, field_count * 3)
+        owner_len = devices * slots
+        taken = pick_cells(partials.reshape(field_count * 3, padded, coarse_z), flat.reshape(-1), owner_len)
         arrived = lax.all_to_all(taken, ("rows", "cols"), split_axis=0, concat_axis=0, tiled=True)
-        summed = jnp.sum(arrived.reshape(devices, -1, field_count * 3), axis=0).T
+        summed = jnp.sum(arrived, axis=0)
         rounded = lax.reduce_precision(summed, exponent_bits=8, mantissa_bits=7)
         mine = lax.dynamic_index_in_dim(by_owner, me, axis=0, keepdims=False).reshape(-1)
         picked = jnp.where(mine[None, :] >= 0, rounded, jnp.zeros_like(rounded))

time: 85.1 us -> 81.4 us (0.957)
  local copies, waits for them, and re-layouts: 11.4 us -> 7.95 us
    reshape x1 -> x0, local copies, waits for them, and re-layouts: 3.05 us -> none  [shards(): taken = taken.reshape(devices, -1, field_count * 3)]
  transfers between devices with their start and end apart: 2 -> 2, of which waited for: 1 -> 1; matrix products, arithmetic and copies ran while one was open for 8% -> 8% of each run, Pallas kernels for 24% -> 26%
where the time goes in v5:
time: 81.4 us; the launch traced here: 80.5 us
  Pallas kernels  38 us (47%)
  waiting for transfers between devices  17.2 us (21%)
  starting transfers between devices  12.9 us (16%)
  local copies, waits for them, and re-layouts  7.95 us (10%)
  other arithmetic  4.2 us (5%)
    pallas_call x1, Pallas kernels, filtered_partials(): pl.pallas_call(filter_kernel(block_count, coarse_block, value_rows, slope...  20.6 us
    pallas_call x1, Pallas kernels, pick_cells(): pl.pallas_call(pick_kernel(group_steps, step, chunk, owner_len), out_shap...  17.4 us
    all_to_all x1, waiting for transfers between devices, shards(): lax.all_to_all(taken, ('rows', 'cols'), split_axis=0, concat_axis=0, tile...  17.2 us
    all_to_all x1, starting transfers between devices, shards(): lax.all_to_all(copies, ('rows', 'cols'), split_axis=0, concat_axis=0, til...  7.1 us
    all_to_all x1, starting transfers between devices, shards(): lax.all_to_all(taken, ('rows', 'cols'), split_axis=0, concat_axis=0, tile...  5.83 us
    gather x4, local copies, waits for them, and re-layouts, local_rows(): return jnp.take(rows, picks, axis=1)  2.22 us
  transfers between devices with their start and end apart: 2, of which 1 were waited for; matrix products, arithmetic and copies ran while one was open for 8% of the time, Pallas kernels for 26%

profile of v5, /device:TPU:1, one launch (start us, length us, event | category | flops | bytes accessed | tf_op | source)
XLA Modules:
  0.0 80.5 jit_solution(7463750967356710984)
XLA Ops:
  0.0 0.7 copy-done
  0.7 0.7 reshape.279
  1.4 7.1 %all-to-all-start = ((s32[32,1,128]{2,1,0:T(1,128)}), s32[32,1,128]{2,1,0:T(1,128)S(1)}, u32[]{:S(2)}, u32[]{:S(2)}) async-start(s32[32,1,128]{2,1,0:T(1,128)} %reshape.279), calls=%async_computation | async-start | bytes 32768 | tf_op jit(solution)/shard_map/all_to_all | solution.py:212
  8.6 0.8 constant_dynamic-slice_fusion
  9.4 0.6 gather_fusion.2
  10.0 0.6 gather_fusion
  10.5 0.8 constant_dynamic-slice_fusion.1
  11.3 0.6 gather_fusion.1
  11.9 0.6 gather_fusion.3
  12.4 0.1 select_bitcast_fusion.3
  12.5 0.1 select_bitcast_fusion.1
  12.6 0.1 broadcast_multiply_fusion.1
  12.7 0.1 mul.140
  12.9 0.1 mul.134
  13.0 0.1 mul.138
  13.2 0.6 pad_maximum_fusion.2.ws_ref
  13.8 0.7 pad_maximum_fusion.1.wv_ref
  14.5 20.6 %shard_map.91 = f32[12,216,512]{2,1,0:T(8,128)} custom-call(bf16[12,256,4096]{2,1,0:T(8,128)(2,1)} %bitcast.79, bf16[1024,256]{1,0:T(8,128)(2,1)} %constant.159.clone.main_ref, bf16[128,256]{1,0:T(8,128)(2,1)} %constant.160.clone.prev_ref, bf16[128,256]{1,0:T(8,128)(2,1)} %constant.161.clone.next_ref, bf16[2,144,256]{2,1,0:T(8,128)(2,1)} %pad_maximum_fusion.1.wv_ref, ...), custom_call_target="tpu_custom_call" | custom-call | tf_op jit(solution)/shard_map/pallas_call | solution.py:98
  35.1 0.5 broadcast.174
  35.6 0.7 reduce.2
  36.3 0.1 reshape.280
  36.4 0.4 fusion.8
  36.8 0.5 copy.36
  37.3 0.9 %reshape.232.idx_ref = s32[4096]{0:T(1024)} reshape(s32[32,32,4]{2,1,0:T(8,128)S(1)} %copy.36) | data formatting | bytes 32768 | tf_op jit(solution)/shard_map/reshape | solution.py:251
  38.2 17.4 %shard_map.92 = f32[32,36,128]{2,1,0:T(8,128)} custom-call(s32[4096]{0:T(1024)} %reshape.232.idx_ref, f32[36,72,512]{2,1,0:T(8,128)} %bitcast.80), custom_call_target="tpu_custom_call" | custom-call | tf_op jit(solution)/shard_map/pallas_call | solution.py:167
  55.6 5.8 %all-to-all-start.1 = ((f32[32,36,128]{2,1,0:T(8,128)}), f32[32,36,128]{2,1,0:T(8,128)S(1)}, u32[]{:S(2)}, u32[]{:S(2)}) async-start(f32[32,36,128]{2,1,0:T(8,128)} %shard_map.92), calls=%async_computation.1 | async-start | bytes 1310720 | tf_op jit(solution)/shard_map/all_to_all | solution.py:252
  61.5 0.7 fusion.12
  62.2 0.1 ge.31
  62.3 17.2 %all-to-all-done.1 = f32[32,36,128]{2,1,0:T(8,128)S(1)} async-done(((f32[32,36,128]{2,1,0:T(8,128)}), f32[32,36,128]{2,1,0:T(8,128)S(1)}, u32[]{:S(2)}, u32[]{:S(2)}) %all-to-all-start.1) | async-done | bytes 589856 | tf_op jit(solution)/shard_map/all_to_all | solution.py:252
  79.5 0.1 reduce_sum.72
  79.7 0.2 concatenate.58
  79.9 0.6 multiply_convert_fusion
  (24 shorter events, 0.3 us)
Async XLA Ops:
  0.0 0.7 copy-start
  1.4 33.7 %all-to-all-start = ((s32[32,1,128]{2,1,0:T(1,128)}), s32[32,1,128]{2,1,0:T(1,128)S(1)}, u32[]{:S(2)}, u32[]{:S(2)}) async-start(s32[32,1,128]{2,1,0:T(1,128)} %reshape.279), calls=%async_computation | async-start | bytes 32768 | tf_op jit(solution)/shard_map/all_to_all | solution.py:212
  55.6 23.9 %all-to-all-start.1 = ((f32[32,36,128]{2,1,0:T(8,128)}), f32[32,36,128]{2,1,0:T(8,128)S(1)}, u32[]{:S(2)}, u32[]{:S(2)}) async-start(f32[32,36,128]{2,1,0:T(8,128)} %shard_map.92), calls=%async_computation.1 | async-start | bytes 1310720 | tf_op jit(solution)/shard_map/all_to_all | solution.py:252

commit v6 on v5

--- a/solution.py
+++ b/solution.py
@@ -46,7 +46,7 @@
 
 
 def filter_kernel(block_count, coarse_block, value_rows, slope_rows):
-    def body(x_ref, main_ref, prev_ref, next_ref, wv_ref, ws_ref, o_ref, zv_ref, zs_ref):
+    def body(x_ref, main_ref, halo_ref, w_ref, o_ref, zv_ref, zs_ref):
         length = x_ref.shape[2]
         blen = length // block_count
         for b in range(block_count):
@@ -55,18 +55,18 @@
             tail = x_ref[0, :, start:start + halo]
             start = ((b + 1) * blen) % length
             head = x_ref[0, :, start:start + halo]
+            edges = jnp.concatenate([tail, head], axis=1)
             acc = jnp.dot(main, main_ref[...], preferred_element_type=jnp.float32)
-            acc = acc + jnp.dot(tail, prev_ref[...], preferred_element_type=jnp.float32)
-            acc = acc + jnp.dot(head, next_ref[...], preferred_element_type=jnp.float32)
+            acc = acc + jnp.dot(edges, halo_ref[...], preferred_element_type=jnp.float32)
             lanes = slice(b * coarse_block, (b + 1) * coarse_block)
             zv_ref[:, lanes] = acc[:, :coarse_block].astype(jnp.bfloat16)
             zs_ref[:, lanes] = acc[:, coarse_block:].astype(jnp.bfloat16)
         zv = zv_ref[...]
         zs = zs_ref[...]
-        pv = jnp.dot(wv_ref[0], zv, preferred_element_type=jnp.float32)
-        pv = pv + jnp.dot(wv_ref[1], zv, preferred_element_type=jnp.float32)
-        ps = jnp.dot(ws_ref[0], zs, preferred_element_type=jnp.float32)
-        ps = ps + jnp.dot(ws_ref[1], zs, preferred_element_type=jnp.float32)
+        pv = jnp.dot(w_ref[0, :value_rows, :], zv, preferred_element_type=jnp.float32)
+        pv = pv + jnp.dot(w_ref[1, :value_rows, :], zv, preferred_element_type=jnp.float32)
+        ps = jnp.dot(w_ref[0, value_rows:, :], zs, preferred_element_type=jnp.float32)
+        ps = ps + jnp.dot(w_ref[1, value_rows:, :], zs, preferred_element_type=jnp.float32)
         o_ref[0, :value_rows, :] = pv
         o_ref[0, value_rows:, :] = ps
 
@@ -79,37 +79,45 @@
     return jnp.stack([hi, lo], axis=0)
 
 
-def filtered_partials(fields3, value_w, slope_w):
+def filtered_partials(fields3, weights):
     field_count, rows, length = fields3.shape
     blen = block_len if (length % block_len == 0 and length > block_len) else length
     block_count = length // blen
     coarse_block = blen // 8
     tables = z_tables(blen)
     joined = [np.concatenate([t[0], t[1]], axis=1) for t in tables]
-    main, prev, nxt = [jnp.asarray(t, jnp.bfloat16) for t in joined]
-    wv = split_hi_lo(value_w)
-    ws = split_hi_lo(slope_w)
-    value_rows = wv.shape[1]
-    slope_rows = ws.shape[1]
-    total_rows = value_rows + slope_rows
+    main = jnp.asarray(joined[0], jnp.bfloat16)
+    halo_w = jnp.asarray(np.concatenate([joined[1], joined[2]], axis=0), jnp.bfloat16)
+    w = split_hi_lo(weights)
+    total_rows = w.shape[1]
+    value_rows = total_rows // 3 * 2
     coarse = length // 8
     const = lambda f: (0, 0)
-    const3 = lambda f: (0, 0, 0)
     return pl.pallas_call(
-        filter_kernel(block_count, coarse_block, value_rows, slope_rows),
+        filter_kernel(block_count, coarse_block, value_rows, total_rows - value_rows),
         out_shape=jax.ShapeDtypeStruct((field_count, total_rows, coarse), jnp.float32),
         grid=(field_count,),
         in_specs=[
             pl.BlockSpec((1, rows, length), lambda f: (f, 0, 0)),
             pl.BlockSpec(main.shape, const),
-            pl.BlockSpec(prev.shape, const),
-            pl.BlockSpec(nxt.shape, const),
-            pl.BlockSpec(wv.shape, const3),
-            pl.BlockSpec(ws.shape, const3),
+            pl.BlockSpec(halo_w.shape, const),
+            pl.BlockSpec(w.shape, lambda f: (0, 0, 0)),
         ],
         out_specs=pl.BlockSpec((1, total_rows, coarse), lambda f: (f, 0, 0)),
         scratch_shapes=[pltpu.VMEM((rows, coarse), jnp.bfloat16), pltpu.VMEM((rows, coarse), jnp.bfloat16)],
-    )(fields3, main, prev, nxt, wv, ws)
+    )(fields3, main, halo_w, w)
+
+
+def window_tables(blocks, count, full):
+    smooth, deriv = line_matrices(full)
+    coarse = full // 8
+    out = []
+    for at in range(blocks):
+        base, width = window(at, count, coarse)
+        picks = (base + np.arange(width)) % coarse
+        part = slice(at * count, (at + 1) * count)
+        out.append(np.stack([smooth[part][:, picks].T, deriv[part][:, picks].T]))
+    return np.stack(out)
 
 
 def pick_kernel(group_steps, step, chunk, owner_len):
@@ -211,32 +219,19 @@
         copies = jnp.broadcast_to(front_cells, (devices,) + front_cells.shape[1:])
         every_cell = lax.all_to_all(copies, ("rows", "cols"), split_axis=0, concat_axis=0, tiled=True)
 
-        smooth_x, deriv_x = line_matrices(full_x)
-        smooth_y, deriv_y = line_matrices(full_y)
         x_base, x_count = window(row, local_x, coarse_x)
         y_base, y_count = window(col, local_y, coarse_y)
-
-        def local_rows(table, at, count, base, width, full):
-            rows = lax.dynamic_slice_in_dim(jnp.asarray(table), at * count, count)
-            picks = (base + jnp.arange(width)) % full
-            return jnp.take(rows, picks, axis=1)
-
-        ax = local_rows(smooth_x, row, local_x, x_base, x_count, coarse_x)
-        bx = local_rows(deriv_x, row, local_x, x_base, x_count, coarse_x)
-        ay = local_rows(smooth_y, col, local_y, y_base, y_count, coarse_y)
-        by = local_rows(deriv_y, col, local_y, y_base, y_count, coarse_y)
+        wx = jnp.asarray(window_tables(row_count, local_x, full_x))[row]
+        wy = jnp.asarray(window_tables(col_count, local_y, full_y))[col]
         group = x_count * y_count
         padded = -(-group // 8) * 8
-
-        def kron(wx, wy):
-            joined = (wx[:, None, :, None] * wy[None, :, None, :]).reshape(local_x * local_y, group)
-            return jnp.pad(joined, ((0, 0), (0, padded - group))).T
-
-        value_w = jnp.concatenate([kron(bx, ay), kron(ax, by)], axis=0)
-        slope_w = kron(ax, ay)
+        xs = jnp.stack([wx[1], wx[0], wx[0]])
+        ys = jnp.stack([wy[0], wy[1], wy[0]])
+        weights = xs[:, :, None, :, None] * ys[:, None, :, None, :]
+        weights = weights.reshape(3, group, local_x * local_y)
+        weights = jnp.pad(weights, ((0, 0), (0, padded - group), (0, 0))).reshape(3 * padded, -1)
         fields3 = fields.reshape(field_count, local_x * local_y, z_length)
-        partials = filtered_partials(fields3, value_w, slope_w)
-        partials = partials.reshape(field_count, 3, padded, coarse_z)
+        partials = filtered_partials(fields3, weights)
 
         by_owner = jnp.transpose(every_cell, (1, 0, 2))
         holder = lax.broadcasted_iota(jnp.int32, by_owner.shape, 1)

time: 81.4 us -> 77.5 us (0.952)
  local copies, waits for them, and re-layouts: 7.95 us -> 5.57 us
    gather x4 -> x0, local copies, waits for them, and re-layouts: 2.22 us -> none  [local_rows(): return jnp.take(rows, picks, axis=1)]
    dynamic_slice x2 -> x0, local copies, waits for them, and re-layouts: 1.58 us -> none  [local_rows(): rows = lax.dynamic_slice_in_dim(jnp.asarray(table), at * count, count)]
    slice x0 -> x2, local copies, waits for them, and re-layouts: none -> 1.51 us  [the longest x1 0.78 us: shards(): xs = jnp.stack([wx[1], wx[0], wx[0]])]
  transfers between devices with their start and end apart: 2 -> 2, of which waited for: 1 -> 1; matrix products, arithmetic and copies ran while one was open for 8% -> 5% of each run, Pallas kernels for 26% -> 26%
where the time goes in v6:
time: 77.5 us; the launch traced here: 76.6 us
  Pallas kernels  37.3 us (48%)
  waiting for transfers between devices  17.2 us (22%)
  starting transfers between devices  12.9 us (17%)
  local copies, waits for them, and re-layouts  5.57 us (7%)
  other arithmetic  3.4 us (4%)
    pallas_call x1, Pallas kernels, filtered_partials(): pl.pallas_call(filter_kernel(block_count, coarse_block, value_rows, total...  19.9 us
    pallas_call x1, Pallas kernels, pick_cells(): pl.pallas_call(pick_kernel(group_steps, step, chunk, owner_len), out_shap...  17.4 us
    all_to_all x1, waiting for transfers between devices, shards(): lax.all_to_all(taken, ('rows', 'cols'), split_axis=0, concat_axis=0, tile...  17.2 us
    all_to_all x1, starting transfers between devices, shards(): lax.all_to_all(copies, ('rows', 'cols'), split_axis=0, concat_axis=0, til...  7.1 us
    all_to_all x1, starting transfers between devices, shards(): lax.all_to_all(taken, ('rows', 'cols'), split_axis=0, concat_axis=0, tile...  5.83 us
  transfers between devices with their start and end apart: 2, of which 1 were waited for; matrix products, arithmetic and copies ran while one was open for 5% of the time, Pallas kernels for 26%

profile of v6, /device:TPU:1, one launch (start us, length us, event | category | flops | bytes accessed | tf_op | source)
XLA Modules:
  0.0 76.6 jit_solution(15883414543672342391)
XLA Ops:
  0.0 0.0 copy-start
  0.0 0.7 copy-done
  0.7 0.7 reshape.186
  1.4 7.1 %all-to-all-start = ((s32[32,1,128]{2,1,0:T(1,128)}), s32[32,1,128]{2,1,0:T(1,128)S(1)}, u32[]{:S(2)}, u32[]{:S(2)}) async-start(s32[32,1,128]{2,1,0:T(1,128)} %reshape.186), calls=%async_computation | async-start | bytes 32768 | tf_op jit(solution)/shard_map/all_to_all | solution.py:220
  8.5 0.8 %dynamic-slice_bitcast_fusion.3 = (f32[1,7,8]{2,0,1:T(1,128)S(1)}, f32[1,7,8]{2,0,1:T(1,128)S(1)}) fusion(f32[8,2,7,8]{3,0,2,1:T(8,128)} %constant.102.clone, s32[]{:T(128)S(6)} %select_n.53, s32[]{:T(128)S(6)} %add.58), kind=kLoop, calls=%fused_computation.45 | loop fusion | bytes 904 | tf_op jit(solution)/shard_map/slice | solution.py:228
  9.3 0.7 dynamic-slice_bitcast_fusion
  10.1 0.1 broadcast_multiply_fusion
  10.2 0.3 mul.94
  10.5 0.7 pad_maximum_fusion.w_ref
  11.3 19.9 %shard_map.64 = f32[12,216,512]{2,1,0:T(8,128)} custom-call(bf16[12,256,4096]{2,1,0:T(8,128)(2,1)} %bitcast.53, bf16[1024,256]{1,0:T(8,128)(2,1)} %constant.104.clone.main_ref, bf16[256,256]{1,0:T(8,128)(2,1)} %constant.105.clone.halo_ref, bf16[2,216,256]{2,1,0:T(8,128)(2,1)} %pad_maximum_fusion.w_ref), custom_call_target="tpu_custom_call" | custom-call | tf_op jit(solution)/shard_map/pallas_call | solution.py:96
  31.2 0.0 all-to-all-done
  31.2 0.5 broadcast.56
  31.7 0.7 reduce.2
  32.4 0.1 reshape.187
  32.5 0.4 fusion.7
  32.9 0.5 copy.37
  33.4 0.9 %reshape.181.idx_ref = s32[4096]{0:T(1024)} reshape(s32[32,32,4]{2,1,0:T(8,128)S(1)} %copy.37) | data formatting | bytes 32768 | tf_op jit(solution)/shard_map/reshape | solution.py:246
  34.3 17.4 %shard_map.65 = f32[32,36,128]{2,1,0:T(8,128)} custom-call(s32[4096]{0:T(1024)} %reshape.181.idx_ref, f32[36,72,512]{2,1,0:T(8,128)} %bitcast.54), custom_call_target="tpu_custom_call" | custom-call | tf_op jit(solution)/shard_map/pallas_call | solution.py:175
  51.7 5.8 %all-to-all-start.1 = ((f32[32,36,128]{2,1,0:T(8,128)}), f32[32,36,128]{2,1,0:T(8,128)S(1)}, u32[]{:S(2)}, u32[]{:S(2)}) async-start(f32[32,36,128]{2,1,0:T(8,128)} %shard_map.65), calls=%async_computation.1 | async-start | bytes 1310720 | tf_op jit(solution)/shard_map/all_to_all | solution.py:247
  57.5 0.7 fusion.11
  58.2 0.1 ge.23
  58.4 17.2 %all-to-all-done.1 = f32[32,36,128]{2,1,0:T(8,128)S(1)} async-done(((f32[32,36,128]{2,1,0:T(8,128)}), f32[32,36,128]{2,1,0:T(8,128)S(1)}, u32[]{:S(2)}, u32[]{:S(2)}) %all-to-all-start.1) | async-done | bytes 589856 | tf_op jit(solution)/shard_map/all_to_all | solution.py:247
  75.6 0.1 reduce_sum.72
  75.7 0.1 multiply_reduce_fusion
  75.8 0.2 concatenate.31
  76.0 0.6 multiply_convert_fusion
  (14 shorter events, 0.1 us)
Async XLA Ops:
  0.0 0.7 copy-start
  1.4 29.8 %all-to-all-start = ((s32[32,1,128]{2,1,0:T(1,128)}), s32[32,1,128]{2,1,0:T(1,128)S(1)}, u32[]{:S(2)}, u32[]{:S(2)}) async-start(s32[32,1,128]{2,1,0:T(1,128)} %reshape.186), calls=%async_computation | async-start | bytes 32768 | tf_op jit(solution)/shard_map/all_to_all | solution.py:220
  51.7 23.9 %all-to-all-start.1 = ((f32[32,36,128]{2,1,0:T(8,128)}), f32[32,36,128]{2,1,0:T(8,128)S(1)}, u32[]{:S(2)}, u32[]{:S(2)}) async-start(f32[32,36,128]{2,1,0:T(8,128)} %shard_map.65), calls=%async_computation.1 | async-start | bytes 1310720 | tf_op jit(solution)/shard_map/all_to_all | solution.py:247

commit v7 on v6

--- a/solution.py
+++ b/solution.py
@@ -120,8 +120,8 @@
     return np.stack(out)
 
 
-def pick_kernel(group_steps, step, chunk, owner_len):
-    def body(idx_ref, x_ref, o_ref, tab_ref, buf_ref):
+def pick_kernel(group_steps, step, chunk, owner_len, pack):
+    def body(idx_ref, x_ref, sel_ref, o_ref, tab_ref, buf_ref):
         j = pl.program_id(0)
         rows = x_ref.shape[0]
         lanes = x_ref.shape[2]
@@ -129,10 +129,11 @@
 
         @pl.when(j < group_steps)
         def _():
-            for gi in range(step):
-                slab = x_ref[:, gi, :]
-                slab = jnp.concatenate([slab, jnp.zeros((width - rows, lanes), slab.dtype)], axis=0)
-                at = pl.multiple_of((j * step + gi) * lanes, lanes)
+            for t in range(step):
+                parts = [x_ref[:, t * pack + k, :] for k in range(pack)]
+                parts.append(jnp.zeros((width - rows * pack, lanes), x_ref.dtype))
+                slab = jnp.concatenate(parts, axis=0)
+                at = pl.multiple_of((j * step + t) * lanes, lanes)
                 tab_ref[pl.ds(at, lanes), :] = slab.T
 
         @pl.when(j == group_steps - 1)
@@ -151,32 +152,39 @@
 
             lax.fori_loop(0, chunk, one, 0, unroll=8)
             flipped = buf_ref[...].T
+            sel = sel_ref[...]
+            picked = flipped[:rows]
+            for k in range(1, pack):
+                picked = jnp.where(sel == k, flipped[k * rows:(k + 1) * rows], picked)
             for owner in range(chunk // owner_len):
-                o_ref[owner] = flipped[:rows, owner * owner_len:(owner + 1) * owner_len]
+                o_ref[owner] = picked[:, owner * owner_len:(owner + 1) * owner_len]
 
     return body
 
 
-def pick_cells(x, flat, owner_len, chunk=2048):
+def pick_cells(x, flat, sel, owner_len, pack, chunk=2048):
     rows, groups, lanes = x.shape
     step = 8
-    group_steps = groups // step
+    group_steps = groups // (step * pack)
     entries = flat.shape[0]
     chunk = min(chunk, entries)
-    width = -(-rows // 128) * 128
+    width = -(-(rows * pack) // 128) * 128
     per_chunk = chunk // owner_len
     grid_spec = pltpu.PrefetchScalarGridSpec(
         num_scalar_prefetch=1,
         grid=(group_steps + entries // chunk,),
-        in_specs=[pl.BlockSpec((rows, step, lanes), lambda j, idx: (0, jnp.minimum(j, group_steps - 1), 0))],
+        in_specs=[
+            pl.BlockSpec((rows, step * pack, lanes), lambda j, idx: (0, jnp.minimum(j, group_steps - 1), 0)),
+            pl.BlockSpec((1, chunk), lambda j, idx: (0, jnp.maximum(j - group_steps, 0))),
+        ],
         out_specs=pl.BlockSpec((per_chunk, rows, owner_len), lambda j, idx: (jnp.maximum(j - group_steps, 0), 0, 0)),
-        scratch_shapes=[pltpu.VMEM((groups * lanes + 8, width), x.dtype), pltpu.VMEM((chunk, width), x.dtype)],
+        scratch_shapes=[pltpu.VMEM((groups // pack * lanes + 8, width), x.dtype), pltpu.VMEM((chunk, width), x.dtype)],
     )
     return pl.pallas_call(
-        pick_kernel(group_steps, step, chunk, owner_len),
+        pick_kernel(group_steps, step, chunk, owner_len, pack),
         out_shape=jax.ShapeDtypeStruct((entries // owner_len, rows, owner_len), x.dtype),
         grid_spec=grid_spec,
-    )(flat, x)
+    )(flat, x, sel)
 
 
 def model_tensors(coarse):
@@ -224,7 +232,8 @@
         wx = jnp.asarray(window_tables(row_count, local_x, full_x))[row]
         wy = jnp.asarray(window_tables(col_count, local_y, full_y))[col]
         group = x_count * y_count
-        padded = -(-group // 8) * 8
+        pack = 3
+        padded = -(-group // (8 * pack)) * 8 * pack
         xs = jnp.stack([wx[1], wx[0], wx[0]])
         ys = jnp.stack([wy[0], wy[1], wy[0]])
         weights = xs[:, :, None, :, None] * ys[:, None, :, None, :]
@@ -241,9 +250,12 @@
         at_x = (cell_pq // coarse_y - x_base) % coarse_x
         at_y = (cell_pq % coarse_y - y_base) % coarse_y
         inside = (at_x < x_count) & (at_y < y_count) & (by_owner >= 0)
-        flat = jnp.where(inside, (at_x * y_count + at_y) * coarse_z + at_z, padded * coarse_z)
+        at_group = at_x * y_count + at_y
+        flat = jnp.where(inside, (at_group // pack) * coarse_z + at_z, padded // pack * coarse_z)
+        sel = jnp.where(inside, at_group % pack, 0).reshape(1, -1)
         owner_len = devices * slots
-        taken = pick_cells(partials.reshape(field_count * 3, padded, coarse_z), flat.reshape(-1), owner_len)
+        partials = partials.reshape(field_count * 3, padded, coarse_z)
+        taken = pick_cells(partials, flat.reshape(-1), sel, owner_len, pack)
         arrived = lax.all_to_all(taken, ("rows", "cols"), split_axis=0, concat_axis=0, tiled=True)
         summed = jnp.sum(arrived, axis=0)
         rounded = lax.reduce_precision(summed, exponent_bits=8, mantissa_bits=7)

time: 77.5 us -> 74.8 us (0.965)
  Pallas kernels: 37.3 us -> 33.2 us
  local copies, waits for them, and re-layouts: 5.57 us -> 7.04 us
    pallas_call x1, Pallas kernels: 17.4 us -> 13.3 us  [pick_cells(): pl.pallas_call(pick_kernel(group_steps, step, chunk, owner_len, pack), ou...]
    reshape x1 -> x2, local copies, waits for them, and re-layouts: 0.87 us -> 1.8 us  [the longest x1 0.94 us: shards(): sel = jnp.where(inside, at_group % pack, 0).reshape(1, -1)]
  transfers between devices with their start and end apart: 2 -> 2, of which waited for: 1 -> 1; matrix products, arithmetic and copies ran while one was open for 5% -> 5% of each run, Pallas kernels for 26% -> 27%
where the time goes in v7:
time: 74.8 us; the launch traced here: 74.1 us
  Pallas kernels  33.2 us (44%)
  waiting for transfers between devices  17.2 us (23%)
  starting transfers between devices  12.9 us (17%)
  local copies, waits for them, and re-layouts  7.04 us (9%)
  other arithmetic  3.52 us (5%)
    pallas_call x1, Pallas kernels, filtered_partials(): pl.pallas_call(filter_kernel(block_count, coarse_block, value_rows, total...  19.9 us
    all_to_all x1, waiting for transfers between devices, shards(): lax.all_to_all(taken, ('rows', 'cols'), split_axis=0, concat_axis=0, tile...  17.2 us
    pallas_call x1, Pallas kernels, pick_cells(): pl.pallas_call(pick_kernel(group_steps, step, chunk, owner_len, pack), ou...  13.3 us
    all_to_all x1, starting transfers between devices, shards(): lax.all_to_all(copies, ('rows', 'cols'), split_axis=0, concat_axis=0, til...  7.1 us
    all_to_all x1, starting transfers between devices, shards(): lax.all_to_all(taken, ('rows', 'cols'), split_axis=0, concat_axis=0, tile...  5.83 us
  transfers between devices with their start and end apart: 2, of which 1 were waited for; matrix products, arithmetic and copies ran while one was open for 5% of the time, Pallas kernels for 27%

profile of v7, /device:TPU:1, one launch (start us, length us, event | category | flops | bytes accessed | tf_op | source)
XLA Modules:
  0.0 74.1 jit_solution(17901023362549447961)
XLA Ops:
  0.0 0.0 copy-start
  0.0 0.7 copy-done
  0.7 0.7 reshape.190
  1.4 7.1 %all-to-all-start = ((s32[32,1,128]{2,1,0:T(1,128)}), s32[32,1,128]{2,1,0:T(1,128)S(1)}, u32[]{:S(2)}, u32[]{:S(2)}) async-start(s32[32,1,128]{2,1,0:T(1,128)} %reshape.190), calls=%async_computation | async-start | bytes 32768 | tf_op jit(solution)/shard_map/all_to_all | solution.py:228
  8.5 0.8 %dynamic-slice_bitcast_fusion.3 = (f32[1,7,8]{2,0,1:T(1,128)S(1)}, f32[1,7,8]{2,0,1:T(1,128)S(1)}) fusion(f32[8,2,7,8]{3,0,2,1:T(8,128)} %constant.113.clone, s32[]{:T(128)S(6)} %select_n.64, s32[]{:T(128)S(6)} %add.64), kind=kLoop, calls=%fused_computation.54 | loop fusion | bytes 904 | tf_op jit(solution)/shard_map/slice | solution.py:237
  9.3 0.7 dynamic-slice_bitcast_fusion
  10.1 0.1 broadcast_multiply_fusion
  10.2 0.3 mul.94
  10.5 0.7 pad_maximum_fusion.w_ref
  11.3 19.9 %shard_map.64 = f32[12,216,512]{2,1,0:T(8,128)} custom-call(bf16[12,256,4096]{2,1,0:T(8,128)(2,1)} %bitcast.63, bf16[1024,256]{1,0:T(8,128)(2,1)} %constant.115.clone.main_ref, bf16[256,256]{1,0:T(8,128)(2,1)} %constant.116.clone.halo_ref, bf16[2,216,256]{2,1,0:T(8,128)(2,1)} %pad_maximum_fusion.w_ref), custom_call_target="tpu_custom_call" | custom-call | tf_op jit(solution)/shard_map/pallas_call | solution.py:96
  31.2 0.0 all-to-all-done
  31.2 0.5 broadcast.67
  31.7 0.7 reduce.2
  32.4 0.1 reshape.191
  32.5 0.5 fusion.8
  33.0 0.5 copy.29
  33.5 0.9 %reshape.188.sel_ref = s32[1,4096]{1,0:T(1,128)} reshape(s32[32,32,4]{2,1,0:T(8,128)S(1)} %copy.29) | data formatting | bytes 32768 | tf_op jit(solution)/shard_map/reshape | solution.py:255
  34.5 0.5 copy.27
  35.0 0.9 %reshape.184.idx_ref = s32[4096]{0:T(1024)} reshape(s32[32,32,4]{2,1,0:T(8,128)S(1)} %copy.27) | data formatting | bytes 32768 | tf_op jit(solution)/shard_map/reshape | solution.py:258
  35.9 13.3 %shard_map.65 = f32[32,36,128]{2,1,0:T(8,128)} custom-call(s32[4096]{0:T(1024)} %reshape.184.idx_ref, f32[36,72,512]{2,1,0:T(8,128)} %bitcast.64, s32[1,4096]{1,0:T(1,128)} %reshape.188.sel_ref), custom_call_target="tpu_custom_call" | custom-call | tf_op jit(solution)/shard_map/pallas_call | solution.py:183
  49.1 5.8 %all-to-all-start.1 = ((f32[32,36,128]{2,1,0:T(8,128)}), f32[32,36,128]{2,1,0:T(8,128)S(1)}, u32[]{:S(2)}, u32[]{:S(2)}) async-start(f32[32,36,128]{2,1,0:T(8,128)} %shard_map.65), calls=%async_computation.1 | async-start | bytes 1310720 | tf_op jit(solution)/shard_map/all_to_all | solution.py:259
  55.0 0.7 fusion.13
  55.7 0.1 ge.23
  55.8 17.2 %all-to-all-done.1 = f32[32,36,128]{2,1,0:T(8,128)S(1)} async-done(((f32[32,36,128]{2,1,0:T(8,128)}), f32[32,36,128]{2,1,0:T(8,128)S(1)}, u32[]{:S(2)}, u32[]{:S(2)}) %all-to-all-start.1) | async-done | bytes 589856 | tf_op jit(solution)/shard_map/all_to_all | solution.py:259
  73.0 0.1 reduce_sum.72
  73.2 0.1 multiply_reduce_fusion
  73.3 0.2 concatenate.31
  73.5 0.6 multiply_convert_fusion
  (14 shorter events, 0.1 us)
Async XLA Ops:
  0.0 0.7 copy-start
  1.4 29.8 %all-to-all-start = ((s32[32,1,128]{2,1,0:T(1,128)}), s32[32,1,128]{2,1,0:T(1,128)S(1)}, u32[]{:S(2)}, u32[]{:S(2)}) async-start(s32[32,1,128]{2,1,0:T(1,128)} %reshape.190), calls=%async_computation | async-start | bytes 32768 | tf_op jit(solution)/shard_map/all_to_all | solution.py:228
  49.1 23.9 %all-to-all-start.1 = ((f32[32,36,128]{2,1,0:T(8,128)}), f32[32,36,128]{2,1,0:T(8,128)S(1)}, u32[]{:S(2)}, u32[]{:S(2)}) async-start(f32[32,36,128]{2,1,0:T(8,128)} %shard_map.65), calls=%async_computation.1 | async-start | bytes 1310720 | tf_op jit(solution)/shard_map/all_to_all | solution.py:259

commit v8 on v7

--- a/solution.py
+++ b/solution.py
@@ -47,28 +47,29 @@
 
 def filter_kernel(block_count, coarse_block, value_rows, slope_rows):
     def body(x_ref, main_ref, halo_ref, w_ref, o_ref, zv_ref, zs_ref):
-        length = x_ref.shape[2]
+        per_step, rows, length = x_ref.shape
         blen = length // block_count
         for b in range(block_count):
-            main = x_ref[0, :, b * blen:(b + 1) * blen]
+            main = x_ref[:, :, b * blen:(b + 1) * blen].reshape(per_step * rows, blen)
             start = (b * blen - halo) % length
-            tail = x_ref[0, :, start:start + halo]
+            tail = x_ref[:, :, start:start + halo].reshape(per_step * rows, halo)
             start = ((b + 1) * blen) % length
-            head = x_ref[0, :, start:start + halo]
+            head = x_ref[:, :, start:start + halo].reshape(per_step * rows, halo)
             edges = jnp.concatenate([tail, head], axis=1)
             acc = jnp.dot(main, main_ref[...], preferred_element_type=jnp.float32)
             acc = acc + jnp.dot(edges, halo_ref[...], preferred_element_type=jnp.float32)
             lanes = slice(b * coarse_block, (b + 1) * coarse_block)
             zv_ref[:, lanes] = acc[:, :coarse_block].astype(jnp.bfloat16)
             zs_ref[:, lanes] = acc[:, coarse_block:].astype(jnp.bfloat16)
-        zv = zv_ref[...]
-        zs = zs_ref[...]
-        pv = jnp.dot(w_ref[0, :value_rows, :], zv, preferred_element_type=jnp.float32)
-        pv = pv + jnp.dot(w_ref[1, :value_rows, :], zv, preferred_element_type=jnp.float32)
-        ps = jnp.dot(w_ref[0, value_rows:, :], zs, preferred_element_type=jnp.float32)
-        ps = ps + jnp.dot(w_ref[1, value_rows:, :], zs, preferred_element_type=jnp.float32)
-        o_ref[0, :value_rows, :] = pv
-        o_ref[0, value_rows:, :] = ps
+        for k in range(per_step):
+            zv = zv_ref[k * rows:(k + 1) * rows, :]
+            zs = zs_ref[k * rows:(k + 1) * rows, :]
+            pv = jnp.dot(w_ref[0, :value_rows, :], zv, preferred_element_type=jnp.float32)
+            pv = pv + jnp.dot(w_ref[1, :value_rows, :], zv, preferred_element_type=jnp.float32)
+            ps = jnp.dot(w_ref[0, value_rows:, :], zs, preferred_element_type=jnp.float32)
+            ps = ps + jnp.dot(w_ref[1, value_rows:, :], zs, preferred_element_type=jnp.float32)
+            o_ref[k, :value_rows, :] = pv
+            o_ref[k, value_rows:, :] = ps
 
     return body
 
@@ -92,19 +93,20 @@
     total_rows = w.shape[1]
     value_rows = total_rows // 3 * 2
     coarse = length // 8
+    per_step = 2 if field_count % 2 == 0 else 1
     const = lambda f: (0, 0)
     return pl.pallas_call(
         filter_kernel(block_count, coarse_block, value_rows, total_rows - value_rows),
         out_shape=jax.ShapeDtypeStruct((field_count, total_rows, coarse), jnp.float32),
-        grid=(field_count,),
+        grid=(field_count // per_step,),
         in_specs=[
-            pl.BlockSpec((1, rows, length), lambda f: (f, 0, 0)),
+            pl.BlockSpec((per_step, rows, length), lambda f: (f, 0, 0)),
             pl.BlockSpec(main.shape, const),
             pl.BlockSpec(halo_w.shape, const),
             pl.BlockSpec(w.shape, lambda f: (0, 0, 0)),
         ],
-        out_specs=pl.BlockSpec((1, total_rows, coarse), lambda f: (f, 0, 0)),
-        scratch_shapes=[pltpu.VMEM((rows, coarse), jnp.bfloat16), pltpu.VMEM((rows, coarse), jnp.bfloat16)],
+        out_specs=pl.BlockSpec((per_step, total_rows, coarse), lambda f: (f, 0, 0)),
+        scratch_shapes=[pltpu.VMEM((per_step * rows, coarse), jnp.bfloat16)] * 2,
     )(fields3, main, halo_w, w)
 
 

time: 74.8 us -> 71 us (0.949)
  Pallas kernels: 33.2 us -> 29.5 us
    pallas_call x1, Pallas kernels: 19.9 us -> 16.2 us  [filtered_partials(): pl.pallas_call(filter_kernel(block_count, coarse_block, value_rows, total...]
  transfers between devices with their start and end apart: 2 -> 2, of which waited for: 1 -> 1; matrix products, arithmetic and copies ran while one was open for 5% -> 5% of each run, Pallas kernels for 27% -> 23%
where the time goes in v8:
time: 71 us; the launch traced here: 70.4 us
  Pallas kernels  29.5 us (42%)
  waiting for transfers between devices  17.2 us (24%)
  starting transfers between devices  12.9 us (18%)
  local copies, waits for them, and re-layouts  7.04 us (10%)
  other arithmetic  3.52 us (5%)
    all_to_all x1, waiting for transfers between devices, shards(): lax.all_to_all(taken, ('rows', 'cols'), split_axis=0, concat_axis=0, tile...  17.2 us
    pallas_call x1, Pallas kernels, filtered_partials(): pl.pallas_call(filter_kernel(block_count, coarse_block, value_rows, total...  16.2 us
    pallas_call x1, Pallas kernels, pick_cells(): pl.pallas_call(pick_kernel(group_steps, step, chunk, owner_len, pack), ou...  13.3 us
    all_to_all x1, starting transfers between devices, shards(): lax.all_to_all(copies, ('rows', 'cols'), split_axis=0, concat_axis=0, til...  7.1 us
    all_to_all x1, starting transfers between devices, shards(): lax.all_to_all(taken, ('rows', 'cols'), split_axis=0, concat_axis=0, tile...  5.81 us
    unnamed x5, local copies, waits for them, and re-layouts  1.49 us
  transfers between devices with their start and end apart: 2, of which 1 were waited for; matrix products, arithmetic and copies ran while one was open for 5% of the time, Pallas kernels for 23%

profile of v8, /device:TPU:1, one launch (start us, length us, event | category | flops | bytes accessed | tf_op | source)
XLA Modules:
  0.0 70.4 jit_solution(17195226564131576164)
XLA Ops:
  0.0 0.0 copy-start
  0.0 0.7 copy-done
  0.7 0.7 %reshape.190 = s32[32,1,128]{2,1,0:T(1,128)} reshape(s32[32,4,32]{2,1,0:T(4,128)S(1)} %broadcast_bitcast_fusion) | data formatting | bytes 32768
  1.4 7.1 %all-to-all-start = ((s32[32,1,128]{2,1,0:T(1,128)}), s32[32,1,128]{2,1,0:T(1,128)S(1)}, u32[]{:S(2)}, u32[]{:S(2)}) async-start(s32[32,1,128]{2,1,0:T(1,128)} %reshape.190), calls=%async_computation | async-start | bytes 32768 | tf_op jit(solution)/shard_map/all_to_all | solution.py:230
  8.5 0.8 %dynamic-slice_bitcast_fusion.3 = (f32[1,7,8]{2,0,1:T(1,128)S(1)}, f32[1,7,8]{2,0,1:T(1,128)S(1)}) fusion(f32[8,2,7,8]{3,0,2,1:T(8,128)} %constant.113.clone, s32[]{:T(128)S(6)} %select_n.64, s32[]{:T(128)S(6)} %add.64), kind=kLoop, calls=%fused_computation.54 | loop fusion | bytes 904 | tf_op jit(solution)/shard_map/slice | solution.py:239
  9.3 0.7 %dynamic-slice_bitcast_fusion = (f32[1,10,32]{2,1,0:T(8,128)S(1)}, f32[1,10,32]{2,1,0:T(8,128)S(1)}) fusion(f32[4,2,10,32]{3,2,1,0:T(8,128)} %constant.114.clone, s32[]{:T(128)S(6)} %select_n.65, s32[]{:T(128)S(6)} %add.64), kind=kLoop, calls=%fused_computation.51 | loop fusion | bytes 5128 | tf_op jit(solution)/shard_map/slice | solution.py:240
  10.1 0.1 broadcast_multiply_fusion
  10.2 0.3 mul.94
  10.5 0.7 %pad_maximum_fusion.w_ref = bf16[2,216,256]{2,1,0:T(8,128)(2,1)} fusion(bf16[1,216,256]{2,1,0:T(8,128)(2,1)S(1)} %get-tuple-element.11, bf16[1,216,256]{2,1,0:T(8,128)(2,1)S(1)} %get-tuple-element.12), kind=kLoop, calls=%fused_computation.1 | loop fusion | flops 110592 | bytes 442368 | tf_op jit(solution)/shard_map/stack | solution.py:80
  11.3 16.2 %shard_map.64 = f32[12,216,512]{2,1,0:T(8,128)} custom-call(bf16[12,256,4096]{2,1,0:T(8,128)(2,1)} %bitcast.63, bf16[1024,256]{1,0:T(8,128)(2,1)} %constant.115.clone.main_ref, bf16[256,256]{1,0:T(8,128)(2,1)} %constant.116.clone.halo_ref, bf16[2,216,256]{2,1,0:T(8,128)(2,1)} %pad_maximum_fusion.w_ref), custom_call_target="tpu_custom_call" | custom-call | tf_op jit(solution)/shard_map/pallas_call | solution.py:98
  27.5 0.0 all-to-all-done
  27.5 0.5 broadcast.67
  28.0 0.7 reduce.2
  28.7 0.1 reshape.191
  28.8 0.5 fusion.8
  29.3 0.5 copy.29
  29.9 0.9 %reshape.188.sel_ref = s32[1,4096]{1,0:T(1,128)} reshape(s32[32,32,4]{2,1,0:T(8,128)S(1)} %copy.29) | data formatting | bytes 32768 | tf_op jit(solution)/shard_map/reshape | solution.py:257
  30.8 0.5 copy.27
  31.3 0.9 %reshape.184.idx_ref = s32[4096]{0:T(1024)} reshape(s32[32,32,4]{2,1,0:T(8,128)S(1)} %copy.27) | data formatting | bytes 32768 | tf_op jit(solution)/shard_map/reshape | solution.py:260
  32.2 13.3 %shard_map.65 = f32[32,36,128]{2,1,0:T(8,128)} custom-call(s32[4096]{0:T(1024)} %reshape.184.idx_ref, f32[36,72,512]{2,1,0:T(8,128)} %bitcast.64, s32[1,4096]{1,0:T(1,128)} %reshape.188.sel_ref), custom_call_target="tpu_custom_call" | custom-call | tf_op jit(solution)/shard_map/pallas_call | solution.py:185
  45.5 5.8 %all-to-all-start.1 = ((f32[32,36,128]{2,1,0:T(8,128)}), f32[32,36,128]{2,1,0:T(8,128)S(1)}, u32[]{:S(2)}, u32[]{:S(2)}) async-start(f32[32,36,128]{2,1,0:T(8,128)} %shard_map.65), calls=%async_computation.1 | async-start | bytes 1310720 | tf_op jit(solution)/shard_map/all_to_all | solution.py:261
  51.3 0.7 fusion.13
  52.0 0.1 ge.23
  52.1 17.2 %all-to-all-done.1 = f32[32,36,128]{2,1,0:T(8,128)S(1)} async-done(((f32[32,36,128]{2,1,0:T(8,128)}), f32[32,36,128]{2,1,0:T(8,128)S(1)}, u32[]{:S(2)}, u32[]{:S(2)}) %all-to-all-start.1) | async-done | bytes 589856 | tf_op jit(solution)/shard_map/all_to_all | solution.py:261
  69.4 0.1 reduce_sum.72
  69.5 0.1 multiply_reduce_fusion
  69.6 0.2 concatenate.31
  69.8 0.6 multiply_convert_fusion
  (14 shorter events, 0.1 us)
Async XLA Ops:
  0.0 0.7 copy-start
  1.4 26.1 %all-to-all-start = ((s32[32,1,128]{2,1,0:T(1,128)}), s32[32,1,128]{2,1,0:T(1,128)S(1)}, u32[]{:S(2)}, u32[]{:S(2)}) async-start(s32[32,1,128]{2,1,0:T(1,128)} %reshape.190), calls=%async_computation | async-start | bytes 32768 | tf_op jit(solution)/shard_map/all_to_all | solution.py:230
  45.5 23.9 %all-to-all-start.1 = ((f32[32,36,128]{2,1,0:T(8,128)}), f32[32,36,128]{2,1,0:T(8,128)S(1)}, u32[]{:S(2)}, u32[]{:S(2)}) async-start(f32[32,36,128]{2,1,0:T(8,128)} %shard_map.65), calls=%async_computation.1 | async-start | bytes 1310720 | tf_op jit(solution)/shard_map/all_to_all | solution.py:261

commit v9 on v8

--- a/solution.py
+++ b/solution.py
@@ -93,7 +93,7 @@
     total_rows = w.shape[1]
     value_rows = total_rows // 3 * 2
     coarse = length // 8
-    per_step = 2 if field_count % 2 == 0 else 1
+    per_step = 4 if field_count % 4 == 0 else 1
     const = lambda f: (0, 0)
     return pl.pallas_call(
         filter_kernel(block_count, coarse_block, value_rows, total_rows - value_rows),

time: 71 us -> 70.6 us (level)
  no operation moved by 1% of the time
where the time goes in v9:
time: 70.6 us; the launch traced here: 70.1 us
  Pallas kernels  29.2 us (41%)
  waiting for transfers between devices  17.2 us (24%)
  starting transfers between devices  12.9 us (18%)
  local copies, waits for them, and re-layouts  7.04 us (10%)
  other arithmetic  3.52 us (5%)
    all_to_all x1, waiting for transfers between devices, shards(): lax.all_to_all(taken, ('rows', 'cols'), split_axis=0, concat_axis=0, tile...  17.2 us
    pallas_call x1, Pallas kernels, filtered_partials(): pl.pallas_call(filter_kernel(block_count, coarse_block, value_rows, total...  15.9 us
    pallas_call x1, Pallas kernels, pick_cells(): pl.pallas_call(pick_kernel(group_steps, step, chunk, owner_len, pack), ou...  13.3 us
    all_to_all x1, starting transfers between devices, shards(): lax.all_to_all(copies, ('rows', 'cols'), split_axis=0, concat_axis=0, til...  7.1 us
    all_to_all x1, starting transfers between devices, shards(): lax.all_to_all(taken, ('rows', 'cols'), split_axis=0, concat_axis=0, tile...  5.84 us
    unnamed x5, local copies, waits for them, and re-layouts  1.49 us
  transfers between devices with their start and end apart: 2, of which 1 were waited for; matrix products, arithmetic and copies ran while one was open for 5% of the time, Pallas kernels for 23%

profile of v9, /device:TPU:1, one launch (start us, length us, event | category | flops | bytes accessed | tf_op | source)
XLA Modules:
  0.0 70.1 jit_solution(354994028737340470)
XLA Ops:
  0.0 0.0 copy-start
  0.0 0.7 copy-done
  0.7 0.7 %reshape.190 = s32[32,1,128]{2,1,0:T(1,128)} reshape(s32[32,4,32]{2,1,0:T(4,128)S(1)} %broadcast_bitcast_fusion) | data formatting | bytes 32768
  1.4 7.1 %all-to-all-start = ((s32[32,1,128]{2,1,0:T(1,128)}), s32[32,1,128]{2,1,0:T(1,128)S(1)}, u32[]{:S(2)}, u32[]{:S(2)}) async-start(s32[32,1,128]{2,1,0:T(1,128)} %reshape.190), calls=%async_computation | async-start | bytes 32768 | tf_op jit(solution)/shard_map/all_to_all | solution.py:230
  8.5 0.8 %dynamic-slice_bitcast_fusion.3 = (f32[1,7,8]{2,0,1:T(1,128)S(1)}, f32[1,7,8]{2,0,1:T(1,128)S(1)}) fusion(f32[8,2,7,8]{3,0,2,1:T(8,128)} %constant.113.clone, s32[]{:T(128)S(6)} %select_n.64, s32[]{:T(128)S(6)} %add.64), kind=kLoop, calls=%fused_computation.54 | loop fusion | bytes 904 | tf_op jit(solution)/shard_map/slice | solution.py:239
  9.3 0.7 %dynamic-slice_bitcast_fusion = (f32[1,10,32]{2,1,0:T(8,128)S(1)}, f32[1,10,32]{2,1,0:T(8,128)S(1)}) fusion(f32[4,2,10,32]{3,2,1,0:T(8,128)} %constant.114.clone, s32[]{:T(128)S(6)} %select_n.65, s32[]{:T(128)S(6)} %add.64), kind=kLoop, calls=%fused_computation.51 | loop fusion | bytes 5128 | tf_op jit(solution)/shard_map/slice | solution.py:240
  10.1 0.1 broadcast_multiply_fusion
  10.2 0.3 mul.94
  10.5 0.7 %pad_maximum_fusion.w_ref = bf16[2,216,256]{2,1,0:T(8,128)(2,1)} fusion(bf16[1,216,256]{2,1,0:T(8,128)(2,1)S(1)} %get-tuple-element.11, bf16[1,216,256]{2,1,0:T(8,128)(2,1)S(1)} %get-tuple-element.12), kind=kLoop, calls=%fused_computation.1 | loop fusion | flops 110592 | bytes 442368 | tf_op jit(solution)/shard_map/stack | solution.py:80
  11.3 15.9 %shard_map.64 = f32[12,216,512]{2,1,0:T(8,128)} custom-call(bf16[12,256,4096]{2,1,0:T(8,128)(2,1)} %bitcast.63, bf16[1024,256]{1,0:T(8,128)(2,1)} %constant.115.clone.main_ref, bf16[256,256]{1,0:T(8,128)(2,1)} %constant.116.clone.halo_ref, bf16[2,216,256]{2,1,0:T(8,128)(2,1)} %pad_maximum_fusion.w_ref), custom_call_target="tpu_custom_call" | custom-call | tf_op jit(solution)/shard_map/pallas_call | solution.py:98
  27.2 0.0 all-to-all-done
  27.2 0.5 broadcast.67
  27.7 0.7 reduce.2
  28.4 0.1 reshape.191
  28.5 0.5 fusion.8
  29.0 0.5 copy.29
  29.6 0.9 %reshape.188.sel_ref = s32[1,4096]{1,0:T(1,128)} reshape(s32[32,32,4]{2,1,0:T(8,128)S(1)} %copy.29) | data formatting | bytes 32768 | tf_op jit(solution)/shard_map/reshape | solution.py:257
  30.5 0.5 copy.27
  31.0 0.9 %reshape.184.idx_ref = s32[4096]{0:T(1024)} reshape(s32[32,32,4]{2,1,0:T(8,128)S(1)} %copy.27) | data formatting | bytes 32768 | tf_op jit(solution)/shard_map/reshape | solution.py:260
  31.9 13.3 %shard_map.65 = f32[32,36,128]{2,1,0:T(8,128)} custom-call(s32[4096]{0:T(1024)} %reshape.184.idx_ref, f32[36,72,512]{2,1,0:T(8,128)} %bitcast.64, s32[1,4096]{1,0:T(1,128)} %reshape.188.sel_ref), custom_call_target="tpu_custom_call" | custom-call | tf_op jit(solution)/shard_map/pallas_call | solution.py:185
  45.2 5.8 %all-to-all-start.1 = ((f32[32,36,128]{2,1,0:T(8,128)}), f32[32,36,128]{2,1,0:T(8,128)S(1)}, u32[]{:S(2)}, u32[]{:S(2)}) async-start(f32[32,36,128]{2,1,0:T(8,128)} %shard_map.65), calls=%async_computation.1 | async-start | bytes 1310720 | tf_op jit(solution)/shard_map/all_to_all | solution.py:261
  51.0 0.7 fusion.13
  51.7 0.1 ge.23
  51.8 17.2 %all-to-all-done.1 = f32[32,36,128]{2,1,0:T(8,128)S(1)} async-done(((f32[32,36,128]{2,1,0:T(8,128)}), f32[32,36,128]{2,1,0:T(8,128)S(1)}, u32[]{:S(2)}, u32[]{:S(2)}) %all-to-all-start.1) | async-done | bytes 589856 | tf_op jit(solution)/shard_map/all_to_all | solution.py:261
  69.1 0.1 reduce_sum.72
  69.2 0.1 multiply_reduce_fusion
  69.3 0.2 concatenate.31
  69.5 0.6 multiply_convert_fusion
  (14 shorter events, 0.1 us)
Async XLA Ops:
  0.0 0.7 copy-start
  1.4 25.8 %all-to-all-start = ((s32[32,1,128]{2,1,0:T(1,128)}), s32[32,1,128]{2,1,0:T(1,128)S(1)}, u32[]{:S(2)}, u32[]{:S(2)}) async-start(s32[32,1,128]{2,1,0:T(1,128)} %reshape.190), calls=%async_computation | async-start | bytes 32768 | tf_op jit(solution)/shard_map/all_to_all | solution.py:230
  45.2 23.9 %all-to-all-start.1 = ((f32[32,36,128]{2,1,0:T(8,128)}), f32[32,36,128]{2,1,0:T(8,128)S(1)}, u32[]{:S(2)}, u32[]{:S(2)}) async-start(f32[32,36,128]{2,1,0:T(8,128)} %shard_map.65), calls=%async_computation.1 | async-start | bytes 1310720 | tf_op jit(solution)/shard_map/all_to_all | solution.py:261

commit v10 on v9

--- a/solution.py
+++ b/solution.py
@@ -258,8 +258,11 @@
         owner_len = devices * slots
         partials = partials.reshape(field_count * 3, padded, coarse_z)
         taken = pick_cells(partials, flat.reshape(-1), sel, owner_len, pack)
-        arrived = lax.all_to_all(taken, ("rows", "cols"), split_axis=0, concat_axis=0, tiled=True)
-        summed = jnp.sum(arrived, axis=0)
+        taken = taken.reshape(row_count, col_count, field_count * 3, owner_len)
+        by_row = lax.all_to_all(taken, "rows", split_axis=0, concat_axis=0, tiled=True)
+        by_row = jnp.sum(by_row, axis=0)
+        by_col = lax.all_to_all(by_row, "cols", split_axis=0, concat_axis=0, tiled=True)
+        summed = jnp.sum(by_col, axis=0)
         rounded = lax.reduce_precision(summed, exponent_bits=8, mantissa_bits=7)
         mine = lax.dynamic_index_in_dim(by_owner, me, axis=0, keepdims=False).reshape(-1)
         picked = jnp.where(mine[None, :] >= 0, rounded, jnp.zeros_like(rounded))

time: 70.6 us -> 73.6 us (1.042)
  the two profiles are of different devices: /device:TPU:1 before, /device:TPU:0 now
where the time goes in v10:
time: 73.6 us; the launch traced here: 73 us
  Pallas kernels  29.2 us (40%)
  blocking collectives  14.2 us (19%)
  starting transfers between devices  11.9 us (16%)
  local copies, waits for them, and re-layouts  8.94 us (12%)
  waiting for transfers between devices  4.97 us (7%)
  other arithmetic  3.58 us (5%)
    pallas_call x1, Pallas kernels, filtered_partials(): pl.pallas_call(filter_kernel(block_count, coarse_block, value_rows, total...  15.9 us
    all_to_all x1, blocking collectives, shards(): lax.all_to_all(taken, 'rows', split_axis=0, concat_axis=0, tiled=True)  14.2 us
    pallas_call x1, Pallas kernels, pick_cells(): pl.pallas_call(pick_kernel(group_steps, step, chunk, owner_len, pack), ou...  13.3 us
    all_to_all x1, starting transfers between devices, shards(): lax.all_to_all(copies, ('rows', 'cols'), split_axis=0, concat_axis=0, til...  7.3 us
    all_to_all x1, waiting for transfers between devices, shards(): lax.all_to_all(by_row, 'cols', split_axis=0, concat_axis=0, tiled=True)  4.97 us
    all_to_all x1, starting transfers between devices, shards(): lax.all_to_all(by_row, 'cols', split_axis=0, concat_axis=0, tiled=True)  4.64 us
    unnamed x5, local copies, waits for them, and re-layouts  1.49 us
  transfers between devices with their start and end apart: 2, of which 1 were waited for; matrix products, arithmetic and copies ran while one was open for 5% of the time, Pallas kernels for 22%

profile of v10, /device:TPU:0, one launch (start us, length us, event | category | flops | bytes accessed | tf_op | source)
XLA Modules:
  0.0 73.0 jit_solution(600835931541707153)
XLA Ops:
  0.0 0.0 copy-start
  0.0 0.7 copy-done
  0.7 0.7 reshape.194
  1.4 7.3 %all-to-all-start = ((s32[32,1,128]{2,1,0:T(1,128)}), s32[32,1,128]{2,1,0:T(1,128)S(1)}, u32[]{:S(2)}, u32[]{:S(2)}) async-start(s32[32,1,128]{2,1,0:T(1,128)} %reshape.194), calls=%async_computation | async-start | bytes 32768 | tf_op jit(solution)/shard_map/all_to_all | solution.py:230
  8.7 0.8 %dynamic-slice_bitcast_fusion.3 = (f32[1,7,8]{2,0,1:T(1,128)S(1)}, f32[1,7,8]{2,0,1:T(1,128)S(1)}) fusion(f32[8,2,7,8]{3,0,2,1:T(8,128)} %constant.113.clone, s32[]{:T(128)S(6)} %select_n.64, s32[]{:T(128)S(6)} %add.64), kind=kLoop, calls=%fused_computation.54 | loop fusion | bytes 904 | tf_op jit(solution)/shard_map/slice | solution.py:239
  9.5 0.7 dynamic-slice_bitcast_fusion
  10.3 0.1 broadcast_multiply_fusion
  10.4 0.3 mul.94
  10.7 0.7 pad_maximum_fusion.w_ref
  11.5 15.9 %shard_map.64 = f32[12,216,512]{2,1,0:T(8,128)} custom-call(bf16[12,256,4096]{2,1,0:T(8,128)(2,1)} %bitcast.64, bf16[1024,256]{1,0:T(8,128)(2,1)} %constant.115.clone.main_ref, bf16[256,256]{1,0:T(8,128)(2,1)} %constant.116.clone.halo_ref, bf16[2,216,256]{2,1,0:T(8,128)(2,1)} %pad_maximum_fusion.w_ref), custom_call_target="tpu_custom_call" | custom-call | tf_op jit(solution)/shard_map/pallas_call | solution.py:98
  27.4 0.0 all-to-all-done
  27.4 0.5 broadcast.67
  27.9 0.7 reduce.2
  28.6 0.1 reshape.195
  28.7 0.5 fusion.8
  29.2 0.6 copy.45
  29.8 0.9 %reshape.191.sel_ref = s32[1,4096]{1,0:T(1,128)} reshape(s32[32,32,4]{2,1,0:T(8,128)S(1)} %copy.45) | data formatting | bytes 32768 | tf_op jit(solution)/shard_map/reshape | solution.py:257
  30.7 0.5 copy.43
  31.3 0.9 %reshape.187.idx_ref = s32[4096]{0:T(1024)} reshape(s32[32,32,4]{2,1,0:T(8,128)S(1)} %copy.43) | data formatting | bytes 32768 | tf_op jit(solution)/shard_map/reshape | solution.py:260
  32.1 13.3 %shard_map.65 = f32[32,36,128]{2,1,0:T(8,128)} custom-call(s32[4096]{0:T(1024)} %reshape.187.idx_ref, f32[36,72,512]{2,1,0:T(8,128)} %bitcast.65, s32[1,4096]{1,0:T(1,128)} %reshape.191.sel_ref), custom_call_target="tpu_custom_call" | custom-call | tf_op jit(solution)/shard_map/pallas_call | solution.py:185
  45.4 1.2 %copy.46 = f32[8,4,36,128]{3,1,2,0:T(4,128)S(1)} copy(f32[8,4,36,128]{3,2,1,0:T(8,128)} %bitcast.66) | data formatting | bytes 1179648 | tf_op jit(solution)/shard_map/reshape | solution.py:261
  46.7 14.2 %all_to_all.15 = f32[8,4,36,128]{3,1,2,0:T(4,128)S(1)} all-to-all(f32[8,4,36,128]{3,1,2,0:T(4,128)S(1)} %copy.46), channel_id=1, replica_groups=mesh['rows'=8,'cols'=4] {'rows'}, dimensions={0} | all-to-all | bytes 1179648 | tf_op jit(solution)/shard_map/all_to_all | solution.py:262
  60.8 0.1 reduce_sum.81
  60.9 0.6 copy.47
  61.6 4.6 %all-to-all-start.2 = ((f32[4,36,128]{2,1,0:T(8,128)}), f32[4,36,128]{2,1,0:T(8,128)S(1)}, u32[]{:S(2)}, u32[]{:S(2)}) async-start(f32[4,36,128]{2,1,0:T(8,128)} %copy.47), calls=%async_computation.2 | async-start | bytes 163840 | tf_op jit(solution)/shard_map/all_to_all | solution.py:264
  66.2 0.7 fusion.13
  66.9 0.1 ge.23
  67.0 5.0 %all-to-all-done.2 = f32[4,36,128]{2,1,0:T(8,128)S(1)} async-done(((f32[4,36,128]{2,1,0:T(8,128)}), f32[4,36,128]{2,1,0:T(8,128)S(1)}, u32[]{:S(2)}, u32[]{:S(2)}) %all-to-all-start.2) | async-done | bytes 73760 | tf_op jit(solution)/shard_map/all_to_all | solution.py:264
  72.1 0.1 multiply_reduce_fusion
  72.2 0.2 concatenate.31
  72.4 0.6 multiply_convert_fusion
  (15 shorter events, 0.2 us)
Async XLA Ops:
  0.0 0.7 copy-start
  1.4 26.0 %all-to-all-start = ((s32[32,1,128]{2,1,0:T(1,128)}), s32[32,1,128]{2,1,0:T(1,128)S(1)}, u32[]{:S(2)}, u32[]{:S(2)}) async-start(s32[32,1,128]{2,1,0:T(1,128)} %reshape.194), calls=%async_computation | async-start | bytes 32768 | tf_op jit(solution)/shard_map/all_to_all | solution.py:230
  61.6 10.4 %all-to-all-start.2 = ((f32[4,36,128]{2,1,0:T(8,128)}), f32[4,36,128]{2,1,0:T(8,128)S(1)}, u32[]{:S(2)}, u32[]{:S(2)}) async-start(f32[4,36,128]{2,1,0:T(8,128)} %copy.47), calls=%async_computation.2 | async-start | bytes 163840 | tf_op jit(solution)/shard_map/all_to_all | solution.py:264

commit v11 on v9

--- a/solution.py
+++ b/solution.py
@@ -148,13 +148,13 @@
             base = (j - group_steps) * chunk
 
             def one(e, carry):
-                at = idx_ref[base + e]
+                at = idx_ref[base + e] // 4
                 buf_ref[pl.ds(e, 1), :] = tab_ref[pl.ds(at, 1), :]
                 return carry
 
             lax.fori_loop(0, chunk, one, 0, unroll=8)
             flipped = buf_ref[...].T
-            sel = sel_ref[...]
+            sel = sel_ref[...] % 4
             picked = flipped[:rows]
             for k in range(1, pack):
                 picked = jnp.where(sel == k, flipped[k * rows:(k + 1) * rows], picked)
@@ -164,11 +164,11 @@
     return body
 
 
-def pick_cells(x, flat, sel, owner_len, pack, chunk=2048):
+def pick_cells(x, coded, owner_len, pack, chunk=4096):
     rows, groups, lanes = x.shape
     step = 8
     group_steps = groups // (step * pack)
-    entries = flat.shape[0]
+    entries = coded.shape[0]
     chunk = min(chunk, entries)
     width = -(-(rows * pack) // 128) * 128
     per_chunk = chunk // owner_len
@@ -186,7 +186,7 @@
         pick_kernel(group_steps, step, chunk, owner_len, pack),
         out_shape=jax.ShapeDtypeStruct((entries // owner_len, rows, owner_len), x.dtype),
         grid_spec=grid_spec,
-    )(flat, x, sel)
+    )(coded, x, coded.reshape(1, -1))
 
 
 def model_tensors(coarse):
@@ -254,10 +254,10 @@
         inside = (at_x < x_count) & (at_y < y_count) & (by_owner >= 0)
         at_group = at_x * y_count + at_y
         flat = jnp.where(inside, (at_group // pack) * coarse_z + at_z, padded // pack * coarse_z)
-        sel = jnp.where(inside, at_group % pack, 0).reshape(1, -1)
+        coded = flat * 4 + jnp.where(inside, at_group % pack, 0)
         owner_len = devices * slots
         partials = partials.reshape(field_count * 3, padded, coarse_z)
-        taken = pick_cells(partials, flat.reshape(-1), sel, owner_len, pack)
+        taken = pick_cells(partials, coded.reshape(-1), owner_len, pack)
         arrived = lax.all_to_all(taken, ("rows", "cols"), split_axis=0, concat_axis=0, tiled=True)
         summed = jnp.sum(arrived, axis=0)
         rounded = lax.reduce_precision(summed, exponent_bits=8, mantissa_bits=7)

time: 70.6 us -> 88.4 us (1.25)
  Pallas kernels: 29.2 us -> 47.5 us
    pallas_call x1, Pallas kernels: 13.3 us -> 31.6 us  [pick_cells(): pl.pallas_call(pick_kernel(group_steps, step, chunk, owner_len, pack), ou...]
    select_n x2 -> x0, local copies, waits for them, and re-layouts: 1.06 us -> none  [the longest x1 0.53 us: shards(): sel = jnp.where(inside, at_group % pack, 0).reshape(1, -1)]
    reshape x2 -> x1, local copies, waits for them, and re-layouts: 1.8 us -> 0.87 us  [shards(): taken = pick_cells(partials, coded.reshape(-1), owner_len, pack)]
    another operation x0 -> x1, local copies, waits for them, and re-layouts: none -> 0.94 us  [pick_cells(): coded.reshape(1, -1)]
  transfers between devices with their start and end apart: 2 -> 2, of which waited for: 1 -> 1; matrix products, arithmetic and copies ran while one was open for 5% -> 4% of each run, Pallas kernels for 23% -> 18%
where the time goes in v11:
time: 88.4 us; the launch traced here: 87.9 us
  Pallas kernels  47.5 us (54%)
  waiting for transfers between devices  17.2 us (19%)
  starting transfers between devices  12.9 us (15%)
  local copies, waits for them, and re-layouts  6.51 us (7%)
  other arithmetic  3.54 us (4%)
    pallas_call x1, Pallas kernels, pick_cells(): pl.pallas_call(pick_kernel(group_steps, step, chunk, owner_len, pack), ou...  31.6 us
    all_to_all x1, waiting for transfers between devices, shards(): lax.all_to_all(taken, ('rows', 'cols'), split_axis=0, concat_axis=0, tile...  17.2 us
    pallas_call x1, Pallas kernels, filtered_partials(): pl.pallas_call(filter_kernel(block_count, coarse_block, value_rows, total...  15.9 us
    all_to_all x1, starting transfers between devices, shards(): lax.all_to_all(copies, ('rows', 'cols'), split_axis=0, concat_axis=0, til...  7.1 us
    all_to_all x1, starting transfers between devices, shards(): lax.all_to_all(taken, ('rows', 'cols'), split_axis=0, concat_axis=0, tile...  5.84 us
  transfers between devices with their start and end apart: 2, of which 1 were waited for; matrix products, arithmetic and copies ran while one was open for 4% of the time, Pallas kernels for 18%

profile of v11, /device:TPU:1, one launch (start us, length us, event | category | flops | bytes accessed | tf_op | source)
XLA Modules:
  0.0 87.9 jit_solution(8624805404395765975)
XLA Ops:
  0.0 0.0 copy-start
  0.0 0.7 copy-done
  0.7 0.7 reshape.186
  1.4 7.1 %all-to-all-start = ((s32[32,1,128]{2,1,0:T(1,128)}), s32[32,1,128]{2,1,0:T(1,128)S(1)}, u32[]{:S(2)}, u32[]{:S(2)}) async-start(s32[32,1,128]{2,1,0:T(1,128)} %reshape.186), calls=%async_computation | async-start | bytes 32768 | tf_op jit(solution)/shard_map/all_to_all | solution.py:230
  8.5 0.8 dynamic-slice_bitcast_fusion.3
  9.3 0.7 dynamic-slice_bitcast_fusion
  10.1 0.1 broadcast_multiply_fusion
  10.2 0.3 mul.99
  10.5 0.7 pad_maximum_fusion.w_ref
  11.3 15.9 %shard_map.64 = f32[12,216,512]{2,1,0:T(8,128)} custom-call(bf16[12,256,4096]{2,1,0:T(8,128)(2,1)} %bitcast.53, bf16[1024,256]{1,0:T(8,128)(2,1)} %constant.116.clone.main_ref, bf16[256,256]{1,0:T(8,128)(2,1)} %constant.117.clone.halo_ref, bf16[2,216,256]{2,1,0:T(8,128)(2,1)} %pad_maximum_fusion.w_ref), custom_call_target="tpu_custom_call" | custom-call | tf_op jit(solution)/shard_map/pallas_call | solution.py:98
  27.2 0.0 all-to-all-done
  27.2 0.5 broadcast.58
  27.7 0.7 reduce.2
  28.4 0.1 reshape.187
  28.5 0.5 fusion.9
  29.0 0.5 copy.27
  29.6 0.9 %reshape_reshape.3.sel_ref = s32[1,4096]{1,0:T(1,128)} reshape(s32[32,32,4]{2,1,0:T(8,128)S(1)} %copy.27) | data formatting | bytes 32768 | tf_op jit(solution)/shard_map/reshape;reshape | solution.py:189
  30.5 0.9 reshape.181.idx_ref
  31.4 31.6 %shard_map.65 = f32[32,36,128]{2,1,0:T(8,128)} custom-call(s32[4096]{0:T(1024)} %reshape.181.idx_ref, f32[36,72,512]{2,1,0:T(8,128)} %bitcast.54, s32[1,4096]{1,0:T(1,128)} %reshape_reshape.3.sel_ref), custom_call_target="tpu_custom_call" | custom-call | tf_op jit(solution)/shard_map/pallas_call | solution.py:185
  63.0 5.8 %all-to-all-start.1 = ((f32[32,36,128]{2,1,0:T(8,128)}), f32[32,36,128]{2,1,0:T(8,128)S(1)}, u32[]{:S(2)}, u32[]{:S(2)}) async-start(f32[32,36,128]{2,1,0:T(8,128)} %shard_map.65), calls=%async_computation.1 | async-start | bytes 1310720 | tf_op jit(solution)/shard_map/all_to_all | solution.py:261
  68.8 0.7 fusion.15
  69.5 0.1 ge.23
  69.7 17.2 %all-to-all-done.1 = f32[32,36,128]{2,1,0:T(8,128)S(1)} async-done(((f32[32,36,128]{2,1,0:T(8,128)}), f32[32,36,128]{2,1,0:T(8,128)S(1)}, u32[]{:S(2)}, u32[]{:S(2)}) %all-to-all-start.1) | async-done | bytes 589856 | tf_op jit(solution)/shard_map/all_to_all | solution.py:261
  86.9 0.1 reduce_sum.72
  87.0 0.1 multiply_reduce_fusion
  87.1 0.2 concatenate.31
  87.3 0.6 multiply_convert_fusion
  (14 shorter events, 0.1 us)
Async XLA Ops:
  0.0 0.7 copy-start
  1.4 25.8 %all-to-all-start = ((s32[32,1,128]{2,1,0:T(1,128)}), s32[32,1,128]{2,1,0:T(1,128)S(1)}, u32[]{:S(2)}, u32[]{:S(2)}) async-start(s32[32,1,128]{2,1,0:T(1,128)} %reshape.186), calls=%async_computation | async-start | bytes 32768 | tf_op jit(solution)/shard_map/all_to_all | solution.py:230
  63.0 23.9 %all-to-all-start.1 = ((f32[32,36,128]{2,1,0:T(8,128)}), f32[32,36,128]{2,1,0:T(8,128)S(1)}, u32[]{:S(2)}, u32[]{:S(2)}) async-start(f32[32,36,128]{2,1,0:T(8,128)} %shard_map.65), calls=%async_computation.1 | async-start | bytes 1310720 | tf_op jit(solution)/shard_map/all_to_all | solution.py:261

commit v12 on v9

--- a/solution.py
+++ b/solution.py
@@ -127,7 +127,7 @@
         j = pl.program_id(0)
         rows = x_ref.shape[0]
         lanes = x_ref.shape[2]
-        width = tab_ref.shape[1]
+        width = tab_ref.shape[2]
 
         @pl.when(j < group_steps)
         def _():
@@ -135,25 +135,27 @@
                 parts = [x_ref[:, t * pack + k, :] for k in range(pack)]
                 parts.append(jnp.zeros((width - rows * pack, lanes), x_ref.dtype))
                 slab = jnp.concatenate(parts, axis=0)
-                at = pl.multiple_of((j * step + t) * lanes, lanes)
-                tab_ref[pl.ds(at, lanes), :] = slab.T
+                at = pl.multiple_of((j * step + t) * (lanes // 8), lanes // 8)
+                tab_ref[pl.ds(at, lanes // 8), :, :] = slab.T.reshape(lanes // 8, 8, width)
 
         @pl.when(j == group_steps - 1)
         def _():
-            tail = tab_ref.shape[0] - 8
-            tab_ref[pl.ds(tail, 8), :] = jnp.zeros((8, width), tab_ref.dtype)
+            tab_ref[tab_ref.shape[0] - 1] = jnp.zeros((8, width), tab_ref.dtype)
 
         @pl.when(j >= group_steps)
         def _():
             base = (j - group_steps) * chunk
 
-            def one(e, carry):
-                at = idx_ref[base + e]
-                buf_ref[pl.ds(e, 1), :] = tab_ref[pl.ds(at, 1), :]
+            def eight(i, carry):
+                for k in range(8):
+                    code = idx_ref[base + i * 8 + k]
+                    tile = lax.shift_right_logical(code, 3)
+                    row = tab_ref[tile, pl.ds(code & 7, 1), :]
+                    buf_ref[i, pl.ds(k, 1), :] = row
                 return carry
 
-            lax.fori_loop(0, chunk, one, 0, unroll=8)
-            flipped = buf_ref[...].T
+            lax.fori_loop(0, chunk // 8, eight, 0)
+            flipped = buf_ref[...].reshape(chunk, width).T
             sel = sel_ref[...]
             picked = flipped[:rows]
             for k in range(1, pack):
@@ -180,7 +182,7 @@
             pl.BlockSpec((1, chunk), lambda j, idx: (0, jnp.maximum(j - group_steps, 0))),
         ],
         out_specs=pl.BlockSpec((per_chunk, rows, owner_len), lambda j, idx: (jnp.maximum(j - group_steps, 0), 0, 0)),
-        scratch_shapes=[pltpu.VMEM((groups // pack * lanes + 8, width), x.dtype), pltpu.VMEM((chunk, width), x.dtype)],
+        scratch_shapes=[pltpu.VMEM((groups // pack * lanes // 8 + 1, 8, width), x.dtype), pltpu.VMEM((chunk // 8, 8, width), x.dtype)],
     )
     return pl.pallas_call(
         pick_kernel(group_steps, step, chunk, owner_len, pack),

time: 70.6 us -> 70.6 us (level)
  no operation moved by 1% of the time
where the time goes in v12:
time: 70.6 us; the launch traced here: 70.1 us
  Pallas kernels  29.2 us (41%)
  waiting for transfers between devices  17.2 us (24%)
  starting transfers between devices  12.9 us (18%)
  local copies, waits for them, and re-layouts  7.04 us (10%)
  other arithmetic  3.52 us (5%)
    all_to_all x1, waiting for transfers between devices, shards(): lax.all_to_all(taken, ('rows', 'cols'), split_axis=0, concat_axis=0, tile...  17.2 us
    pallas_call x1, Pallas kernels, filtered_partials(): pl.pallas_call(filter_kernel(block_count, coarse_block, value_rows, total...  15.9 us
    pallas_call x1, Pallas kernels, pick_cells(): pl.pallas_call(pick_kernel(group_steps, step, chunk, owner_len, pack), ou...  13.3 us
    all_to_all x1, starting transfers between devices, shards(): lax.all_to_all(copies, ('rows', 'cols'), split_axis=0, concat_axis=0, til...  7.1 us
    all_to_all x1, starting transfers between devices, shards(): lax.all_to_all(taken, ('rows', 'cols'), split_axis=0, concat_axis=0, tile...  5.84 us
    unnamed x5, local copies, waits for them, and re-layouts  1.49 us
  transfers between devices with their start and end apart: 2, of which 1 were waited for; matrix products, arithmetic and copies ran while one was open for 5% of the time, Pallas kernels for 23%

profile of v12, /device:TPU:1, one launch (start us, length us, event | category | flops | bytes accessed | tf_op | source)
XLA Modules:
  0.0 70.1 jit_solution(4619430415438527499)
XLA Ops:
  0.0 0.0 copy-start
  0.0 0.7 copy-done
  0.7 0.7 %reshape.190 = s32[32,1,128]{2,1,0:T(1,128)} reshape(s32[32,4,32]{2,1,0:T(4,128)S(1)} %broadcast_bitcast_fusion) | data formatting | bytes 32768
  1.4 7.1 %all-to-all-start = ((s32[32,1,128]{2,1,0:T(1,128)}), s32[32,1,128]{2,1,0:T(1,128)S(1)}, u32[]{:S(2)}, u32[]{:S(2)}) async-start(s32[32,1,128]{2,1,0:T(1,128)} %reshape.190), calls=%async_computation | async-start | bytes 32768 | tf_op jit(solution)/shard_map/all_to_all | solution.py:232
  8.5 0.8 %dynamic-slice_bitcast_fusion.3 = (f32[1,7,8]{2,0,1:T(1,128)S(1)}, f32[1,7,8]{2,0,1:T(1,128)S(1)}) fusion(f32[8,2,7,8]{3,0,2,1:T(8,128)} %constant.113.clone, s32[]{:T(128)S(6)} %select_n.64, s32[]{:T(128)S(6)} %add.64), kind=kLoop, calls=%fused_computation.54 | loop fusion | bytes 904 | tf_op jit(solution)/shard_map/slice | solution.py:241
  9.3 0.7 %dynamic-slice_bitcast_fusion = (f32[1,10,32]{2,1,0:T(8,128)S(1)}, f32[1,10,32]{2,1,0:T(8,128)S(1)}) fusion(f32[4,2,10,32]{3,2,1,0:T(8,128)} %constant.114.clone, s32[]{:T(128)S(6)} %select_n.65, s32[]{:T(128)S(6)} %add.64), kind=kLoop, calls=%fused_computation.51 | loop fusion | bytes 5128 | tf_op jit(solution)/shard_map/slice | solution.py:242
  10.1 0.1 broadcast_multiply_fusion
  10.2 0.3 mul.94
  10.5 0.7 %pad_maximum_fusion.w_ref = bf16[2,216,256]{2,1,0:T(8,128)(2,1)} fusion(bf16[1,216,256]{2,1,0:T(8,128)(2,1)S(1)} %get-tuple-element.11, bf16[1,216,256]{2,1,0:T(8,128)(2,1)S(1)} %get-tuple-element.12), kind=kLoop, calls=%fused_computation.1 | loop fusion | flops 110592 | bytes 442368 | tf_op jit(solution)/shard_map/stack | solution.py:80
  11.3 15.9 %shard_map.64 = f32[12,216,512]{2,1,0:T(8,128)} custom-call(bf16[12,256,4096]{2,1,0:T(8,128)(2,1)} %bitcast.63, bf16[1024,256]{1,0:T(8,128)(2,1)} %constant.115.clone.main_ref, bf16[256,256]{1,0:T(8,128)(2,1)} %constant.116.clone.halo_ref, bf16[2,216,256]{2,1,0:T(8,128)(2,1)} %pad_maximum_fusion.w_ref), custom_call_target="tpu_custom_call" | custom-call | tf_op jit(solution)/shard_map/pallas_call | solution.py:98
  27.2 0.0 all-to-all-done
  27.2 0.5 broadcast.67
  27.7 0.7 reduce.2
  28.4 0.1 reshape.191
  28.5 0.5 fusion.8
  29.0 0.5 copy.29
  29.6 0.9 %reshape.188.sel_ref = s32[1,4096]{1,0:T(1,128)} reshape(s32[32,32,4]{2,1,0:T(8,128)S(1)} %copy.29) | data formatting | bytes 32768 | tf_op jit(solution)/shard_map/reshape | solution.py:259
  30.5 0.5 copy.27
  31.0 0.9 %reshape.184.idx_ref = s32[4096]{0:T(1024)} reshape(s32[32,32,4]{2,1,0:T(8,128)S(1)} %copy.27) | data formatting | bytes 32768 | tf_op jit(solution)/shard_map/reshape | solution.py:262
  31.9 13.3 %shard_map.65 = f32[32,36,128]{2,1,0:T(8,128)} custom-call(s32[4096]{0:T(1024)} %reshape.184.idx_ref, f32[36,72,512]{2,1,0:T(8,128)} %bitcast.64, s32[1,4096]{1,0:T(1,128)} %reshape.188.sel_ref), custom_call_target="tpu_custom_call" | custom-call | tf_op jit(solution)/shard_map/pallas_call | solution.py:187
  45.2 5.8 %all-to-all-start.1 = ((f32[32,36,128]{2,1,0:T(8,128)}), f32[32,36,128]{2,1,0:T(8,128)S(1)}, u32[]{:S(2)}, u32[]{:S(2)}) async-start(f32[32,36,128]{2,1,0:T(8,128)} %shard_map.65), calls=%async_computation.1 | async-start | bytes 1310720 | tf_op jit(solution)/shard_map/all_to_all | solution.py:263
  51.0 0.7 fusion.13
  51.7 0.1 ge.23
  51.8 17.2 %all-to-all-done.1 = f32[32,36,128]{2,1,0:T(8,128)S(1)} async-done(((f32[32,36,128]{2,1,0:T(8,128)}), f32[32,36,128]{2,1,0:T(8,128)S(1)}, u32[]{:S(2)}, u32[]{:S(2)}) %all-to-all-start.1) | async-done | bytes 589856 | tf_op jit(solution)/shard_map/all_to_all | solution.py:263
  69.1 0.1 reduce_sum.72
  69.2 0.1 multiply_reduce_fusion
  69.3 0.2 concatenate.31
  69.5 0.6 multiply_convert_fusion
  (14 shorter events, 0.1 us)
Async XLA Ops:
  0.0 0.7 copy-start
  1.4 25.8 %all-to-all-start = ((s32[32,1,128]{2,1,0:T(1,128)}), s32[32,1,128]{2,1,0:T(1,128)S(1)}, u32[]{:S(2)}, u32[]{:S(2)}) async-start(s32[32,1,128]{2,1,0:T(1,128)} %reshape.190), calls=%async_computation | async-start | bytes 32768 | tf_op jit(solution)/shard_map/all_to_all | solution.py:232
  45.2 23.9 %all-to-all-start.1 = ((f32[32,36,128]{2,1,0:T(8,128)}), f32[32,36,128]{2,1,0:T(8,128)S(1)}, u32[]{:S(2)}, u32[]{:S(2)}) async-start(f32[32,36,128]{2,1,0:T(8,128)} %shard_map.65), calls=%async_computation.1 | async-start | bytes 1310720 | tf_op jit(solution)/shard_map/all_to_all | solution.py:263

commit v13 on v12

--- a/solution.py
+++ b/solution.py
@@ -46,7 +46,7 @@
 
 
 def filter_kernel(block_count, coarse_block, value_rows, slope_rows):
-    def body(x_ref, main_ref, halo_ref, w_ref, o_ref, zv_ref, zs_ref):
+    def body(x_ref, main_ref, halo_ref, w_ref, ov_ref, os_ref, zv_ref, zs_ref):
         per_step, rows, length = x_ref.shape
         blen = length // block_count
         for b in range(block_count):
@@ -68,8 +68,8 @@
             pv = pv + jnp.dot(w_ref[1, :value_rows, :], zv, preferred_element_type=jnp.float32)
             ps = jnp.dot(w_ref[0, value_rows:, :], zs, preferred_element_type=jnp.float32)
             ps = ps + jnp.dot(w_ref[1, value_rows:, :], zs, preferred_element_type=jnp.float32)
-            o_ref[k, :value_rows, :] = pv
-            o_ref[k, value_rows:, :] = ps
+            ov_ref[k] = pv
+            os_ref[k] = ps
 
     return body
 
@@ -97,7 +97,10 @@
     const = lambda f: (0, 0)
     return pl.pallas_call(
         filter_kernel(block_count, coarse_block, value_rows, total_rows - value_rows),
-        out_shape=jax.ShapeDtypeStruct((field_count, total_rows, coarse), jnp.float32),
+        out_shape=[
+            jax.ShapeDtypeStruct((field_count, value_rows, coarse), jnp.float32),
+            jax.ShapeDtypeStruct((field_count, total_rows - value_rows, coarse), jnp.float32),
+        ],
         grid=(field_count // per_step,),
         in_specs=[
             pl.BlockSpec((per_step, rows, length), lambda f: (f, 0, 0)),
@@ -105,7 +108,10 @@
             pl.BlockSpec(halo_w.shape, const),
             pl.BlockSpec(w.shape, lambda f: (0, 0, 0)),
         ],
-        out_specs=pl.BlockSpec((per_step, total_rows, coarse), lambda f: (f, 0, 0)),
+        out_specs=[
+            pl.BlockSpec((per_step, value_rows, coarse), lambda f: (f, 0, 0)),
+            pl.BlockSpec((per_step, total_rows - value_rows, coarse), lambda f: (f, 0, 0)),
+        ],
         scratch_shapes=[pltpu.VMEM((per_step * rows, coarse), jnp.bfloat16)] * 2,
     )(fields3, main, halo_w, w)
 
@@ -123,17 +129,21 @@
 
 
 def pick_kernel(group_steps, step, chunk, owner_len, pack):
-    def body(idx_ref, x_ref, sel_ref, o_ref, tab_ref, buf_ref):
+    def body(idx_ref, xv_ref, xs_ref, sel_ref, o_ref, tab_ref, buf_ref):
         j = pl.program_id(0)
-        rows = x_ref.shape[0]
-        lanes = x_ref.shape[2]
+        fields = xv_ref.shape[0]
+        lanes = xv_ref.shape[2]
         width = tab_ref.shape[2]
+        per_field = 3 * pack
 
         @pl.when(j < group_steps)
         def _():
             for t in range(step):
-                parts = [x_ref[:, t * pack + k, :] for k in range(pack)]
-                parts.append(jnp.zeros((width - rows * pack, lanes), x_ref.dtype))
+                parts = []
+                for f in range(fields):
+                    parts.append(xv_ref[f, 2 * pack * t:2 * pack * (t + 1), :])
+                    parts.append(xs_ref[f, pack * t:pack * (t + 1), :])
+                parts.append(jnp.zeros((width - fields * per_field, lanes), xv_ref.dtype))
                 slab = jnp.concatenate(parts, axis=0)
                 at = pl.multiple_of((j * step + t) * (lanes // 8), lanes // 8)
                 tab_ref[pl.ds(at, lanes // 8), :, :] = slab.T.reshape(lanes // 8, 8, width)
@@ -157,17 +167,27 @@
             lax.fori_loop(0, chunk // 8, eight, 0)
             flipped = buf_ref[...].reshape(chunk, width).T
             sel = sel_ref[...]
-            picked = flipped[:rows]
-            for k in range(1, pack):
-                picked = jnp.where(sel == k, flipped[k * rows:(k + 1) * rows], picked)
+            picked = []
+            for f in range(fields):
+                for m in range(3):
+                    choices = []
+                    for k in range(pack):
+                        at = f * per_field + (2 * k + m if m < 2 else 2 * pack + k)
+                        choices.append(flipped[at:at + 1])
+                    row = choices[0]
+                    for k in range(1, pack):
+                        row = jnp.where(sel == k, choices[k], row)
+                    picked.append(row)
+            picked = jnp.concatenate(picked, axis=0)
             for owner in range(chunk // owner_len):
                 o_ref[owner] = picked[:, owner * owner_len:(owner + 1) * owner_len]
 
     return body
 
 
-def pick_cells(x, flat, sel, owner_len, pack, chunk=2048):
-    rows, groups, lanes = x.shape
+def pick_cells(xv, xs, flat, sel, owner_len, pack, chunk=2048):
+    fields, groups, lanes = xs.shape
+    rows = fields * 3
     step = 8
     group_steps = groups // (step * pack)
     entries = flat.shape[0]
@@ -178,17 +198,18 @@
         num_scalar_prefetch=1,
         grid=(group_steps + entries // chunk,),
         in_specs=[
-            pl.BlockSpec((rows, step * pack, lanes), lambda j, idx: (0, jnp.minimum(j, group_steps - 1), 0)),
+            pl.BlockSpec((fields, 2 * step * pack, lanes), lambda j, idx: (0, jnp.minimum(j, group_steps - 1), 0)),
+            pl.BlockSpec((fields, step * pack, lanes), lambda j, idx: (0, jnp.minimum(j, group_steps - 1), 0)),
             pl.BlockSpec((1, chunk), lambda j, idx: (0, jnp.maximum(j - group_steps, 0))),
         ],
         out_specs=pl.BlockSpec((per_chunk, rows, owner_len), lambda j, idx: (jnp.maximum(j - group_steps, 0), 0, 0)),
-        scratch_shapes=[pltpu.VMEM((groups // pack * lanes // 8 + 1, 8, width), x.dtype), pltpu.VMEM((chunk // 8, 8, width), x.dtype)],
+        scratch_shapes=[pltpu.VMEM((groups // pack * lanes // 8 + 1, 8, width), xs.dtype), pltpu.VMEM((chunk // 8, 8, width), xs.dtype)],
     )
     return pl.pallas_call(
         pick_kernel(group_steps, step, chunk, owner_len, pack),
-        out_shape=jax.ShapeDtypeStruct((entries // owner_len, rows, owner_len), x.dtype),
+        out_shape=jax.ShapeDtypeStruct((entries // owner_len, rows, owner_len), xs.dtype),
         grid_spec=grid_spec,
-    )(flat, x, sel)
+    )(flat, xv, xs, sel)
 
 
 def model_tensors(coarse):
@@ -242,7 +263,8 @@
         ys = jnp.stack([wy[0], wy[1], wy[0]])
         weights = xs[:, :, None, :, None] * ys[:, None, :, None, :]
         weights = weights.reshape(3, group, local_x * local_y)
-        weights = jnp.pad(weights, ((0, 0), (0, padded - group), (0, 0))).reshape(3 * padded, -1)
+        weights = jnp.pad(weights, ((0, 0), (0, padded - group), (0, 0)))
+        weights = jnp.concatenate([jnp.transpose(weights[:2], (1, 0, 2)).reshape(2 * padded, -1), weights[2]], axis=0)
         fields3 = fields.reshape(field_count, local_x * local_y, z_length)
         partials = filtered_partials(fields3, weights)
 
@@ -258,8 +280,8 @@
         flat = jnp.where(inside, (at_group // pack) * coarse_z + at_z, padded // pack * coarse_z)
         sel = jnp.where(inside, at_group % pack, 0).reshape(1, -1)
         owner_len = devices * slots
-        partials = partials.reshape(field_count * 3, padded, coarse_z)
-        taken = pick_cells(partials, flat.reshape(-1), sel, owner_len, pack)
+        value_part, slope_part = partials
+        taken = pick_cells(value_part, slope_part, flat.reshape(-1), sel, owner_len, pack)
         arrived = lax.all_to_all(taken, ("rows", "cols"), split_axis=0, concat_axis=0, tiled=True)
         summed = jnp.sum(arrived, axis=0)
         rounded = lax.reduce_precision(summed, exponent_bits=8, mantissa_bits=7)

time: 70.6 us -> 70.8 us (level)
  no operation moved by 1% of the time
where the time goes in v13:
time: 70.8 us; the launch traced here: 70.3 us
  Pallas kernels  29.2 us (41%)
  waiting for transfers between devices  17.2 us (24%)
  starting transfers between devices  12.9 us (18%)
  local copies, waits for them, and re-layouts  7.22 us (10%)
  other arithmetic  3.53 us (5%)
    all_to_all x1, waiting for transfers between devices, shards(): lax.all_to_all(taken, ('rows', 'cols'), split_axis=0, concat_axis=0, tile...  17.2 us
    pallas_call x1, Pallas kernels, filtered_partials(): pl.pallas_call(filter_kernel(block_count, coarse_block, value_rows, total...  15.8 us
    pallas_call x1, Pallas kernels, pick_cells(): pl.pallas_call(pick_kernel(group_steps, step, chunk, owner_len, pack), ou...  13.3 us
    all_to_all x1, starting transfers between devices, shards(): lax.all_to_all(copies, ('rows', 'cols'), split_axis=0, concat_axis=0, til...  7.1 us
    all_to_all x1, starting transfers between devices, shards(): lax.all_to_all(taken, ('rows', 'cols'), split_axis=0, concat_axis=0, tile...  5.84 us
    unnamed x5, local copies, waits for them, and re-layouts  1.49 us
  transfers between devices with their start and end apart: 2, of which 1 were waited for; matrix products, arithmetic and copies ran while one was open for 5% of the time, Pallas kernels for 23%

profile of v13, /device:TPU:1, one launch (start us, length us, event | category | flops | bytes accessed | tf_op | source)
XLA Modules:
  0.0 70.3 jit_solution(17726200016501581264)
XLA Ops:
  0.0 0.0 copy-start
  0.0 0.7 copy-done
  0.7 0.7 %reshape.228 = s32[32,1,128]{2,1,0:T(1,128)} reshape(s32[32,4,32]{2,1,0:T(4,128)S(1)} %broadcast_bitcast_fusion) | data formatting | bytes 32768
  1.4 7.1 %all-to-all-start = ((s32[32,1,128]{2,1,0:T(1,128)}), s32[32,1,128]{2,1,0:T(1,128)S(1)}, u32[]{:S(2)}, u32[]{:S(2)}) async-start(s32[32,1,128]{2,1,0:T(1,128)} %reshape.228), calls=%async_computation | async-start | bytes 32768 | tf_op jit(solution)/shard_map/all_to_all | solution.py:253
  8.5 0.8 %dynamic-slice_bitcast_fusion.3 = (f32[1,7,8]{2,0,1:T(1,128)S(1)}, f32[1,7,8]{2,0,1:T(1,128)S(1)}) fusion(f32[8,2,7,8]{3,0,2,1:T(8,128)} %constant.113.clone, s32[]{:T(128)S(6)} %select_n.64, s32[]{:T(128)S(6)} %add.64), kind=kLoop, calls=%fused_computation.57 | loop fusion | bytes 904 | tf_op jit(solution)/shard_map/slice | solution.py:262
  9.3 0.7 %dynamic-slice_bitcast_fusion = (f32[1,10,32]{2,1,0:T(8,128)S(1)}, f32[1,10,32]{2,1,0:T(8,128)S(1)}) fusion(f32[4,2,10,32]{3,2,1,0:T(8,128)} %constant.114.clone, s32[]{:T(128)S(6)} %select_n.65, s32[]{:T(128)S(6)} %add.64), kind=kLoop, calls=%fused_computation.54 | loop fusion | bytes 5128 | tf_op jit(solution)/shard_map/slice | solution.py:263
  10.1 0.1 broadcast_multiply_fusion
  10.2 0.3 mul.94
  10.5 0.1 copy.32
  10.6 0.1 concatenate.46
  10.8 0.7 %pad_maximum_fusion.1.w_ref = bf16[2,216,256]{2,1,0:T(8,128)(2,1)} fusion(bf16[1,216,256]{2,1,0:T(8,128)(2,1)S(1)} %subtract_convert_fusion, bf16[1,216,256]{2,1,0:T(8,128)(2,1)S(1)} %fusion), kind=kLoop, calls=%fused_computation.2 | loop fusion | flops 110592 | bytes 442368 | tf_op jit(solution)/shard_map/stack | solution.py:80
  11.5 15.8 %shard_map.64 = (f32[12,144,512]{2,1,0:T(8,128)}, f32[12,72,512]{2,1,0:T(8,128)}) custom-call(bf16[12,256,4096]{2,1,0:T(8,128)(2,1)} %bitcast.57, bf16[1024,256]{1,0:T(8,128)(2,1)} %constant.115.clone.main_ref, bf16[256,256]{1,0:T(8,128)(2,1)} %constant.116.clone.halo_ref, bf16[2,216,256]{2,1,0:T(8,128)(2,1)} %pad_maximum_fusion.1.w_ref), custom_call_target="tpu_custom_call" | custom-call | tf_op jit(solution)/shard_map/pallas_call | solution.py:98
  27.3 0.0 all-to-all-done
  27.3 0.5 broadcast.67
  27.8 0.7 reduce.2
  28.5 0.1 reshape.229
  28.6 0.5 fusion.9
  29.1 0.5 copy.33
  29.7 0.9 %reshape.226.sel_ref = s32[1,4096]{1,0:T(1,128)} reshape(s32[32,32,4]{2,1,0:T(8,128)S(1)} %copy.33) | data formatting | bytes 32768 | tf_op jit(solution)/shard_map/reshape | solution.py:281
  30.6 0.5 copy.30
  31.2 0.9 %reshape.224.idx_ref = s32[4096]{0:T(1024)} reshape(s32[32,32,4]{2,1,0:T(8,128)S(1)} %copy.30) | data formatting | bytes 32768 | tf_op jit(solution)/shard_map/reshape | solution.py:284
  32.0 13.3 %shard_map.65 = f32[32,36,128]{2,1,0:T(8,128)} custom-call(s32[4096]{0:T(1024)} %reshape.224.idx_ref, f32[12,144,512]{2,1,0:T(8,128)} %get-tuple-element.7.xv_ref, f32[12,72,512]{2,1,0:T(8,128)} %get-tuple-element.8.xs_ref, s32[1,4096]{1,0:T(1,128)} %reshape.226.sel_ref), custom_call_target="tpu_custom_call" | custom-call | tf_op jit(solution)/shard_map/pallas_call | solution.py:208
  45.4 5.8 %all-to-all-start.1 = ((f32[32,36,128]{2,1,0:T(8,128)}), f32[32,36,128]{2,1,0:T(8,128)S(1)}, u32[]{:S(2)}, u32[]{:S(2)}) async-start(f32[32,36,128]{2,1,0:T(8,128)} %shard_map.65), calls=%async_computation.1 | async-start | bytes 1310720 | tf_op jit(solution)/shard_map/all_to_all | solution.py:285
  51.2 0.7 fusion.14
  51.9 0.1 ge.23
  52.0 17.2 %all-to-all-done.1 = f32[32,36,128]{2,1,0:T(8,128)S(1)} async-done(((f32[32,36,128]{2,1,0:T(8,128)}), f32[32,36,128]{2,1,0:T(8,128)S(1)}, u32[]{:S(2)}, u32[]{:S(2)}) %all-to-all-start.1) | async-done | bytes 589856 | tf_op jit(solution)/shard_map/all_to_all | solution.py:285
  69.3 0.1 reduce_sum.72
  69.4 0.1 multiply_reduce_fusion
  69.5 0.2 concatenate.55
  69.7 0.6 multiply_convert_fusion
  (16 shorter events, 0.2 us)
Async XLA Ops:
  0.0 0.7 copy-start
  1.4 25.9 %all-to-all-start = ((s32[32,1,128]{2,1,0:T(1,128)}), s32[32,1,128]{2,1,0:T(1,128)S(1)}, u32[]{:S(2)}, u32[]{:S(2)}) async-start(s32[32,1,128]{2,1,0:T(1,128)} %reshape.228), calls=%async_computation | async-start | bytes 32768 | tf_op jit(solution)/shard_map/all_to_all | solution.py:253
  45.4 23.9 %all-to-all-start.1 = ((f32[32,36,128]{2,1,0:T(8,128)}), f32[32,36,128]{2,1,0:T(8,128)S(1)}, u32[]{:S(2)}, u32[]{:S(2)}) async-start(f32[32,36,128]{2,1,0:T(8,128)} %shard_map.65), calls=%async_computation.1 | async-start | bytes 1310720 | tf_op jit(solution)/shard_map/all_to_all | solution.py:285

commit v14 on v13

--- a/solution.py
+++ b/solution.py
@@ -249,8 +249,8 @@
         col = lax.axis_index("cols")
         me = row * col_count + col
 
-        copies = jnp.broadcast_to(front_cells, (devices,) + front_cells.shape[1:])
-        every_cell = lax.all_to_all(copies, ("rows", "cols"), split_axis=0, concat_axis=0, tiled=True)
+        copies = jnp.broadcast_to(front_cells[:, :, None, :], (devices,) + front_cells.shape[1:2] + (1,) + front_cells.shape[2:])
+        by_owner = lax.all_to_all(copies, ("rows", "cols"), split_axis=0, concat_axis=2, tiled=True)[0]
 
         x_base, x_count = window(row, local_x, coarse_x)
         y_base, y_count = window(col, local_y, coarse_y)
@@ -268,7 +268,6 @@
         fields3 = fields.reshape(field_count, local_x * local_y, z_length)
         partials = filtered_partials(fields3, weights)
 
-        by_owner = jnp.transpose(every_cell, (1, 0, 2))
         holder = lax.broadcasted_iota(jnp.int32, by_owner.shape, 1)
         clipped = jnp.clip(by_owner, 0, coarse_x * coarse_y * slab - 1)
         cell_pq = clipped // slab

time: 70.8 us -> 71.9 us (1.016)
  other arithmetic: 3.53 us -> 4.73 us
    reshape x2 -> x0, local copies, waits for them, and re-layouts: 1.8 us -> none  [the longest x1 0.94 us: shards(): sel = jnp.where(inside, at_group % pack, 0).reshape(1, -1)]
    ge x0 -> x3, local copies, waits for them, and re-layouts: none -> 1.2 us  [shards(): inside = (at_x < x_count) & (at_y < y_count) & (by_owner >= 0)]
    min x0 -> x3, local copies, waits for them, and re-layouts: none -> 1.13 us  [shards(): clipped = jnp.clip(by_owner, 0, coarse_x * coarse_y * slab - 1)]
    select_n x2 -> x0, local copies, waits for them, and re-layouts: 1.06 us -> none  [the longest x1 0.53 us: shards(): sel = jnp.where(inside, at_group % pack, 0).reshape(1, -1)]
  transfers between devices with their start and end apart: 2 -> 2, of which waited for: 1 -> 1; matrix products, arithmetic and copies ran while one was open for 5% -> 6% of each run, Pallas kernels for 23% -> 22%
where the time goes in v14:
time: 71.9 us; the launch traced here: 71.4 us
  Pallas kernels  29.2 us (41%)
  waiting for transfers between devices  17.2 us (24%)
  starting transfers between devices  12.9 us (18%)
  local copies, waits for them, and re-layouts  7.07 us (10%)
  other arithmetic  4.73 us (7%)
    all_to_all x1, waiting for transfers between devices, shards(): lax.all_to_all(taken, ('rows', 'cols'), split_axis=0, concat_axis=0, tile...  17.2 us
    pallas_call x1, Pallas kernels, filtered_partials(): pl.pallas_call(filter_kernel(block_count, coarse_block, value_rows, total...  15.8 us
    pallas_call x1, Pallas kernels, pick_cells(): pl.pallas_call(pick_kernel(group_steps, step, chunk, owner_len, pack), ou...  13.3 us
    all_to_all x1, starting transfers between devices, shards(): lax.all_to_all(copies, ('rows', 'cols'), split_axis=0, concat_axis=2, til...  7.1 us
    all_to_all x1, starting transfers between devices, shards(): lax.all_to_all(taken, ('rows', 'cols'), split_axis=0, concat_axis=0, tile...  5.84 us
    unnamed x5, local copies, waits for them, and re-layouts  1.49 us
  transfers between devices with their start and end apart: 2, of which 1 were waited for; matrix products, arithmetic and copies ran while one was open for 6% of the time, Pallas kernels for 22%

profile of v14, /device:TPU:1, one launch (start us, length us, event | category | flops | bytes accessed | tf_op | source)
XLA Modules:
  0.0 71.4 jit_solution(12771774064276808358)
XLA Ops:
  0.0 0.7 copy-done
  0.7 0.7 reshape.491
  1.4 7.1 %all-to-all-start = ((s32[32,1,128]{2,1,0:T(1,128)}), s32[32,1,128]{2,1,0:T(1,128)S(1)}, u32[]{:S(2)}, u32[]{:S(2)}) async-start(s32[32,1,128]{2,1,0:T(1,128)} %reshape.491), calls=%async_computation | async-start | bytes 32768 | tf_op jit(solution)/shard_map/all_to_all | solution.py:253
  8.5 0.8 %dynamic-slice_bitcast_fusion.3 = (f32[1,7,8]{2,0,1:T(1,128)S(1)}, f32[1,7,8]{2,0,1:T(1,128)S(1)}) fusion(f32[8,2,7,8]{3,0,2,1:T(8,128)} %constant.120.clone, s32[]{:T(128)S(6)} %select_n.131, s32[]{:T(128)S(6)} %add.135), kind=kLoop, calls=%fused_computation.73 | loop fusion | bytes 904 | tf_op jit(solution)/shard_map/slice | solution.py:262
  9.3 0.7 %dynamic-slice_bitcast_fusion = (f32[1,10,32]{2,1,0:T(8,128)S(1)}, f32[1,10,32]{2,1,0:T(8,128)S(1)}) fusion(f32[4,2,10,32]{3,2,1,0:T(8,128)} %constant.121.clone, s32[]{:T(128)S(6)} %select_n.132, s32[]{:T(128)S(6)} %add.135), kind=kLoop, calls=%fused_computation.70 | loop fusion | bytes 5128 | tf_op jit(solution)/shard_map/slice | solution.py:263
  10.1 0.1 broadcast_multiply_fusion
  10.2 0.3 mul.105
  10.5 0.1 copy.27
  10.6 0.1 concatenate.46
  10.8 0.7 pad_maximum_fusion.1.w_ref
  11.5 0.1 iota.9
  11.6 0.3 iota.10
  11.9 15.8 %shard_map.64 = (f32[12,144,512]{2,1,0:T(8,128)}, f32[12,72,512]{2,1,0:T(8,128)}) custom-call(bf16[12,256,4096]{2,1,0:T(8,128)(2,1)} %bitcast.50, bf16[1024,256]{1,0:T(8,128)(2,1)} %constant.122.clone.main_ref, bf16[256,256]{1,0:T(8,128)(2,1)} %constant.123.clone.halo_ref, bf16[2,216,256]{2,1,0:T(8,128)(2,1)} %pad_maximum_fusion.1.w_ref), custom_call_target="tpu_custom_call" | custom-call | tf_op jit(solution)/shard_map/pallas_call | solution.py:98
  27.7 0.5 broadcast.411
  28.2 0.7 reduce.2
  28.9 0.1 reshape.492
  29.1 0.5 copy.25
  29.6 0.3 ge.46
  30.0 0.3 ge.47
  30.3 0.5 copy.24
  30.8 0.3 min.21
  31.2 0.3 min.20
  31.5 1.0 %and_select_fusion.1.sel_ref = s32[1,4096]{1,0:T(1,128)} fusion(pred[1,4096]{1,0:T(4,128)(4,1)S(1)} %ge.47, s32[1,4096]{1,0:T(1,128)S(1)} %min.21, s32[]{:T(128)S(6)} %sub.75, s32[]{:T(128)S(6)} %sub.72), kind=kLoop, calls=%fused_computation.15 | loop fusion | flops 290816 | bytes 36872 | tf_op jit(solution)/shard_map/jit(_where)/select_n | solution.py:280
  32.5 0.7 fusion.9.idx_ref
  33.1 13.3 %shard_map.65 = f32[32,36,128]{2,1,0:T(8,128)} custom-call(s32[4096]{0:T(1024)} %fusion.9.idx_ref, f32[12,144,512]{2,1,0:T(8,128)} %get-tuple-element.7.xv_ref, f32[12,72,512]{2,1,0:T(8,128)} %get-tuple-element.8.xs_ref, s32[1,4096]{1,0:T(1,128)} %and_select_fusion.1.sel_ref), custom_call_target="tpu_custom_call" | custom-call | tf_op jit(solution)/shard_map/pallas_call | solution.py:208
  46.5 5.8 %all-to-all-start.1 = ((f32[32,36,128]{2,1,0:T(8,128)}), f32[32,36,128]{2,1,0:T(8,128)S(1)}, u32[]{:S(2)}, u32[]{:S(2)}) async-start(f32[32,36,128]{2,1,0:T(8,128)} %shard_map.65), calls=%async_computation.1 | async-start | bytes 1310720 | tf_op jit(solution)/shard_map/all_to_all | solution.py:284
  52.3 0.7 fusion.2
  53.0 0.1 ge.42
  53.1 17.2 %all-to-all-done.1 = f32[32,36,128]{2,1,0:T(8,128)S(1)} async-done(((f32[32,36,128]{2,1,0:T(8,128)}), f32[32,36,128]{2,1,0:T(8,128)S(1)}, u32[]{:S(2)}, u32[]{:S(2)}) %all-to-all-start.1) | async-done | bytes 589856 | tf_op jit(solution)/shard_map/all_to_all | solution.py:284
  70.4 0.1 reduce_sum.72
  70.6 0.2 concatenate.55
  70.8 0.6 multiply_convert_fusion
  (21 shorter events, 0.3 us)
Async XLA Ops:
  0.0 0.7 copy-start
  1.4 26.3 %all-to-all-start = ((s32[32,1,128]{2,1,0:T(1,128)}), s32[32,1,128]{2,1,0:T(1,128)S(1)}, u32[]{:S(2)}, u32[]{:S(2)}) async-start(s32[32,1,128]{2,1,0:T(1,128)} %reshape.491), calls=%async_computation | async-start | bytes 32768 | tf_op jit(solution)/shard_map/all_to_all | solution.py:253
  46.5 23.9 %all-to-all-start.1 = ((f32[32,36,128]{2,1,0:T(8,128)}), f32[32,36,128]{2,1,0:T(8,128)S(1)}, u32[]{:S(2)}, u32[]{:S(2)}) async-start(f32[32,36,128]{2,1,0:T(8,128)} %shard_map.65), calls=%async_computation.1 | async-start | bytes 1310720 | tf_op jit(solution)/shard_map/all_to_all | solution.py:284

commit v15 on v13

--- a/solution.py
+++ b/solution.py
@@ -164,7 +164,7 @@
                     buf_ref[i, pl.ds(k, 1), :] = row
                 return carry
 
-            lax.fori_loop(0, chunk // 8, eight, 0)
+            lax.fori_loop(0, chunk // 8, eight, 0, unroll=4)
             flipped = buf_ref[...].reshape(chunk, width).T
             sel = sel_ref[...]
             picked = []

time: 70.8 us -> 68.2 us (0.963)
  Pallas kernels: 29.2 us -> 26.6 us
    pallas_call x1, Pallas kernels: 13.3 us -> 10.8 us  [pick_cells(): pl.pallas_call(pick_kernel(group_steps, step, chunk, owner_len, pack), ou...]
where the time goes in v15:
time: 68.2 us; the launch traced here: 67.7 us
  Pallas kernels  26.6 us (39%)
  waiting for transfers between devices  17.2 us (25%)
  starting transfers between devices  12.9 us (19%)
  local copies, waits for them, and re-layouts  7.22 us (11%)
  other arithmetic  3.53 us (5%)
    all_to_all x1, waiting for transfers between devices, shards(): lax.all_to_all(taken, ('rows', 'cols'), split_axis=0, concat_axis=0, tile...  17.2 us
    pallas_call x1, Pallas kernels, filtered_partials(): pl.pallas_call(filter_kernel(block_count, coarse_block, value_rows, total...  15.8 us
    pallas_call x1, Pallas kernels, pick_cells(): pl.pallas_call(pick_kernel(group_steps, step, chunk, owner_len, pack), ou...  10.8 us
    all_to_all x1, starting transfers between devices, shards(): lax.all_to_all(copies, ('rows', 'cols'), split_axis=0, concat_axis=0, til...  7.1 us
    all_to_all x1, starting transfers between devices, shards(): lax.all_to_all(taken, ('rows', 'cols'), split_axis=0, concat_axis=0, tile...  5.84 us
    unnamed x5, local copies, waits for them, and re-layouts  1.49 us
  transfers between devices with their start and end apart: 2, of which 1 were waited for; matrix products, arithmetic and copies ran while one was open for 5% of the time, Pallas kernels for 23%

profile of v15, /device:TPU:1, one launch (start us, length us, event | category | flops | bytes accessed | tf_op | source)
XLA Modules:
  0.0 67.7 jit_solution(9609917855501119033)
XLA Ops:
  0.0 0.0 copy-start
  0.0 0.7 %copy-done = s32[1,32,4]{1,2,0:T(4,128)S(1)} copy-done((s32[1,32,4]{1,2,0:T(4,128)S(1)}, s32[1,32,4]{1,2,0:T(4,128)}, u32[]{:S(2)}) %copy-start) | copy-done | bytes 536
  0.7 0.7 %reshape.228 = s32[32,1,128]{2,1,0:T(1,128)} reshape(s32[32,4,32]{2,1,0:T(4,128)S(1)} %broadcast_bitcast_fusion) | data formatting | bytes 32768
  1.4 7.1 %all-to-all-start = ((s32[32,1,128]{2,1,0:T(1,128)}), s32[32,1,128]{2,1,0:T(1,128)S(1)}, u32[]{:S(2)}, u32[]{:S(2)}) async-start(s32[32,1,128]{2,1,0:T(1,128)} %reshape.228), calls=%async_computation | async-start | bytes 32768 | tf_op jit(solution)/shard_map/all_to_all | solution.py:253
  8.5 0.8 %dynamic-slice_bitcast_fusion.3 = (f32[1,7,8]{2,0,1:T(1,128)S(1)}, f32[1,7,8]{2,0,1:T(1,128)S(1)}) fusion(f32[8,2,7,8]{3,0,2,1:T(8,128)} %constant.113.clone, s32[]{:T(128)S(6)} %select_n.64, s32[]{:T(128)S(6)} %add.64), kind=kLoop, calls=%fused_computation.57 | loop fusion | bytes 904 | tf_op jit(solution)/shard_map/slice | solution.py:262
  9.3 0.7 %dynamic-slice_bitcast_fusion = (f32[1,10,32]{2,1,0:T(8,128)S(1)}, f32[1,10,32]{2,1,0:T(8,128)S(1)}) fusion(f32[4,2,10,32]{3,2,1,0:T(8,128)} %constant.114.clone, s32[]{:T(128)S(6)} %select_n.65, s32[]{:T(128)S(6)} %add.64), kind=kLoop, calls=%fused_computation.54 | loop fusion | bytes 5128 | tf_op jit(solution)/shard_map/slice | solution.py:263
  10.1 0.1 broadcast_multiply_fusion
  10.2 0.3 mul.94
  10.5 0.1 copy.32
  10.6 0.1 concatenate.46
  10.8 0.7 %pad_maximum_fusion.1.w_ref = bf16[2,216,256]{2,1,0:T(8,128)(2,1)} fusion(bf16[1,216,256]{2,1,0:T(8,128)(2,1)S(1)} %subtract_convert_fusion, bf16[1,216,256]{2,1,0:T(8,128)(2,1)S(1)} %fusion), kind=kLoop, calls=%fused_computation.2 | loop fusion | flops 110592 | bytes 442368 | tf_op jit(solution)/shard_map/stack | solution.py:80
  11.5 15.8 %shard_map.64 = (f32[12,144,512]{2,1,0:T(8,128)}, f32[12,72,512]{2,1,0:T(8,128)}) custom-call(bf16[12,256,4096]{2,1,0:T(8,128)(2,1)} %bitcast.57, bf16[1024,256]{1,0:T(8,128)(2,1)} %constant.115.clone.main_ref, bf16[256,256]{1,0:T(8,128)(2,1)} %constant.116.clone.halo_ref, bf16[2,216,256]{2,1,0:T(8,128)(2,1)} %pad_maximum_fusion.1.w_ref), custom_call_target="tpu_custom_call" | custom-call | tf_op jit(solution)/shard_map/pallas_call | solution.py:98
  27.3 0.0 all-to-all-done
  27.3 0.5 broadcast.67
  27.8 0.7 %reduce.2 = s32[32,128]{1,0:T(8,128)S(1)} reduce(s32[32,1,128]{2,1,0:T(1,128)S(1)} %all-to-all-done, s32[]{:T(128)} %broadcast.67), dimensions={1}, to_apply=%all_to_all.6.reduce_sub_computation | reduce | bytes 32772 | tf_op jit(solution)/shard_map/all_to_all | solution.py:253
  28.5 0.1 reshape.229
  28.6 0.5 fusion.9
  29.1 0.5 copy.33
  29.7 0.9 %reshape.226.sel_ref = s32[1,4096]{1,0:T(1,128)} reshape(s32[32,32,4]{2,1,0:T(8,128)S(1)} %copy.33) | data formatting | bytes 32768 | tf_op jit(solution)/shard_map/reshape | solution.py:281
  30.6 0.5 copy.30
  31.2 0.9 %reshape.224.idx_ref = s32[4096]{0:T(1024)} reshape(s32[32,32,4]{2,1,0:T(8,128)S(1)} %copy.30) | data formatting | bytes 32768 | tf_op jit(solution)/shard_map/reshape | solution.py:284
  32.0 10.8 %shard_map.65 = f32[32,36,128]{2,1,0:T(8,128)} custom-call(s32[4096]{0:T(1024)} %reshape.224.idx_ref, f32[12,144,512]{2,1,0:T(8,128)} %get-tuple-element.7.xv_ref, f32[12,72,512]{2,1,0:T(8,128)} %get-tuple-element.8.xs_ref, s32[1,4096]{1,0:T(1,128)} %reshape.226.sel_ref), custom_call_target="tpu_custom_call" | custom-call | tf_op jit(solution)/shard_map/pallas_call | solution.py:208
  42.8 5.8 %all-to-all-start.1 = ((f32[32,36,128]{2,1,0:T(8,128)}), f32[32,36,128]{2,1,0:T(8,128)S(1)}, u32[]{:S(2)}, u32[]{:S(2)}) async-start(f32[32,36,128]{2,1,0:T(8,128)} %shard_map.65), calls=%async_computation.1 | async-start | bytes 1310720 | tf_op jit(solution)/shard_map/all_to_all | solution.py:285
  48.6 0.7 %fusion.14 = pred[32,4]{1,0:T(8,128)(4,1)S(1)} fusion(s32[32,32,4]{1,2,0:T(4,128)S(1)} %bitcast.58, s32[]{:T(128)S(6)} %select_n.55), kind=kLoop, calls=%fused_computation.45 | loop fusion | flops 128 | bytes 644 | tf_op jit(solution)/shard_map/ge | solution.py:289
  49.3 0.1 ge.23
  49.5 17.2 %all-to-all-done.1 = f32[32,36,128]{2,1,0:T(8,128)S(1)} async-done(((f32[32,36,128]{2,1,0:T(8,128)}), f32[32,36,128]{2,1,0:T(8,128)S(1)}, u32[]{:S(2)}, u32[]{:S(2)}) %all-to-all-start.1) | async-done | bytes 589856 | tf_op jit(solution)/shard_map/all_to_all | solution.py:285
  66.7 0.1 reduce_sum.72
  66.8 0.1 multiply_reduce_fusion
  66.9 0.2 concatenate.55
  67.1 0.6 multiply_convert_fusion
  (16 shorter events, 0.2 us)
Async XLA Ops:
  0.0 0.7 %copy-start = (s32[1,32,4]{1,2,0:T(4,128)S(1)}, s32[1,32,4]{1,2,0:T(4,128)}, u32[]{:S(2)}) copy-start(s32[1,32,4]{1,2,0:T(4,128)} %param.7) | copy-start | bytes 1540
  1.4 25.9 %all-to-all-start = ((s32[32,1,128]{2,1,0:T(1,128)}), s32[32,1,128]{2,1,0:T(1,128)S(1)}, u32[]{:S(2)}, u32[]{:S(2)}) async-start(s32[32,1,128]{2,1,0:T(1,128)} %reshape.228), calls=%async_computation | async-start | bytes 32768 | tf_op jit(solution)/shard_map/all_to_all | solution.py:253
  42.8 23.9 %all-to-all-start.1 = ((f32[32,36,128]{2,1,0:T(8,128)}), f32[32,36,128]{2,1,0:T(8,128)S(1)}, u32[]{:S(2)}, u32[]{:S(2)}) async-start(f32[32,36,128]{2,1,0:T(8,128)} %shard_map.65), calls=%async_computation.1 | async-start | bytes 1310720 | tf_op jit(solution)/shard_map/all_to_all | solution.py:285

commit v16 on v15

--- a/solution.py
+++ b/solution.py
@@ -164,7 +164,7 @@
                     buf_ref[i, pl.ds(k, 1), :] = row
                 return carry
 
-            lax.fori_loop(0, chunk // 8, eight, 0, unroll=4)
+            lax.fori_loop(0, chunk // 8, eight, 0, unroll=16)
             flipped = buf_ref[...].reshape(chunk, width).T
             sel = sel_ref[...]
             picked = []

time: 68.2 us -> 67.8 us (level)
  transfers between devices with their start and end apart: 2 -> 2, of which waited for: 1 -> 1; matrix products, arithmetic and copies ran while one was open for 5% -> 6% of each run, Pallas kernels for 23% -> 24%
where the time goes in v16:
time: 67.8 us; the launch traced here: 67.3 us
  Pallas kernels  26.2 us (39%)
  waiting for transfers between devices  17.2 us (25%)
  starting transfers between devices  12.9 us (19%)
  local copies, waits for them, and re-layouts  7.22 us (11%)
  other arithmetic  3.53 us (5%)
    all_to_all x1, waiting for transfers between devices, shards(): lax.all_to_all(taken, ('rows', 'cols'), split_axis=0, concat_axis=0, tile...  17.2 us
    pallas_call x1, Pallas kernels, filtered_partials(): pl.pallas_call(filter_kernel(block_count, coarse_block, value_rows, total...  15.8 us
    pallas_call x1, Pallas kernels, pick_cells(): pl.pallas_call(pick_kernel(group_steps, step, chunk, owner_len, pack), ou...  10.4 us
    all_to_all x1, starting transfers between devices, shards(): lax.all_to_all(copies, ('rows', 'cols'), split_axis=0, concat_axis=0, til...  7.1 us
    all_to_all x1, starting transfers between devices, shards(): lax.all_to_all(taken, ('rows', 'cols'), split_axis=0, concat_axis=0, tile...  5.84 us
    unnamed x5, local copies, waits for them, and re-layouts  1.49 us
  transfers between devices with their start and end apart: 2, of which 1 were waited for; matrix products, arithmetic and copies ran while one was open for 6% of the time, Pallas kernels for 24%

profile of v16, /device:TPU:1, one launch (start us, length us, event | category | flops | bytes accessed | tf_op | source)
XLA Modules:
  0.0 67.3 jit_solution(2823979918263908983)
XLA Ops:
  0.0 0.0 copy-start
  0.0 0.7 %copy-done = s32[1,32,4]{1,2,0:T(4,128)S(1)} copy-done((s32[1,32,4]{1,2,0:T(4,128)S(1)}, s32[1,32,4]{1,2,0:T(4,128)}, u32[]{:S(2)}) %copy-start) | copy-done | bytes 536
  0.7 0.7 %reshape.228 = s32[32,1,128]{2,1,0:T(1,128)} reshape(s32[32,4,32]{2,1,0:T(4,128)S(1)} %broadcast_bitcast_fusion) | data formatting | bytes 32768
  1.4 7.1 %all-to-all-start = ((s32[32,1,128]{2,1,0:T(1,128)}), s32[32,1,128]{2,1,0:T(1,128)S(1)}, u32[]{:S(2)}, u32[]{:S(2)}) async-start(s32[32,1,128]{2,1,0:T(1,128)} %reshape.228), calls=%async_computation | async-start | bytes 32768 | tf_op jit(solution)/shard_map/all_to_all | solution.py:253
  8.5 0.8 %dynamic-slice_bitcast_fusion.3 = (f32[1,7,8]{2,0,1:T(1,128)S(1)}, f32[1,7,8]{2,0,1:T(1,128)S(1)}) fusion(f32[8,2,7,8]{3,0,2,1:T(8,128)} %constant.113.clone, s32[]{:T(128)S(6)} %select_n.64, s32[]{:T(128)S(6)} %add.64), kind=kLoop, calls=%fused_computation.57 | loop fusion | bytes 904 | tf_op jit(solution)/shard_map/slice | solution.py:262
  9.3 0.7 %dynamic-slice_bitcast_fusion = (f32[1,10,32]{2,1,0:T(8,128)S(1)}, f32[1,10,32]{2,1,0:T(8,128)S(1)}) fusion(f32[4,2,10,32]{3,2,1,0:T(8,128)} %constant.114.clone, s32[]{:T(128)S(6)} %select_n.65, s32[]{:T(128)S(6)} %add.64), kind=kLoop, calls=%fused_computation.54 | loop fusion | bytes 5128 | tf_op jit(solution)/shard_map/slice | solution.py:263
  10.1 0.1 broadcast_multiply_fusion
  10.2 0.3 mul.94
  10.5 0.1 copy.32
  10.6 0.1 concatenate.46
  10.8 0.7 %pad_maximum_fusion.1.w_ref = bf16[2,216,256]{2,1,0:T(8,128)(2,1)} fusion(bf16[1,216,256]{2,1,0:T(8,128)(2,1)S(1)} %subtract_convert_fusion, bf16[1,216,256]{2,1,0:T(8,128)(2,1)S(1)} %fusion), kind=kLoop, calls=%fused_computation.2 | loop fusion | flops 110592 | bytes 442368 | tf_op jit(solution)/shard_map/stack | solution.py:80
  11.5 15.8 %shard_map.64 = (f32[12,144,512]{2,1,0:T(8,128)}, f32[12,72,512]{2,1,0:T(8,128)}) custom-call(bf16[12,256,4096]{2,1,0:T(8,128)(2,1)} %bitcast.57, bf16[1024,256]{1,0:T(8,128)(2,1)} %constant.115.clone.main_ref, bf16[256,256]{1,0:T(8,128)(2,1)} %constant.116.clone.halo_ref, bf16[2,216,256]{2,1,0:T(8,128)(2,1)} %pad_maximum_fusion.1.w_ref), custom_call_target="tpu_custom_call" | custom-call | tf_op jit(solution)/shard_map/pallas_call | solution.py:98
  27.3 0.0 all-to-all-done
  27.3 0.5 broadcast.67
  27.8 0.7 %reduce.2 = s32[32,128]{1,0:T(8,128)S(1)} reduce(s32[32,1,128]{2,1,0:T(1,128)S(1)} %all-to-all-done, s32[]{:T(128)} %broadcast.67), dimensions={1}, to_apply=%all_to_all.6.reduce_sub_computation | reduce | bytes 32772 | tf_op jit(solution)/shard_map/all_to_all | solution.py:253
  28.5 0.1 reshape.229
  28.6 0.5 fusion.9
  29.1 0.5 copy.33
  29.7 0.9 %reshape.226.sel_ref = s32[1,4096]{1,0:T(1,128)} reshape(s32[32,32,4]{2,1,0:T(8,128)S(1)} %copy.33) | data formatting | bytes 32768 | tf_op jit(solution)/shard_map/reshape | solution.py:281
  30.6 0.5 copy.30
  31.2 0.9 %reshape.224.idx_ref = s32[4096]{0:T(1024)} reshape(s32[32,32,4]{2,1,0:T(8,128)S(1)} %copy.30) | data formatting | bytes 32768 | tf_op jit(solution)/shard_map/reshape | solution.py:284
  32.0 10.4 %shard_map.65 = f32[32,36,128]{2,1,0:T(8,128)} custom-call(s32[4096]{0:T(1024)} %reshape.224.idx_ref, f32[12,144,512]{2,1,0:T(8,128)} %get-tuple-element.7.xv_ref, f32[12,72,512]{2,1,0:T(8,128)} %get-tuple-element.8.xs_ref, s32[1,4096]{1,0:T(1,128)} %reshape.226.sel_ref), custom_call_target="tpu_custom_call" | custom-call | tf_op jit(solution)/shard_map/pallas_call | solution.py:208
  42.4 5.8 %all-to-all-start.1 = ((f32[32,36,128]{2,1,0:T(8,128)}), f32[32,36,128]{2,1,0:T(8,128)S(1)}, u32[]{:S(2)}, u32[]{:S(2)}) async-start(f32[32,36,128]{2,1,0:T(8,128)} %shard_map.65), calls=%async_computation.1 | async-start | bytes 1310720 | tf_op jit(solution)/shard_map/all_to_all | solution.py:285
  48.2 0.7 %fusion.14 = pred[32,4]{1,0:T(8,128)(4,1)S(1)} fusion(s32[32,32,4]{1,2,0:T(4,128)S(1)} %bitcast.58, s32[]{:T(128)S(6)} %select_n.55), kind=kLoop, calls=%fused_computation.45 | loop fusion | flops 128 | bytes 644 | tf_op jit(solution)/shard_map/ge | solution.py:289
  48.9 0.1 ge.23
  49.1 17.2 %all-to-all-done.1 = f32[32,36,128]{2,1,0:T(8,128)S(1)} async-done(((f32[32,36,128]{2,1,0:T(8,128)}), f32[32,36,128]{2,1,0:T(8,128)S(1)}, u32[]{:S(2)}, u32[]{:S(2)}) %all-to-all-start.1) | async-done | bytes 589856 | tf_op jit(solution)/shard_map/all_to_all | solution.py:285
  66.3 0.1 reduce_sum.72
  66.4 0.1 multiply_reduce_fusion
  66.5 0.2 concatenate.55
  66.7 0.6 multiply_convert_fusion
  (16 shorter events, 0.2 us)
Async XLA Ops:
  0.0 0.7 %copy-start = (s32[1,32,4]{1,2,0:T(4,128)S(1)}, s32[1,32,4]{1,2,0:T(4,128)}, u32[]{:S(2)}) copy-start(s32[1,32,4]{1,2,0:T(4,128)} %param.7) | copy-start | bytes 1540
  1.4 25.9 %all-to-all-start = ((s32[32,1,128]{2,1,0:T(1,128)}), s32[32,1,128]{2,1,0:T(1,128)S(1)}, u32[]{:S(2)}, u32[]{:S(2)}) async-start(s32[32,1,128]{2,1,0:T(1,128)} %reshape.228), calls=%async_computation | async-start | bytes 32768 | tf_op jit(solution)/shard_map/all_to_all | solution.py:253
  42.4 23.9 %all-to-all-start.1 = ((f32[32,36,128]{2,1,0:T(8,128)}), f32[32,36,128]{2,1,0:T(8,128)S(1)}, u32[]{:S(2)}, u32[]{:S(2)}) async-start(f32[32,36,128]{2,1,0:T(8,128)} %shard_map.65), calls=%async_computation.1 | async-start | bytes 1310720 | tf_op jit(solution)/shard_map/all_to_all | solution.py:285

commit v17 on v16

--- a/solution.py
+++ b/solution.py
@@ -185,7 +185,7 @@
     return body
 
 
-def pick_cells(xv, xs, flat, sel, owner_len, pack, chunk=2048):
+def pick_cells(xv, xs, flat, sel, owner_len, pack, chunk=4096):
     fields, groups, lanes = xs.shape
     rows = fields * 3
     step = 8

time: 67.8 us -> 67.8 us (level)
  no operation moved by 1% of the time
where the time goes in v17:
time: 67.8 us; the launch traced here: 67.3 us
  Pallas kernels  26.2 us (39%)
  waiting for transfers between devices  17.2 us (25%)
  starting transfers between devices  12.9 us (19%)
  local copies, waits for them, and re-layouts  7.22 us (11%)
  other arithmetic  3.53 us (5%)
    all_to_all x1, waiting for transfers between devices, shards(): lax.all_to_all(taken, ('rows', 'cols'), split_axis=0, concat_axis=0, tile...  17.2 us
    pallas_call x1, Pallas kernels, filtered_partials(): pl.pallas_call(filter_kernel(block_count, coarse_block, value_rows, total...  15.8 us
    pallas_call x1, Pallas kernels, pick_cells(): pl.pallas_call(pick_kernel(group_steps, step, chunk, owner_len, pack), ou...  10.3 us
    all_to_all x1, starting transfers between devices, shards(): lax.all_to_all(copies, ('rows', 'cols'), split_axis=0, concat_axis=0, til...  7.1 us
    all_to_all x1, starting transfers between devices, shards(): lax.all_to_all(taken, ('rows', 'cols'), split_axis=0, concat_axis=0, tile...  5.84 us
    unnamed x5, local copies, waits for them, and re-layouts  1.49 us
  transfers between devices with their start and end apart: 2, of which 1 were waited for; matrix products, arithmetic and copies ran while one was open for 6% of the time, Pallas kernels for 24%

profile of v17, /device:TPU:1, one launch (start us, length us, event | category | flops | bytes accessed | tf_op | source)
XLA Modules:
  0.0 67.3 jit_solution(4492329525377791900)
XLA Ops:
  0.0 0.0 copy-start
  0.0 0.7 %copy-done = s32[1,32,4]{1,2,0:T(4,128)S(1)} copy-done((s32[1,32,4]{1,2,0:T(4,128)S(1)}, s32[1,32,4]{1,2,0:T(4,128)}, u32[]{:S(2)}) %copy-start) | copy-done | bytes 536
  0.7 0.7 %reshape.228 = s32[32,1,128]{2,1,0:T(1,128)} reshape(s32[32,4,32]{2,1,0:T(4,128)S(1)} %broadcast_bitcast_fusion) | data formatting | bytes 32768
  1.4 7.1 %all-to-all-start = ((s32[32,1,128]{2,1,0:T(1,128)}), s32[32,1,128]{2,1,0:T(1,128)S(1)}, u32[]{:S(2)}, u32[]{:S(2)}) async-start(s32[32,1,128]{2,1,0:T(1,128)} %reshape.228), calls=%async_computation | async-start | bytes 32768 | tf_op jit(solution)/shard_map/all_to_all | solution.py:253
  8.5 0.8 %dynamic-slice_bitcast_fusion.3 = (f32[1,7,8]{2,0,1:T(1,128)S(1)}, f32[1,7,8]{2,0,1:T(1,128)S(1)}) fusion(f32[8,2,7,8]{3,0,2,1:T(8,128)} %constant.113.clone, s32[]{:T(128)S(6)} %select_n.64, s32[]{:T(128)S(6)} %add.64), kind=kLoop, calls=%fused_computation.57 | loop fusion | bytes 904 | tf_op jit(solution)/shard_map/slice | solution.py:262
  9.3 0.7 %dynamic-slice_bitcast_fusion = (f32[1,10,32]{2,1,0:T(8,128)S(1)}, f32[1,10,32]{2,1,0:T(8,128)S(1)}) fusion(f32[4,2,10,32]{3,2,1,0:T(8,128)} %constant.114.clone, s32[]{:T(128)S(6)} %select_n.65, s32[]{:T(128)S(6)} %add.64), kind=kLoop, calls=%fused_computation.54 | loop fusion | bytes 5128 | tf_op jit(solution)/shard_map/slice | solution.py:263
  10.1 0.1 broadcast_multiply_fusion
  10.2 0.3 mul.94
  10.5 0.1 copy.32
  10.6 0.1 concatenate.46
  10.8 0.7 %pad_maximum_fusion.1.w_ref = bf16[2,216,256]{2,1,0:T(8,128)(2,1)} fusion(bf16[1,216,256]{2,1,0:T(8,128)(2,1)S(1)} %subtract_convert_fusion, bf16[1,216,256]{2,1,0:T(8,128)(2,1)S(1)} %fusion), kind=kLoop, calls=%fused_computation.2 | loop fusion | flops 110592 | bytes 442368 | tf_op jit(solution)/shard_map/stack | solution.py:80
  11.5 15.8 %shard_map.64 = (f32[12,144,512]{2,1,0:T(8,128)}, f32[12,72,512]{2,1,0:T(8,128)}) custom-call(bf16[12,256,4096]{2,1,0:T(8,128)(2,1)} %bitcast.57, bf16[1024,256]{1,0:T(8,128)(2,1)} %constant.115.clone.main_ref, bf16[256,256]{1,0:T(8,128)(2,1)} %constant.116.clone.halo_ref, bf16[2,216,256]{2,1,0:T(8,128)(2,1)} %pad_maximum_fusion.1.w_ref), custom_call_target="tpu_custom_call" | custom-call | tf_op jit(solution)/shard_map/pallas_call | solution.py:98
  27.3 0.0 all-to-all-done
  27.3 0.5 broadcast.67
  27.8 0.7 %reduce.2 = s32[32,128]{1,0:T(8,128)S(1)} reduce(s32[32,1,128]{2,1,0:T(1,128)S(1)} %all-to-all-done, s32[]{:T(128)} %broadcast.67), dimensions={1}, to_apply=%all_to_all.6.reduce_sub_computation | reduce | bytes 32772 | tf_op jit(solution)/shard_map/all_to_all | solution.py:253
  28.5 0.1 reshape.229
  28.6 0.5 fusion.9
  29.1 0.5 copy.33
  29.7 0.9 %reshape.226.sel_ref = s32[1,4096]{1,0:T(1,128)} reshape(s32[32,32,4]{2,1,0:T(8,128)S(1)} %copy.33) | data formatting | bytes 32768 | tf_op jit(solution)/shard_map/reshape | solution.py:281
  30.6 0.5 copy.30
  31.2 0.9 %reshape.224.idx_ref = s32[4096]{0:T(1024)} reshape(s32[32,32,4]{2,1,0:T(8,128)S(1)} %copy.30) | data formatting | bytes 32768 | tf_op jit(solution)/shard_map/reshape | solution.py:284
  32.0 10.3 %shard_map.65 = f32[32,36,128]{2,1,0:T(8,128)} custom-call(s32[4096]{0:T(1024)} %reshape.224.idx_ref, f32[12,144,512]{2,1,0:T(8,128)} %get-tuple-element.7.xv_ref, f32[12,72,512]{2,1,0:T(8,128)} %get-tuple-element.8.xs_ref, s32[1,4096]{1,0:T(1,128)} %reshape.226.sel_ref), custom_call_target="tpu_custom_call" | custom-call | tf_op jit(solution)/shard_map/pallas_call | solution.py:208
  42.3 5.8 %all-to-all-start.1 = ((f32[32,36,128]{2,1,0:T(8,128)}), f32[32,36,128]{2,1,0:T(8,128)S(1)}, u32[]{:S(2)}, u32[]{:S(2)}) async-start(f32[32,36,128]{2,1,0:T(8,128)} %shard_map.65), calls=%async_computation.1 | async-start | bytes 1310720 | tf_op jit(solution)/shard_map/all_to_all | solution.py:285
  48.2 0.7 %fusion.14 = pred[32,4]{1,0:T(8,128)(4,1)S(1)} fusion(s32[32,32,4]{1,2,0:T(4,128)S(1)} %bitcast.58, s32[]{:T(128)S(6)} %select_n.55), kind=kLoop, calls=%fused_computation.45 | loop fusion | flops 128 | bytes 644 | tf_op jit(solution)/shard_map/ge | solution.py:289
  48.9 0.1 ge.23
  49.0 17.2 %all-to-all-done.1 = f32[32,36,128]{2,1,0:T(8,128)S(1)} async-done(((f32[32,36,128]{2,1,0:T(8,128)}), f32[32,36,128]{2,1,0:T(8,128)S(1)}, u32[]{:S(2)}, u32[]{:S(2)}) %all-to-all-start.1) | async-done | bytes 589856 | tf_op jit(solution)/shard_map/all_to_all | solution.py:285
  66.3 0.1 reduce_sum.72
  66.4 0.1 multiply_reduce_fusion
  66.5 0.2 concatenate.55
  66.7 0.6 multiply_convert_fusion
  (16 shorter events, 0.2 us)
Async XLA Ops:
  0.0 0.7 %copy-start = (s32[1,32,4]{1,2,0:T(4,128)S(1)}, s32[1,32,4]{1,2,0:T(4,128)}, u32[]{:S(2)}) copy-start(s32[1,32,4]{1,2,0:T(4,128)} %param.7) | copy-start | bytes 1540
  1.4 25.9 %all-to-all-start = ((s32[32,1,128]{2,1,0:T(1,128)}), s32[32,1,128]{2,1,0:T(1,128)S(1)}, u32[]{:S(2)}, u32[]{:S(2)}) async-start(s32[32,1,128]{2,1,0:T(1,128)} %reshape.228), calls=%async_computation | async-start | bytes 32768 | tf_op jit(solution)/shard_map/all_to_all | solution.py:253
  42.3 23.9 %all-to-all-start.1 = ((f32[32,36,128]{2,1,0:T(8,128)}), f32[32,36,128]{2,1,0:T(8,128)S(1)}, u32[]{:S(2)}, u32[]{:S(2)}) async-start(f32[32,36,128]{2,1,0:T(8,128)} %shard_map.65), calls=%async_computation.1 | async-start | bytes 1310720 | tf_op jit(solution)/shard_map/all_to_all | solution.py:285

commit v18 on v17

--- a/solution.py
+++ b/solution.py
@@ -164,7 +164,7 @@
                     buf_ref[i, pl.ds(k, 1), :] = row
                 return carry
 
-            lax.fori_loop(0, chunk // 8, eight, 0, unroll=16)
+            lax.fori_loop(0, chunk // 8, eight, 0, unroll=32)
             flipped = buf_ref[...].reshape(chunk, width).T
             sel = sel_ref[...]
             picked = []

time: 67.8 us -> 67.7 us (level)
  no operation moved by 1% of the time
where the time goes in v18:
time: 67.7 us; the launch traced here: 67.2 us
  Pallas kernels  26.1 us (39%)
  waiting for transfers between devices  17.2 us (25%)
  starting transfers between devices  12.9 us (19%)
  local copies, waits for them, and re-layouts  7.22 us (11%)
  other arithmetic  3.53 us (5%)
    all_to_all x1, waiting for transfers between devices, shards(): lax.all_to_all(taken, ('rows', 'cols'), split_axis=0, concat_axis=0, tile...  17.2 us
    pallas_call x1, Pallas kernels, filtered_partials(): pl.pallas_call(filter_kernel(block_count, coarse_block, value_rows, total...  15.8 us
    pallas_call x1, Pallas kernels, pick_cells(): pl.pallas_call(pick_kernel(group_steps, step, chunk, owner_len, pack), ou...  10.3 us
    all_to_all x1, starting transfers between devices, shards(): lax.all_to_all(copies, ('rows', 'cols'), split_axis=0, concat_axis=0, til...  7.1 us
    all_to_all x1, starting transfers between devices, shards(): lax.all_to_all(taken, ('rows', 'cols'), split_axis=0, concat_axis=0, tile...  5.84 us
    unnamed x5, local copies, waits for them, and re-layouts  1.49 us
  transfers between devices with their start and end apart: 2, of which 1 were waited for; matrix products, arithmetic and copies ran while one was open for 6% of the time, Pallas kernels for 24%

profile of v18, /device:TPU:1, one launch (start us, length us, event | category | flops | bytes accessed | tf_op | source)
XLA Modules:
  0.0 67.2 jit_solution(15908528916427229934)
XLA Ops:
  0.0 0.0 copy-start
  0.0 0.7 %copy-done = s32[1,32,4]{1,2,0:T(4,128)S(1)} copy-done((s32[1,32,4]{1,2,0:T(4,128)S(1)}, s32[1,32,4]{1,2,0:T(4,128)}, u32[]{:S(2)}) %copy-start) | copy-done | bytes 536
  0.7 0.7 %reshape.228 = s32[32,1,128]{2,1,0:T(1,128)} reshape(s32[32,4,32]{2,1,0:T(4,128)S(1)} %broadcast_bitcast_fusion) | data formatting | bytes 32768
  1.4 7.1 %all-to-all-start = ((s32[32,1,128]{2,1,0:T(1,128)}), s32[32,1,128]{2,1,0:T(1,128)S(1)}, u32[]{:S(2)}, u32[]{:S(2)}) async-start(s32[32,1,128]{2,1,0:T(1,128)} %reshape.228), calls=%async_computation | async-start | bytes 32768 | tf_op jit(solution)/shard_map/all_to_all | solution.py:253
  8.5 0.8 %dynamic-slice_bitcast_fusion.3 = (f32[1,7,8]{2,0,1:T(1,128)S(1)}, f32[1,7,8]{2,0,1:T(1,128)S(1)}) fusion(f32[8,2,7,8]{3,0,2,1:T(8,128)} %constant.113.clone, s32[]{:T(128)S(6)} %select_n.64, s32[]{:T(128)S(6)} %add.64), kind=kLoop, calls=%fused_computation.57 | loop fusion | bytes 904 | tf_op jit(solution)/shard_map/slice | solution.py:262
  9.3 0.7 %dynamic-slice_bitcast_fusion = (f32[1,10,32]{2,1,0:T(8,128)S(1)}, f32[1,10,32]{2,1,0:T(8,128)S(1)}) fusion(f32[4,2,10,32]{3,2,1,0:T(8,128)} %constant.114.clone, s32[]{:T(128)S(6)} %select_n.65, s32[]{:T(128)S(6)} %add.64), kind=kLoop, calls=%fused_computation.54 | loop fusion | bytes 5128 | tf_op jit(solution)/shard_map/slice | solution.py:263
  10.1 0.1 broadcast_multiply_fusion
  10.2 0.3 mul.94
  10.5 0.1 copy.32
  10.6 0.1 concatenate.46
  10.8 0.7 %pad_maximum_fusion.1.w_ref = bf16[2,216,256]{2,1,0:T(8,128)(2,1)} fusion(bf16[1,216,256]{2,1,0:T(8,128)(2,1)S(1)} %subtract_convert_fusion, bf16[1,216,256]{2,1,0:T(8,128)(2,1)S(1)} %fusion), kind=kLoop, calls=%fused_computation.2 | loop fusion | flops 110592 | bytes 442368 | tf_op jit(solution)/shard_map/stack | solution.py:80
  11.5 15.8 %shard_map.64 = (f32[12,144,512]{2,1,0:T(8,128)}, f32[12,72,512]{2,1,0:T(8,128)}) custom-call(bf16[12,256,4096]{2,1,0:T(8,128)(2,1)} %bitcast.57, bf16[1024,256]{1,0:T(8,128)(2,1)} %constant.115.clone.main_ref, bf16[256,256]{1,0:T(8,128)(2,1)} %constant.116.clone.halo_ref, bf16[2,216,256]{2,1,0:T(8,128)(2,1)} %pad_maximum_fusion.1.w_ref), custom_call_target="tpu_custom_call" | custom-call | tf_op jit(solution)/shard_map/pallas_call | solution.py:98
  27.3 0.0 all-to-all-done
  27.3 0.5 broadcast.67
  27.8 0.7 %reduce.2 = s32[32,128]{1,0:T(8,128)S(1)} reduce(s32[32,1,128]{2,1,0:T(1,128)S(1)} %all-to-all-done, s32[]{:T(128)} %broadcast.67), dimensions={1}, to_apply=%all_to_all.6.reduce_sub_computation | reduce | bytes 32772 | tf_op jit(solution)/shard_map/all_to_all | solution.py:253
  28.5 0.1 reshape.229
  28.6 0.5 fusion.9
  29.1 0.5 copy.33
  29.7 0.9 %reshape.226.sel_ref = s32[1,4096]{1,0:T(1,128)} reshape(s32[32,32,4]{2,1,0:T(8,128)S(1)} %copy.33) | data formatting | bytes 32768 | tf_op jit(solution)/shard_map/reshape | solution.py:281
  30.6 0.5 copy.30
  31.2 0.9 %reshape.224.idx_ref = s32[4096]{0:T(1024)} reshape(s32[32,32,4]{2,1,0:T(8,128)S(1)} %copy.30) | data formatting | bytes 32768 | tf_op jit(solution)/shard_map/reshape | solution.py:284
  32.0 10.3 %shard_map.65 = f32[32,36,128]{2,1,0:T(8,128)} custom-call(s32[4096]{0:T(1024)} %reshape.224.idx_ref, f32[12,144,512]{2,1,0:T(8,128)} %get-tuple-element.7.xv_ref, f32[12,72,512]{2,1,0:T(8,128)} %get-tuple-element.8.xs_ref, s32[1,4096]{1,0:T(1,128)} %reshape.226.sel_ref), custom_call_target="tpu_custom_call" | custom-call | tf_op jit(solution)/shard_map/pallas_call | solution.py:208
  42.3 5.8 %all-to-all-start.1 = ((f32[32,36,128]{2,1,0:T(8,128)}), f32[32,36,128]{2,1,0:T(8,128)S(1)}, u32[]{:S(2)}, u32[]{:S(2)}) async-start(f32[32,36,128]{2,1,0:T(8,128)} %shard_map.65), calls=%async_computation.1 | async-start | bytes 1310720 | tf_op jit(solution)/shard_map/all_to_all | solution.py:285
  48.1 0.7 %fusion.14 = pred[32,4]{1,0:T(8,128)(4,1)S(1)} fusion(s32[32,32,4]{1,2,0:T(4,128)S(1)} %bitcast.58, s32[]{:T(128)S(6)} %select_n.55), kind=kLoop, calls=%fused_computation.45 | loop fusion | flops 128 | bytes 644 | tf_op jit(solution)/shard_map/ge | solution.py:289
  48.8 0.1 ge.23
  49.0 17.2 %all-to-all-done.1 = f32[32,36,128]{2,1,0:T(8,128)S(1)} async-done(((f32[32,36,128]{2,1,0:T(8,128)}), f32[32,36,128]{2,1,0:T(8,128)S(1)}, u32[]{:S(2)}, u32[]{:S(2)}) %all-to-all-start.1) | async-done | bytes 589856 | tf_op jit(solution)/shard_map/all_to_all | solution.py:285
  66.2 0.1 reduce_sum.72
  66.3 0.1 multiply_reduce_fusion
  66.4 0.2 concatenate.55
  66.6 0.6 multiply_convert_fusion
  (16 shorter events, 0.2 us)
Async XLA Ops:
  0.0 0.7 %copy-start = (s32[1,32,4]{1,2,0:T(4,128)S(1)}, s32[1,32,4]{1,2,0:T(4,128)}, u32[]{:S(2)}) copy-start(s32[1,32,4]{1,2,0:T(4,128)} %param.7) | copy-start | bytes 1540
  1.4 25.9 %all-to-all-start = ((s32[32,1,128]{2,1,0:T(1,128)}), s32[32,1,128]{2,1,0:T(1,128)S(1)}, u32[]{:S(2)}, u32[]{:S(2)}) async-start(s32[32,1,128]{2,1,0:T(1,128)} %reshape.228), calls=%async_computation | async-start | bytes 32768 | tf_op jit(solution)/shard_map/all_to_all | solution.py:253
  42.3 23.9 %all-to-all-start.1 = ((f32[32,36,128]{2,1,0:T(8,128)}), f32[32,36,128]{2,1,0:T(8,128)S(1)}, u32[]{:S(2)}, u32[]{:S(2)}) async-start(f32[32,36,128]{2,1,0:T(8,128)} %shard_map.65), calls=%async_computation.1 | async-start | bytes 1310720 | tf_op jit(solution)/shard_map/all_to_all | solution.py:285

commit v19 on v17

--- a/solution.py
+++ b/solution.py
@@ -93,7 +93,7 @@
     total_rows = w.shape[1]
     value_rows = total_rows // 3 * 2
     coarse = length // 8
-    per_step = 4 if field_count % 4 == 0 else 1
+    per_step = 6 if field_count % 6 == 0 else 1
     const = lambda f: (0, 0)
     return pl.pallas_call(
         filter_kernel(block_count, coarse_block, value_rows, total_rows - value_rows),

time: 67.8 us -> 68.7 us (1.013)
  Pallas kernels: 26.2 us -> 27.1 us
    pallas_call x1, Pallas kernels: 15.8 us -> 16.8 us  [filtered_partials(): pl.pallas_call(filter_kernel(block_count, coarse_block, value_rows, total...]
  transfers between devices with their start and end apart: 2 -> 2, of which waited for: 1 -> 1; matrix products, arithmetic and copies ran while one was open for 6% -> 5% of each run, Pallas kernels for 24% -> 25%
where the time goes in v19:
time: 68.7 us; the launch traced here: 68.2 us
  Pallas kernels  27.1 us (39%)
  waiting for transfers between devices  17.2 us (25%)
  starting transfers between devices  12.9 us (19%)
  local copies, waits for them, and re-layouts  7.22 us (11%)
  other arithmetic  3.53 us (5%)
    all_to_all x1, waiting for transfers between devices, shards(): lax.all_to_all(taken, ('rows', 'cols'), split_axis=0, concat_axis=0, tile...  17.2 us
    pallas_call x1, Pallas kernels, filtered_partials(): pl.pallas_call(filter_kernel(block_count, coarse_block, value_rows, total...  16.8 us
    pallas_call x1, Pallas kernels, pick_cells(): pl.pallas_call(pick_kernel(group_steps, step, chunk, owner_len, pack), ou...  10.3 us
    all_to_all x1, starting transfers between devices, shards(): lax.all_to_all(copies, ('rows', 'cols'), split_axis=0, concat_axis=0, til...  7.1 us
    all_to_all x1, starting transfers between devices, shards(): lax.all_to_all(taken, ('rows', 'cols'), split_axis=0, concat_axis=0, tile...  5.82 us
    unnamed x5, local copies, waits for them, and re-layouts  1.49 us
  transfers between devices with their start and end apart: 2, of which 1 were waited for; matrix products, arithmetic and copies ran while one was open for 5% of the time, Pallas kernels for 25%

profile of v19, /device:TPU:1, one launch (start us, length us, event | category | flops | bytes accessed | tf_op | source)
XLA Modules:
  0.0 68.2 jit_solution(12578246457615290265)
XLA Ops:
  0.0 0.0 copy-start
  0.0 0.7 copy-done
  0.7 0.7 %reshape.228 = s32[32,1,128]{2,1,0:T(1,128)} reshape(s32[32,4,32]{2,1,0:T(4,128)S(1)} %broadcast_bitcast_fusion) | data formatting | bytes 32768
  1.4 7.1 %all-to-all-start = ((s32[32,1,128]{2,1,0:T(1,128)}), s32[32,1,128]{2,1,0:T(1,128)S(1)}, u32[]{:S(2)}, u32[]{:S(2)}) async-start(s32[32,1,128]{2,1,0:T(1,128)} %reshape.228), calls=%async_computation | async-start | bytes 32768 | tf_op jit(solution)/shard_map/all_to_all | solution.py:253
  8.5 0.8 %dynamic-slice_bitcast_fusion.3 = (f32[1,7,8]{2,0,1:T(1,128)S(1)}, f32[1,7,8]{2,0,1:T(1,128)S(1)}) fusion(f32[8,2,7,8]{3,0,2,1:T(8,128)} %constant.113.clone, s32[]{:T(128)S(6)} %select_n.64, s32[]{:T(128)S(6)} %add.64), kind=kLoop, calls=%fused_computation.57 | loop fusion | bytes 904 | tf_op jit(solution)/shard_map/slice | solution.py:262
  9.3 0.7 %dynamic-slice_bitcast_fusion = (f32[1,10,32]{2,1,0:T(8,128)S(1)}, f32[1,10,32]{2,1,0:T(8,128)S(1)}) fusion(f32[4,2,10,32]{3,2,1,0:T(8,128)} %constant.114.clone, s32[]{:T(128)S(6)} %select_n.65, s32[]{:T(128)S(6)} %add.64), kind=kLoop, calls=%fused_computation.54 | loop fusion | bytes 5128 | tf_op jit(solution)/shard_map/slice | solution.py:263
  10.1 0.1 broadcast_multiply_fusion
  10.2 0.3 mul.94
  10.5 0.1 copy.32
  10.6 0.1 concatenate.46
  10.8 0.7 %pad_maximum_fusion.1.w_ref = bf16[2,216,256]{2,1,0:T(8,128)(2,1)} fusion(bf16[1,216,256]{2,1,0:T(8,128)(2,1)S(1)} %subtract_convert_fusion, bf16[1,216,256]{2,1,0:T(8,128)(2,1)S(1)} %fusion), kind=kLoop, calls=%fused_computation.2 | loop fusion | flops 110592 | bytes 442368 | tf_op jit(solution)/shard_map/stack | solution.py:80
  11.5 16.8 %shard_map.64 = (f32[12,144,512]{2,1,0:T(8,128)}, f32[12,72,512]{2,1,0:T(8,128)}) custom-call(bf16[12,256,4096]{2,1,0:T(8,128)(2,1)} %bitcast.57, bf16[1024,256]{1,0:T(8,128)(2,1)} %constant.115.clone.main_ref, bf16[256,256]{1,0:T(8,128)(2,1)} %constant.116.clone.halo_ref, bf16[2,216,256]{2,1,0:T(8,128)(2,1)} %pad_maximum_fusion.1.w_ref), custom_call_target="tpu_custom_call" | custom-call | tf_op jit(solution)/shard_map/pallas_call | solution.py:98
  28.3 0.0 all-to-all-done
  28.3 0.5 broadcast.67
  28.8 0.7 %reduce.2 = s32[32,128]{1,0:T(8,128)S(1)} reduce(s32[32,1,128]{2,1,0:T(1,128)S(1)} %all-to-all-done, s32[]{:T(128)} %broadcast.67), dimensions={1}, to_apply=%all_to_all.6.reduce_sub_computation | reduce | bytes 32772 | tf_op jit(solution)/shard_map/all_to_all | solution.py:253
  29.5 0.1 reshape.229
  29.6 0.5 fusion.9
  30.1 0.5 copy.33
  30.7 0.9 %reshape.226.sel_ref = s32[1,4096]{1,0:T(1,128)} reshape(s32[32,32,4]{2,1,0:T(8,128)S(1)} %copy.33) | data formatting | bytes 32768 | tf_op jit(solution)/shard_map/reshape | solution.py:281
  31.6 0.5 copy.30
  32.1 0.9 %reshape.224.idx_ref = s32[4096]{0:T(1024)} reshape(s32[32,32,4]{2,1,0:T(8,128)S(1)} %copy.30) | data formatting | bytes 32768 | tf_op jit(solution)/shard_map/reshape | solution.py:284
  33.0 10.3 %shard_map.65 = f32[32,36,128]{2,1,0:T(8,128)} custom-call(s32[4096]{0:T(1024)} %reshape.224.idx_ref, f32[12,144,512]{2,1,0:T(8,128)} %get-tuple-element.7.xv_ref, f32[12,72,512]{2,1,0:T(8,128)} %get-tuple-element.8.xs_ref, s32[1,4096]{1,0:T(1,128)} %reshape.226.sel_ref), custom_call_target="tpu_custom_call" | custom-call | tf_op jit(solution)/shard_map/pallas_call | solution.py:208
  43.3 5.8 %all-to-all-start.1 = ((f32[32,36,128]{2,1,0:T(8,128)}), f32[32,36,128]{2,1,0:T(8,128)S(1)}, u32[]{:S(2)}, u32[]{:S(2)}) async-start(f32[32,36,128]{2,1,0:T(8,128)} %shard_map.65), calls=%async_computation.1 | async-start | bytes 1310720 | tf_op jit(solution)/shard_map/all_to_all | solution.py:285
  49.2 0.7 %fusion.14 = pred[32,4]{1,0:T(8,128)(4,1)S(1)} fusion(s32[32,32,4]{1,2,0:T(4,128)S(1)} %bitcast.58, s32[]{:T(128)S(6)} %select_n.55), kind=kLoop, calls=%fused_computation.45 | loop fusion | flops 128 | bytes 644 | tf_op jit(solution)/shard_map/ge | solution.py:289
  49.9 0.1 ge.23
  50.0 17.2 %all-to-all-done.1 = f32[32,36,128]{2,1,0:T(8,128)S(1)} async-done(((f32[32,36,128]{2,1,0:T(8,128)}), f32[32,36,128]{2,1,0:T(8,128)S(1)}, u32[]{:S(2)}, u32[]{:S(2)}) %all-to-all-start.1) | async-done | bytes 589856 | tf_op jit(solution)/shard_map/all_to_all | solution.py:285
  67.2 0.1 reduce_sum.72
  67.4 0.1 multiply_reduce_fusion
  67.4 0.2 concatenate.55
  67.6 0.6 multiply_convert_fusion
  (16 shorter events, 0.2 us)
Async XLA Ops:
  0.0 0.7 copy-start
  1.4 26.9 %all-to-all-start = ((s32[32,1,128]{2,1,0:T(1,128)}), s32[32,1,128]{2,1,0:T(1,128)S(1)}, u32[]{:S(2)}, u32[]{:S(2)}) async-start(s32[32,1,128]{2,1,0:T(1,128)} %reshape.228), calls=%async_computation | async-start | bytes 32768 | tf_op jit(solution)/shard_map/all_to_all | solution.py:253
  43.3 23.9 %all-to-all-start.1 = ((f32[32,36,128]{2,1,0:T(8,128)}), f32[32,36,128]{2,1,0:T(8,128)S(1)}, u32[]{:S(2)}, u32[]{:S(2)}) async-start(f32[32,36,128]{2,1,0:T(8,128)} %shard_map.65), calls=%async_computation.1 | async-start | bytes 1310720 | tf_op jit(solution)/shard_map/all_to_all | solution.py:285

commit v20 on v17

--- a/solution.py
+++ b/solution.py
@@ -140,9 +140,11 @@
         def _():
             for t in range(step):
                 parts = []
-                for f in range(fields):
-                    parts.append(xv_ref[f, 2 * pack * t:2 * pack * (t + 1), :])
-                    parts.append(xs_ref[f, pack * t:pack * (t + 1), :])
+                for k in range(pack):
+                    for f in range(fields):
+                        at = 2 * (pack * t + k)
+                        parts.append(xv_ref[f, at:at + 2, :])
+                        parts.append(xs_ref[f, pack * t + k:pack * t + k + 1, :])
                 parts.append(jnp.zeros((width - fields * per_field, lanes), xv_ref.dtype))
                 slab = jnp.concatenate(parts, axis=0)
                 at = pl.multiple_of((j * step + t) * (lanes // 8), lanes // 8)
@@ -167,18 +169,10 @@
             lax.fori_loop(0, chunk // 8, eight, 0, unroll=16)
             flipped = buf_ref[...].reshape(chunk, width).T
             sel = sel_ref[...]
-            picked = []
-            for f in range(fields):
-                for m in range(3):
-                    choices = []
-                    for k in range(pack):
-                        at = f * per_field + (2 * k + m if m < 2 else 2 * pack + k)
-                        choices.append(flipped[at:at + 1])
-                    row = choices[0]
-                    for k in range(1, pack):
-                        row = jnp.where(sel == k, choices[k], row)
-                    picked.append(row)
-            picked = jnp.concatenate(picked, axis=0)
+            rows = fields * 3
+            picked = flipped[:rows]
+            for k in range(1, pack):
+                picked = jnp.where(sel == k, flipped[k * rows:(k + 1) * rows], picked)
             for owner in range(chunk // owner_len):
                 o_ref[owner] = picked[:, owner * owner_len:(owner + 1) * owner_len]
 

time: 67.8 us -> 67.7 us (level)
  no operation moved by 1% of the time
where the time goes in v20:
time: 67.7 us; the launch traced here: 67.2 us
  Pallas kernels  26 us (38%)
  waiting for transfers between devices  17.2 us (25%)
  starting transfers between devices  12.9 us (19%)
  local copies, waits for them, and re-layouts  7.22 us (11%)
  other arithmetic  3.53 us (5%)
    all_to_all x1, waiting for transfers between devices, shards(): lax.all_to_all(taken, ('rows', 'cols'), split_axis=0, concat_axis=0, tile...  17.2 us
    pallas_call x1, Pallas kernels, filtered_partials(): pl.pallas_call(filter_kernel(block_count, coarse_block, value_rows, total...  15.8 us
    pallas_call x1, Pallas kernels, pick_cells(): pl.pallas_call(pick_kernel(group_steps, step, chunk, owner_len, pack), ou...  10.2 us
    all_to_all x1, starting transfers between devices, shards(): lax.all_to_all(copies, ('rows', 'cols'), split_axis=0, concat_axis=0, til...  7.1 us
    all_to_all x1, starting transfers between devices, shards(): lax.all_to_all(taken, ('rows', 'cols'), split_axis=0, concat_axis=0, tile...  5.84 us
    unnamed x5, local copies, waits for them, and re-layouts  1.49 us
  transfers between devices with their start and end apart: 2, of which 1 were waited for; matrix products, arithmetic and copies ran while one was open for 6% of the time, Pallas kernels for 24%

profile of v20, /device:TPU:1, one launch (start us, length us, event | category | flops | bytes accessed | tf_op | source)
XLA Modules:
  0.0 67.2 jit_solution(6833867153173324365)
XLA Ops:
  0.0 0.0 copy-start
  0.0 0.7 %copy-done = s32[1,32,4]{1,2,0:T(4,128)S(1)} copy-done((s32[1,32,4]{1,2,0:T(4,128)S(1)}, s32[1,32,4]{1,2,0:T(4,128)}, u32[]{:S(2)}) %copy-start) | copy-done | bytes 536
  0.7 0.7 %reshape.228 = s32[32,1,128]{2,1,0:T(1,128)} reshape(s32[32,4,32]{2,1,0:T(4,128)S(1)} %broadcast_bitcast_fusion) | data formatting | bytes 32768
  1.4 7.1 %all-to-all-start = ((s32[32,1,128]{2,1,0:T(1,128)}), s32[32,1,128]{2,1,0:T(1,128)S(1)}, u32[]{:S(2)}, u32[]{:S(2)}) async-start(s32[32,1,128]{2,1,0:T(1,128)} %reshape.228), calls=%async_computation | async-start | bytes 32768 | tf_op jit(solution)/shard_map/all_to_all | solution.py:247
  8.5 0.8 %dynamic-slice_bitcast_fusion.3 = (f32[1,7,8]{2,0,1:T(1,128)S(1)}, f32[1,7,8]{2,0,1:T(1,128)S(1)}) fusion(f32[8,2,7,8]{3,0,2,1:T(8,128)} %constant.113.clone, s32[]{:T(128)S(6)} %select_n.64, s32[]{:T(128)S(6)} %add.64), kind=kLoop, calls=%fused_computation.57 | loop fusion | bytes 904 | tf_op jit(solution)/shard_map/slice | solution.py:256
  9.3 0.7 %dynamic-slice_bitcast_fusion = (f32[1,10,32]{2,1,0:T(8,128)S(1)}, f32[1,10,32]{2,1,0:T(8,128)S(1)}) fusion(f32[4,2,10,32]{3,2,1,0:T(8,128)} %constant.114.clone, s32[]{:T(128)S(6)} %select_n.65, s32[]{:T(128)S(6)} %add.64), kind=kLoop, calls=%fused_computation.54 | loop fusion | bytes 5128 | tf_op jit(solution)/shard_map/slice | solution.py:257
  10.1 0.1 broadcast_multiply_fusion
  10.2 0.3 mul.94
  10.5 0.1 copy.32
  10.6 0.1 concatenate.46
  10.8 0.7 %pad_maximum_fusion.1.w_ref = bf16[2,216,256]{2,1,0:T(8,128)(2,1)} fusion(bf16[1,216,256]{2,1,0:T(8,128)(2,1)S(1)} %subtract_convert_fusion, bf16[1,216,256]{2,1,0:T(8,128)(2,1)S(1)} %fusion), kind=kLoop, calls=%fused_computation.2 | loop fusion | flops 110592 | bytes 442368 | tf_op jit(solution)/shard_map/stack | solution.py:80
  11.5 15.8 %shard_map.64 = (f32[12,144,512]{2,1,0:T(8,128)}, f32[12,72,512]{2,1,0:T(8,128)}) custom-call(bf16[12,256,4096]{2,1,0:T(8,128)(2,1)} %bitcast.57, bf16[1024,256]{1,0:T(8,128)(2,1)} %constant.115.clone.main_ref, bf16[256,256]{1,0:T(8,128)(2,1)} %constant.116.clone.halo_ref, bf16[2,216,256]{2,1,0:T(8,128)(2,1)} %pad_maximum_fusion.1.w_ref), custom_call_target="tpu_custom_call" | custom-call | tf_op jit(solution)/shard_map/pallas_call | solution.py:98
  27.3 0.0 all-to-all-done
  27.3 0.5 broadcast.67
  27.8 0.7 %reduce.2 = s32[32,128]{1,0:T(8,128)S(1)} reduce(s32[32,1,128]{2,1,0:T(1,128)S(1)} %all-to-all-done, s32[]{:T(128)} %broadcast.67), dimensions={1}, to_apply=%all_to_all.6.reduce_sub_computation | reduce | bytes 32772 | tf_op jit(solution)/shard_map/all_to_all | solution.py:247
  28.5 0.1 reshape.229
  28.6 0.5 fusion.9
  29.1 0.5 copy.33
  29.7 0.9 %reshape.226.sel_ref = s32[1,4096]{1,0:T(1,128)} reshape(s32[32,32,4]{2,1,0:T(8,128)S(1)} %copy.33) | data formatting | bytes 32768 | tf_op jit(solution)/shard_map/reshape | solution.py:275
  30.6 0.5 copy.30
  31.2 0.9 %reshape.224.idx_ref = s32[4096]{0:T(1024)} reshape(s32[32,32,4]{2,1,0:T(8,128)S(1)} %copy.30) | data formatting | bytes 32768 | tf_op jit(solution)/shard_map/reshape | solution.py:278
  32.0 10.2 %shard_map.65 = f32[32,36,128]{2,1,0:T(8,128)} custom-call(s32[4096]{0:T(1024)} %reshape.224.idx_ref, f32[12,144,512]{2,1,0:T(8,128)} %get-tuple-element.7.xv_ref, f32[12,72,512]{2,1,0:T(8,128)} %get-tuple-element.8.xs_ref, s32[1,4096]{1,0:T(1,128)} %reshape.226.sel_ref), custom_call_target="tpu_custom_call" | custom-call | tf_op jit(solution)/shard_map/pallas_call | solution.py:202
  42.2 5.8 %all-to-all-start.1 = ((f32[32,36,128]{2,1,0:T(8,128)}), f32[32,36,128]{2,1,0:T(8,128)S(1)}, u32[]{:S(2)}, u32[]{:S(2)}) async-start(f32[32,36,128]{2,1,0:T(8,128)} %shard_map.65), calls=%async_computation.1 | async-start | bytes 1310720 | tf_op jit(solution)/shard_map/all_to_all | solution.py:279
  48.1 0.7 %fusion.14 = pred[32,4]{1,0:T(8,128)(4,1)S(1)} fusion(s32[32,32,4]{1,2,0:T(4,128)S(1)} %bitcast.58, s32[]{:T(128)S(6)} %select_n.55), kind=kLoop, calls=%fused_computation.45 | loop fusion | flops 128 | bytes 644 | tf_op jit(solution)/shard_map/ge | solution.py:283
  48.8 0.1 ge.23
  48.9 17.2 %all-to-all-done.1 = f32[32,36,128]{2,1,0:T(8,128)S(1)} async-done(((f32[32,36,128]{2,1,0:T(8,128)}), f32[32,36,128]{2,1,0:T(8,128)S(1)}, u32[]{:S(2)}, u32[]{:S(2)}) %all-to-all-start.1) | async-done | bytes 589856 | tf_op jit(solution)/shard_map/all_to_all | solution.py:279
  66.2 0.1 reduce_sum.72
  66.3 0.1 multiply_reduce_fusion
  66.4 0.2 concatenate.55
  66.6 0.6 multiply_convert_fusion
  (16 shorter events, 0.2 us)
Async XLA Ops:
  0.0 0.7 %copy-start = (s32[1,32,4]{1,2,0:T(4,128)S(1)}, s32[1,32,4]{1,2,0:T(4,128)}, u32[]{:S(2)}) copy-start(s32[1,32,4]{1,2,0:T(4,128)} %param.7) | copy-start | bytes 1540
  1.4 25.9 %all-to-all-start = ((s32[32,1,128]{2,1,0:T(1,128)}), s32[32,1,128]{2,1,0:T(1,128)S(1)}, u32[]{:S(2)}, u32[]{:S(2)}) async-start(s32[32,1,128]{2,1,0:T(1,128)} %reshape.228), calls=%async_computation | async-start | bytes 32768 | tf_op jit(solution)/shard_map/all_to_all | solution.py:247
  42.2 23.9 %all-to-all-start.1 = ((f32[32,36,128]{2,1,0:T(8,128)}), f32[32,36,128]{2,1,0:T(8,128)S(1)}, u32[]{:S(2)}, u32[]{:S(2)}) async-start(f32[32,36,128]{2,1,0:T(8,128)} %shard_map.65), calls=%async_computation.1 | async-start | bytes 1310720 | tf_op jit(solution)/shard_map/all_to_all | solution.py:279

commit v21 on v20

--- a/solution.py
+++ b/solution.py
@@ -93,7 +93,7 @@
     total_rows = w.shape[1]
     value_rows = total_rows // 3 * 2
     coarse = length // 8
-    per_step = 4 if field_count % 4 == 0 else 1
+    per_step = 3 if field_count % 3 == 0 else 1
     const = lambda f: (0, 0)
     return pl.pallas_call(
         filter_kernel(block_count, coarse_block, value_rows, total_rows - value_rows),

time: 67.7 us -> 67.4 us (level)
  transfers between devices with their start and end apart: 2 -> 2, of which waited for: 1 -> 1; matrix products, arithmetic and copies ran while one was open for 6% -> 6% of each run, Pallas kernels for 24% -> 23%
where the time goes in v21:
time: 67.4 us; the launch traced here: 66.9 us
  Pallas kernels  25.7 us (38%)
  waiting for transfers between devices  17.2 us (26%)
  starting transfers between devices  12.9 us (19%)
  local copies, waits for them, and re-layouts  7.22 us (11%)
  other arithmetic  3.53 us (5%)
    all_to_all x1, waiting for transfers between devices, shards(): lax.all_to_all(taken, ('rows', 'cols'), split_axis=0, concat_axis=0, tile...  17.2 us
    pallas_call x1, Pallas kernels, filtered_partials(): pl.pallas_call(filter_kernel(block_count, coarse_block, value_rows, total...  15.5 us
    pallas_call x1, Pallas kernels, pick_cells(): pl.pallas_call(pick_kernel(group_steps, step, chunk, owner_len, pack), ou...  10.2 us
    all_to_all x1, starting transfers between devices, shards(): lax.all_to_all(copies, ('rows', 'cols'), split_axis=0, concat_axis=0, til...  7.1 us
    all_to_all x1, starting transfers between devices, shards(): lax.all_to_all(taken, ('rows', 'cols'), split_axis=0, concat_axis=0, tile...  5.83 us
    unnamed x5, local copies, waits for them, and re-layouts  1.49 us
  transfers between devices with their start and end apart: 2, of which 1 were waited for; matrix products, arithmetic and copies ran while one was open for 6% of the time, Pallas kernels for 23%

profile of v21, /device:TPU:1, one launch (start us, length us, event | category | flops | bytes accessed | tf_op | source)
XLA Modules:
  0.0 66.9 jit_solution(13698329057106609632)
XLA Ops:
  0.0 0.0 copy-start
  0.0 0.7 %copy-done = s32[1,32,4]{1,2,0:T(4,128)S(1)} copy-done((s32[1,32,4]{1,2,0:T(4,128)S(1)}, s32[1,32,4]{1,2,0:T(4,128)}, u32[]{:S(2)}) %copy-start) | copy-done | bytes 536
  0.7 0.7 %reshape.228 = s32[32,1,128]{2,1,0:T(1,128)} reshape(s32[32,4,32]{2,1,0:T(4,128)S(1)} %broadcast_bitcast_fusion) | data formatting | bytes 32768
  1.4 7.1 %all-to-all-start = ((s32[32,1,128]{2,1,0:T(1,128)}), s32[32,1,128]{2,1,0:T(1,128)S(1)}, u32[]{:S(2)}, u32[]{:S(2)}) async-start(s32[32,1,128]{2,1,0:T(1,128)} %reshape.228), calls=%async_computation | async-start | bytes 32768 | tf_op jit(solution)/shard_map/all_to_all | solution.py:247
  8.5 0.8 %dynamic-slice_bitcast_fusion.3 = (f32[1,7,8]{2,0,1:T(1,128)S(1)}, f32[1,7,8]{2,0,1:T(1,128)S(1)}) fusion(f32[8,2,7,8]{3,0,2,1:T(8,128)} %constant.113.clone, s32[]{:T(128)S(6)} %select_n.64, s32[]{:T(128)S(6)} %add.64), kind=kLoop, calls=%fused_computation.57 | loop fusion | bytes 904 | tf_op jit(solution)/shard_map/slice | solution.py:256
  9.3 0.7 %dynamic-slice_bitcast_fusion = (f32[1,10,32]{2,1,0:T(8,128)S(1)}, f32[1,10,32]{2,1,0:T(8,128)S(1)}) fusion(f32[4,2,10,32]{3,2,1,0:T(8,128)} %constant.114.clone, s32[]{:T(128)S(6)} %select_n.65, s32[]{:T(128)S(6)} %add.64), kind=kLoop, calls=%fused_computation.54 | loop fusion | bytes 5128 | tf_op jit(solution)/shard_map/slice | solution.py:257
  10.1 0.1 broadcast_multiply_fusion
  10.2 0.3 mul.94
  10.5 0.1 copy.32
  10.6 0.1 concatenate.46
  10.8 0.7 %pad_maximum_fusion.1.w_ref = bf16[2,216,256]{2,1,0:T(8,128)(2,1)} fusion(bf16[1,216,256]{2,1,0:T(8,128)(2,1)S(1)} %subtract_convert_fusion, bf16[1,216,256]{2,1,0:T(8,128)(2,1)S(1)} %fusion), kind=kLoop, calls=%fused_computation.2 | loop fusion | flops 110592 | bytes 442368 | tf_op jit(solution)/shard_map/stack | solution.py:80
  11.5 15.5 %shard_map.64 = (f32[12,144,512]{2,1,0:T(8,128)}, f32[12,72,512]{2,1,0:T(8,128)}) custom-call(bf16[12,256,4096]{2,1,0:T(8,128)(2,1)} %bitcast.57, bf16[1024,256]{1,0:T(8,128)(2,1)} %constant.115.clone.main_ref, bf16[256,256]{1,0:T(8,128)(2,1)} %constant.116.clone.halo_ref, bf16[2,216,256]{2,1,0:T(8,128)(2,1)} %pad_maximum_fusion.1.w_ref), custom_call_target="tpu_custom_call" | custom-call | tf_op jit(solution)/shard_map/pallas_call | solution.py:98
  27.0 0.0 all-to-all-done
  27.0 0.5 broadcast.67
  27.5 0.7 %reduce.2 = s32[32,128]{1,0:T(8,128)S(1)} reduce(s32[32,1,128]{2,1,0:T(1,128)S(1)} %all-to-all-done, s32[]{:T(128)} %broadcast.67), dimensions={1}, to_apply=%all_to_all.6.reduce_sub_computation | reduce | bytes 32772 | tf_op jit(solution)/shard_map/all_to_all | solution.py:247
  28.2 0.1 reshape.229
  28.3 0.5 fusion.9
  28.8 0.5 copy.33
  29.4 0.9 %reshape.226.sel_ref = s32[1,4096]{1,0:T(1,128)} reshape(s32[32,32,4]{2,1,0:T(8,128)S(1)} %copy.33) | data formatting | bytes 32768 | tf_op jit(solution)/shard_map/reshape | solution.py:275
  30.3 0.5 copy.30
  30.9 0.9 %reshape.224.idx_ref = s32[4096]{0:T(1024)} reshape(s32[32,32,4]{2,1,0:T(8,128)S(1)} %copy.30) | data formatting | bytes 32768 | tf_op jit(solution)/shard_map/reshape | solution.py:278
  31.7 10.2 %shard_map.65 = f32[32,36,128]{2,1,0:T(8,128)} custom-call(s32[4096]{0:T(1024)} %reshape.224.idx_ref, f32[12,144,512]{2,1,0:T(8,128)} %get-tuple-element.7.xv_ref, f32[12,72,512]{2,1,0:T(8,128)} %get-tuple-element.8.xs_ref, s32[1,4096]{1,0:T(1,128)} %reshape.226.sel_ref), custom_call_target="tpu_custom_call" | custom-call | tf_op jit(solution)/shard_map/pallas_call | solution.py:202
  41.9 5.8 %all-to-all-start.1 = ((f32[32,36,128]{2,1,0:T(8,128)}), f32[32,36,128]{2,1,0:T(8,128)S(1)}, u32[]{:S(2)}, u32[]{:S(2)}) async-start(f32[32,36,128]{2,1,0:T(8,128)} %shard_map.65), calls=%async_computation.1 | async-start | bytes 1310720 | tf_op jit(solution)/shard_map/all_to_all | solution.py:279
  47.8 0.7 %fusion.14 = pred[32,4]{1,0:T(8,128)(4,1)S(1)} fusion(s32[32,32,4]{1,2,0:T(4,128)S(1)} %bitcast.58, s32[]{:T(128)S(6)} %select_n.55), kind=kLoop, calls=%fused_computation.45 | loop fusion | flops 128 | bytes 644 | tf_op jit(solution)/shard_map/ge | solution.py:283
  48.5 0.1 ge.23
  48.6 17.2 %all-to-all-done.1 = f32[32,36,128]{2,1,0:T(8,128)S(1)} async-done(((f32[32,36,128]{2,1,0:T(8,128)}), f32[32,36,128]{2,1,0:T(8,128)S(1)}, u32[]{:S(2)}, u32[]{:S(2)}) %all-to-all-start.1) | async-done | bytes 589856 | tf_op jit(solution)/shard_map/all_to_all | solution.py:279
  65.8 0.1 reduce_sum.72
  66.0 0.1 multiply_reduce_fusion
  66.1 0.2 concatenate.55
  66.3 0.6 multiply_convert_fusion
  (16 shorter events, 0.2 us)
Async XLA Ops:
  0.0 0.7 %copy-start = (s32[1,32,4]{1,2,0:T(4,128)S(1)}, s32[1,32,4]{1,2,0:T(4,128)}, u32[]{:S(2)}) copy-start(s32[1,32,4]{1,2,0:T(4,128)} %param.7) | copy-start | bytes 1540
  1.4 25.6 %all-to-all-start = ((s32[32,1,128]{2,1,0:T(1,128)}), s32[32,1,128]{2,1,0:T(1,128)S(1)}, u32[]{:S(2)}, u32[]{:S(2)}) async-start(s32[32,1,128]{2,1,0:T(1,128)} %reshape.228), calls=%async_computation | async-start | bytes 32768 | tf_op jit(solution)/shard_map/all_to_all | solution.py:247
  41.9 23.9 %all-to-all-start.1 = ((f32[32,36,128]{2,1,0:T(8,128)}), f32[32,36,128]{2,1,0:T(8,128)S(1)}, u32[]{:S(2)}, u32[]{:S(2)}) async-start(f32[32,36,128]{2,1,0:T(8,128)} %shard_map.65), calls=%async_computation.1 | async-start | bytes 1310720 | tf_op jit(solution)/shard_map/all_to_all | solution.py:279

commit v22 on v21

--- a/solution.py
+++ b/solution.py
@@ -93,7 +93,7 @@
     total_rows = w.shape[1]
     value_rows = total_rows // 3 * 2
     coarse = length // 8
-    per_step = 3 if field_count % 3 == 0 else 1
+    per_step = 2 if field_count % 2 == 0 else 1
     const = lambda f: (0, 0)
     return pl.pallas_call(
         filter_kernel(block_count, coarse_block, value_rows, total_rows - value_rows),

time: 67.4 us -> 68 us (level)
  transfers between devices with their start and end apart: 2 -> 2, of which waited for: 1 -> 1; matrix products, arithmetic and copies ran while one was open for 6% -> 6% of each run, Pallas kernels for 23% -> 24%
where the time goes in v22:
time: 68 us; the launch traced here: 67.4 us
  Pallas kernels  26.3 us (39%)
  waiting for transfers between devices  17.2 us (25%)
  starting transfers between devices  12.9 us (19%)
  local copies, waits for them, and re-layouts  7.22 us (11%)
  other arithmetic  3.53 us (5%)
    all_to_all x1, waiting for transfers between devices, shards(): lax.all_to_all(taken, ('rows', 'cols'), split_axis=0, concat_axis=0, tile...  17.2 us
    pallas_call x1, Pallas kernels, filtered_partials(): pl.pallas_call(filter_kernel(block_count, coarse_block, value_rows, total...  16 us
    pallas_call x1, Pallas kernels, pick_cells(): pl.pallas_call(pick_kernel(group_steps, step, chunk, owner_len, pack), ou...  10.2 us
    all_to_all x1, starting transfers between devices, shards(): lax.all_to_all(copies, ('rows', 'cols'), split_axis=0, concat_axis=0, til...  7.1 us
    all_to_all x1, starting transfers between devices, shards(): lax.all_to_all(taken, ('rows', 'cols'), split_axis=0, concat_axis=0, tile...  5.83 us
    unnamed x5, local copies, waits for them, and re-layouts  1.49 us
  transfers between devices with their start and end apart: 2, of which 1 were waited for; matrix products, arithmetic and copies ran while one was open for 6% of the time, Pallas kernels for 24%

profile of v22, /device:TPU:1, one launch (start us, length us, event | category | flops | bytes accessed | tf_op | source)
XLA Modules:
  0.0 67.4 jit_solution(6530435280532543999)
XLA Ops:
  0.0 0.0 copy-start
  0.0 0.7 %copy-done = s32[1,32,4]{1,2,0:T(4,128)S(1)} copy-done((s32[1,32,4]{1,2,0:T(4,128)S(1)}, s32[1,32,4]{1,2,0:T(4,128)}, u32[]{:S(2)}) %copy-start) | copy-done | bytes 536
  0.7 0.7 %reshape.228 = s32[32,1,128]{2,1,0:T(1,128)} reshape(s32[32,4,32]{2,1,0:T(4,128)S(1)} %broadcast_bitcast_fusion) | data formatting | bytes 32768
  1.4 7.1 %all-to-all-start = ((s32[32,1,128]{2,1,0:T(1,128)}), s32[32,1,128]{2,1,0:T(1,128)S(1)}, u32[]{:S(2)}, u32[]{:S(2)}) async-start(s32[32,1,128]{2,1,0:T(1,128)} %reshape.228), calls=%async_computation | async-start | bytes 32768 | tf_op jit(solution)/shard_map/all_to_all | solution.py:247
  8.5 0.8 %dynamic-slice_bitcast_fusion.3 = (f32[1,7,8]{2,0,1:T(1,128)S(1)}, f32[1,7,8]{2,0,1:T(1,128)S(1)}) fusion(f32[8,2,7,8]{3,0,2,1:T(8,128)} %constant.113.clone, s32[]{:T(128)S(6)} %select_n.64, s32[]{:T(128)S(6)} %add.64), kind=kLoop, calls=%fused_computation.57 | loop fusion | bytes 904 | tf_op jit(solution)/shard_map/slice | solution.py:256
  9.3 0.7 %dynamic-slice_bitcast_fusion = (f32[1,10,32]{2,1,0:T(8,128)S(1)}, f32[1,10,32]{2,1,0:T(8,128)S(1)}) fusion(f32[4,2,10,32]{3,2,1,0:T(8,128)} %constant.114.clone, s32[]{:T(128)S(6)} %select_n.65, s32[]{:T(128)S(6)} %add.64), kind=kLoop, calls=%fused_computation.54 | loop fusion | bytes 5128 | tf_op jit(solution)/shard_map/slice | solution.py:257
  10.1 0.1 broadcast_multiply_fusion
  10.2 0.3 mul.94
  10.5 0.1 copy.32
  10.6 0.1 concatenate.46
  10.8 0.7 %pad_maximum_fusion.1.w_ref = bf16[2,216,256]{2,1,0:T(8,128)(2,1)} fusion(bf16[1,216,256]{2,1,0:T(8,128)(2,1)S(1)} %subtract_convert_fusion, bf16[1,216,256]{2,1,0:T(8,128)(2,1)S(1)} %fusion), kind=kLoop, calls=%fused_computation.2 | loop fusion | flops 110592 | bytes 442368 | tf_op jit(solution)/shard_map/stack | solution.py:80
  11.5 16.0 %shard_map.64 = (f32[12,144,512]{2,1,0:T(8,128)}, f32[12,72,512]{2,1,0:T(8,128)}) custom-call(bf16[12,256,4096]{2,1,0:T(8,128)(2,1)} %bitcast.57, bf16[1024,256]{1,0:T(8,128)(2,1)} %constant.115.clone.main_ref, bf16[256,256]{1,0:T(8,128)(2,1)} %constant.116.clone.halo_ref, bf16[2,216,256]{2,1,0:T(8,128)(2,1)} %pad_maximum_fusion.1.w_ref), custom_call_target="tpu_custom_call" | custom-call | tf_op jit(solution)/shard_map/pallas_call | solution.py:98
  27.5 0.0 all-to-all-done
  27.5 0.5 broadcast.67
  28.0 0.7 %reduce.2 = s32[32,128]{1,0:T(8,128)S(1)} reduce(s32[32,1,128]{2,1,0:T(1,128)S(1)} %all-to-all-done, s32[]{:T(128)} %broadcast.67), dimensions={1}, to_apply=%all_to_all.6.reduce_sub_computation | reduce | bytes 32772 | tf_op jit(solution)/shard_map/all_to_all | solution.py:247
  28.7 0.1 reshape.229
  28.8 0.5 fusion.9
  29.4 0.5 copy.33
  29.9 0.9 %reshape.226.sel_ref = s32[1,4096]{1,0:T(1,128)} reshape(s32[32,32,4]{2,1,0:T(8,128)S(1)} %copy.33) | data formatting | bytes 32768 | tf_op jit(solution)/shard_map/reshape | solution.py:275
  30.8 0.5 copy.30
  31.4 0.9 %reshape.224.idx_ref = s32[4096]{0:T(1024)} reshape(s32[32,32,4]{2,1,0:T(8,128)S(1)} %copy.30) | data formatting | bytes 32768 | tf_op jit(solution)/shard_map/reshape | solution.py:278
  32.2 10.2 %shard_map.65 = f32[32,36,128]{2,1,0:T(8,128)} custom-call(s32[4096]{0:T(1024)} %reshape.224.idx_ref, f32[12,144,512]{2,1,0:T(8,128)} %get-tuple-element.7.xv_ref, f32[12,72,512]{2,1,0:T(8,128)} %get-tuple-element.8.xs_ref, s32[1,4096]{1,0:T(1,128)} %reshape.226.sel_ref), custom_call_target="tpu_custom_call" | custom-call | tf_op jit(solution)/shard_map/pallas_call | solution.py:202
  42.5 5.8 %all-to-all-start.1 = ((f32[32,36,128]{2,1,0:T(8,128)}), f32[32,36,128]{2,1,0:T(8,128)S(1)}, u32[]{:S(2)}, u32[]{:S(2)}) async-start(f32[32,36,128]{2,1,0:T(8,128)} %shard_map.65), calls=%async_computation.1 | async-start | bytes 1310720 | tf_op jit(solution)/shard_map/all_to_all | solution.py:279
  48.3 0.7 %fusion.14 = pred[32,4]{1,0:T(8,128)(4,1)S(1)} fusion(s32[32,32,4]{1,2,0:T(4,128)S(1)} %bitcast.58, s32[]{:T(128)S(6)} %select_n.55), kind=kLoop, calls=%fused_computation.45 | loop fusion | flops 128 | bytes 644 | tf_op jit(solution)/shard_map/ge | solution.py:283
  49.0 0.1 ge.23
  49.1 17.2 %all-to-all-done.1 = f32[32,36,128]{2,1,0:T(8,128)S(1)} async-done(((f32[32,36,128]{2,1,0:T(8,128)}), f32[32,36,128]{2,1,0:T(8,128)S(1)}, u32[]{:S(2)}, u32[]{:S(2)}) %all-to-all-start.1) | async-done | bytes 589856 | tf_op jit(solution)/shard_map/all_to_all | solution.py:279
  66.4 0.1 reduce_sum.72
  66.5 0.1 multiply_reduce_fusion
  66.6 0.2 concatenate.55
  66.8 0.6 multiply_convert_fusion
  (16 shorter events, 0.2 us)
Async XLA Ops:
  0.0 0.7 %copy-start = (s32[1,32,4]{1,2,0:T(4,128)S(1)}, s32[1,32,4]{1,2,0:T(4,128)}, u32[]{:S(2)}) copy-start(s32[1,32,4]{1,2,0:T(4,128)} %param.7) | copy-start | bytes 1540
  1.4 26.1 %all-to-all-start = ((s32[32,1,128]{2,1,0:T(1,128)}), s32[32,1,128]{2,1,0:T(1,128)S(1)}, u32[]{:S(2)}, u32[]{:S(2)}) async-start(s32[32,1,128]{2,1,0:T(1,128)} %reshape.228), calls=%async_computation | async-start | bytes 32768 | tf_op jit(solution)/shard_map/all_to_all | solution.py:247
  42.5 23.9 %all-to-all-start.1 = ((f32[32,36,128]{2,1,0:T(8,128)}), f32[32,36,128]{2,1,0:T(8,128)S(1)}, u32[]{:S(2)}, u32[]{:S(2)}) async-start(f32[32,36,128]{2,1,0:T(8,128)} %shard_map.65), calls=%async_computation.1 | async-start | bytes 1310720 | tf_op jit(solution)/shard_map/all_to_all | solution.py:279

commit v23 on v21

--- a/solution.py
+++ b/solution.py
@@ -55,9 +55,9 @@
             tail = x_ref[:, :, start:start + halo].reshape(per_step * rows, halo)
             start = ((b + 1) * blen) % length
             head = x_ref[:, :, start:start + halo].reshape(per_step * rows, halo)
-            edges = jnp.concatenate([tail, head], axis=1)
             acc = jnp.dot(main, main_ref[...], preferred_element_type=jnp.float32)
-            acc = acc + jnp.dot(edges, halo_ref[...], preferred_element_type=jnp.float32)
+            acc = acc + jnp.dot(tail, halo_ref[:halo, :], preferred_element_type=jnp.float32)
+            acc = acc + jnp.dot(head, halo_ref[halo:, :], preferred_element_type=jnp.float32)
             lanes = slice(b * coarse_block, (b + 1) * coarse_block)
             zv_ref[:, lanes] = acc[:, :coarse_block].astype(jnp.bfloat16)
             zs_ref[:, lanes] = acc[:, coarse_block:].astype(jnp.bfloat16)

time: 67.4 us -> 68.5 us (1.016)
  Pallas kernels: 25.7 us -> 26.8 us
    pallas_call x1, Pallas kernels: 15.5 us -> 16.6 us  [filtered_partials(): pl.pallas_call(filter_kernel(block_count, coarse_block, value_rows, total...]
  transfers between devices with their start and end apart: 2 -> 2, of which waited for: 1 -> 1; matrix products, arithmetic and copies ran while one was open for 6% -> 5% of each run, Pallas kernels for 23% -> 24%
where the time goes in v23:
time: 68.5 us; the launch traced here: 67.9 us
  Pallas kernels  26.8 us (39%)
  waiting for transfers between devices  17.2 us (25%)
  starting transfers between devices  12.9 us (19%)
  local copies, waits for them, and re-layouts  7.22 us (11%)
  other arithmetic  3.53 us (5%)
    all_to_all x1, waiting for transfers between devices, shards(): lax.all_to_all(taken, ('rows', 'cols'), split_axis=0, concat_axis=0, tile...  17.2 us
    pallas_call x1, Pallas kernels, filtered_partials(): pl.pallas_call(filter_kernel(block_count, coarse_block, value_rows, total...  16.6 us
    pallas_call x1, Pallas kernels, pick_cells(): pl.pallas_call(pick_kernel(group_steps, step, chunk, owner_len, pack), ou...  10.2 us
    all_to_all x1, starting transfers between devices, shards(): lax.all_to_all(copies, ('rows', 'cols'), split_axis=0, concat_axis=0, til...  7.1 us
    all_to_all x1, starting transfers between devices, shards(): lax.all_to_all(taken, ('rows', 'cols'), split_axis=0, concat_axis=0, tile...  5.84 us
    unnamed x5, local copies, waits for them, and re-layouts  1.49 us
  transfers between devices with their start and end apart: 2, of which 1 were waited for; matrix products, arithmetic and copies ran while one was open for 5% of the time, Pallas kernels for 24%

profile of v23, /device:TPU:1, one launch (start us, length us, event | category | flops | bytes accessed | tf_op | source)
XLA Modules:
  0.0 67.9 jit_solution(83273493082258969)
XLA Ops:
  0.0 0.0 copy-start
  0.0 0.7 %copy-done = s32[1,32,4]{1,2,0:T(4,128)S(1)} copy-done((s32[1,32,4]{1,2,0:T(4,128)S(1)}, s32[1,32,4]{1,2,0:T(4,128)}, u32[]{:S(2)}) %copy-start) | copy-done | bytes 536
  0.7 0.7 %reshape.228 = s32[32,1,128]{2,1,0:T(1,128)} reshape(s32[32,4,32]{2,1,0:T(4,128)S(1)} %broadcast_bitcast_fusion) | data formatting | bytes 32768
  1.4 7.1 %all-to-all-start = ((s32[32,1,128]{2,1,0:T(1,128)}), s32[32,1,128]{2,1,0:T(1,128)S(1)}, u32[]{:S(2)}, u32[]{:S(2)}) async-start(s32[32,1,128]{2,1,0:T(1,128)} %reshape.228), calls=%async_computation | async-start | bytes 32768 | tf_op jit(solution)/shard_map/all_to_all | solution.py:247
  8.5 0.8 %dynamic-slice_bitcast_fusion.3 = (f32[1,7,8]{2,0,1:T(1,128)S(1)}, f32[1,7,8]{2,0,1:T(1,128)S(1)}) fusion(f32[8,2,7,8]{3,0,2,1:T(8,128)} %constant.113.clone, s32[]{:T(128)S(6)} %select_n.64, s32[]{:T(128)S(6)} %add.64), kind=kLoop, calls=%fused_computation.57 | loop fusion | bytes 904 | tf_op jit(solution)/shard_map/slice | solution.py:256
  9.3 0.7 %dynamic-slice_bitcast_fusion = (f32[1,10,32]{2,1,0:T(8,128)S(1)}, f32[1,10,32]{2,1,0:T(8,128)S(1)}) fusion(f32[4,2,10,32]{3,2,1,0:T(8,128)} %constant.114.clone, s32[]{:T(128)S(6)} %select_n.65, s32[]{:T(128)S(6)} %add.64), kind=kLoop, calls=%fused_computation.54 | loop fusion | bytes 5128 | tf_op jit(solution)/shard_map/slice | solution.py:257
  10.1 0.1 broadcast_multiply_fusion
  10.2 0.3 mul.94
  10.5 0.1 copy.32
  10.6 0.1 concatenate.46
  10.8 0.7 %pad_maximum_fusion.1.w_ref = bf16[2,216,256]{2,1,0:T(8,128)(2,1)} fusion(bf16[1,216,256]{2,1,0:T(8,128)(2,1)S(1)} %subtract_convert_fusion, bf16[1,216,256]{2,1,0:T(8,128)(2,1)S(1)} %fusion), kind=kLoop, calls=%fused_computation.2 | loop fusion | flops 110592 | bytes 442368 | tf_op jit(solution)/shard_map/stack | solution.py:80
  11.5 16.6 %shard_map.64 = (f32[12,144,512]{2,1,0:T(8,128)}, f32[12,72,512]{2,1,0:T(8,128)}) custom-call(bf16[12,256,4096]{2,1,0:T(8,128)(2,1)} %bitcast.57, bf16[1024,256]{1,0:T(8,128)(2,1)} %constant.115.clone.main_ref, bf16[256,256]{1,0:T(8,128)(2,1)} %constant.116.clone.halo_ref, bf16[2,216,256]{2,1,0:T(8,128)(2,1)} %pad_maximum_fusion.1.w_ref), custom_call_target="tpu_custom_call" | custom-call | tf_op jit(solution)/shard_map/pallas_call | solution.py:98
  28.1 0.0 all-to-all-done
  28.1 0.5 broadcast.67
  28.6 0.7 %reduce.2 = s32[32,128]{1,0:T(8,128)S(1)} reduce(s32[32,1,128]{2,1,0:T(1,128)S(1)} %all-to-all-done, s32[]{:T(128)} %broadcast.67), dimensions={1}, to_apply=%all_to_all.6.reduce_sub_computation | reduce | bytes 32772 | tf_op jit(solution)/shard_map/all_to_all | solution.py:247
  29.3 0.1 reshape.229
  29.4 0.5 fusion.9
  29.9 0.5 copy.33
  30.4 0.9 %reshape.226.sel_ref = s32[1,4096]{1,0:T(1,128)} reshape(s32[32,32,4]{2,1,0:T(8,128)S(1)} %copy.33) | data formatting | bytes 32768 | tf_op jit(solution)/shard_map/reshape | solution.py:275
  31.4 0.5 copy.30
  31.9 0.9 %reshape.224.idx_ref = s32[4096]{0:T(1024)} reshape(s32[32,32,4]{2,1,0:T(8,128)S(1)} %copy.30) | data formatting | bytes 32768 | tf_op jit(solution)/shard_map/reshape | solution.py:278
  32.8 10.2 %shard_map.65 = f32[32,36,128]{2,1,0:T(8,128)} custom-call(s32[4096]{0:T(1024)} %reshape.224.idx_ref, f32[12,144,512]{2,1,0:T(8,128)} %get-tuple-element.7.xv_ref, f32[12,72,512]{2,1,0:T(8,128)} %get-tuple-element.8.xs_ref, s32[1,4096]{1,0:T(1,128)} %reshape.226.sel_ref), custom_call_target="tpu_custom_call" | custom-call | tf_op jit(solution)/shard_map/pallas_call | solution.py:202
  43.0 5.8 %all-to-all-start.1 = ((f32[32,36,128]{2,1,0:T(8,128)}), f32[32,36,128]{2,1,0:T(8,128)S(1)}, u32[]{:S(2)}, u32[]{:S(2)}) async-start(f32[32,36,128]{2,1,0:T(8,128)} %shard_map.65), calls=%async_computation.1 | async-start | bytes 1310720 | tf_op jit(solution)/shard_map/all_to_all | solution.py:279
  48.9 0.7 %fusion.14 = pred[32,4]{1,0:T(8,128)(4,1)S(1)} fusion(s32[32,32,4]{1,2,0:T(4,128)S(1)} %bitcast.58, s32[]{:T(128)S(6)} %select_n.55), kind=kLoop, calls=%fused_computation.45 | loop fusion | flops 128 | bytes 644 | tf_op jit(solution)/shard_map/ge | solution.py:283
  49.6 0.1 ge.23
  49.7 17.2 %all-to-all-done.1 = f32[32,36,128]{2,1,0:T(8,128)S(1)} async-done(((f32[32,36,128]{2,1,0:T(8,128)}), f32[32,36,128]{2,1,0:T(8,128)S(1)}, u32[]{:S(2)}, u32[]{:S(2)}) %all-to-all-start.1) | async-done | bytes 589856 | tf_op jit(solution)/shard_map/all_to_all | solution.py:279
  66.9 0.1 reduce_sum.72
  67.1 0.1 multiply_reduce_fusion
  67.1 0.2 concatenate.55
  67.3 0.6 multiply_convert_fusion
  (16 shorter events, 0.2 us)
Async XLA Ops:
  0.0 0.7 %copy-start = (s32[1,32,4]{1,2,0:T(4,128)S(1)}, s32[1,32,4]{1,2,0:T(4,128)}, u32[]{:S(2)}) copy-start(s32[1,32,4]{1,2,0:T(4,128)} %param.7) | copy-start | bytes 1540
  1.4 26.7 %all-to-all-start = ((s32[32,1,128]{2,1,0:T(1,128)}), s32[32,1,128]{2,1,0:T(1,128)S(1)}, u32[]{:S(2)}, u32[]{:S(2)}) async-start(s32[32,1,128]{2,1,0:T(1,128)} %reshape.228), calls=%async_computation | async-start | bytes 32768 | tf_op jit(solution)/shard_map/all_to_all | solution.py:247
  43.0 23.9 %all-to-all-start.1 = ((f32[32,36,128]{2,1,0:T(8,128)}), f32[32,36,128]{2,1,0:T(8,128)S(1)}, u32[]{:S(2)}, u32[]{:S(2)}) async-start(f32[32,36,128]{2,1,0:T(8,128)} %shard_map.65), calls=%async_computation.1 | async-start | bytes 1310720 | tf_op jit(solution)/shard_map/all_to_all | solution.py:279

commit v24 on v21

--- a/solution.py
+++ b/solution.py
@@ -179,7 +179,7 @@
     return body
 
 
-def pick_cells(xv, xs, flat, sel, owner_len, pack, chunk=4096):
+def pick_cells(xv, xs, flat, sel, owner_len, pack, chunk=2048):
     fields, groups, lanes = xs.shape
     rows = fields * 3
     step = 8

time: 67.4 us -> 67.4 us (level)
  no operation moved by 1% of the time
where the time goes in v24:
time: 67.4 us; the launch traced here: 66.8 us
  Pallas kernels  25.7 us (38%)
  waiting for transfers between devices  17.2 us (26%)
  starting transfers between devices  12.9 us (19%)
  local copies, waits for them, and re-layouts  7.22 us (11%)
  other arithmetic  3.53 us (5%)
    all_to_all x1, waiting for transfers between devices, shards(): lax.all_to_all(taken, ('rows', 'cols'), split_axis=0, concat_axis=0, tile...  17.2 us
    pallas_call x1, Pallas kernels, filtered_partials(): pl.pallas_call(filter_kernel(block_count, coarse_block, value_rows, total...  15.5 us
    pallas_call x1, Pallas kernels, pick_cells(): pl.pallas_call(pick_kernel(group_steps, step, chunk, owner_len, pack), ou...  10.2 us
    all_to_all x1, starting transfers between devices, shards(): lax.all_to_all(copies, ('rows', 'cols'), split_axis=0, concat_axis=0, til...  7.1 us
    all_to_all x1, starting transfers between devices, shards(): lax.all_to_all(taken, ('rows', 'cols'), split_axis=0, concat_axis=0, tile...  5.83 us
    unnamed x5, local copies, waits for them, and re-layouts  1.49 us
  transfers between devices with their start and end apart: 2, of which 1 were waited for; matrix products, arithmetic and copies ran while one was open for 6% of the time, Pallas kernels for 23%

profile of v24, /device:TPU:1, one launch (start us, length us, event | category | flops | bytes accessed | tf_op | source)
XLA Modules:
  0.0 66.8 jit_solution(13275742908441903225)
XLA Ops:
  0.0 0.0 copy-start
  0.0 0.7 %copy-done = s32[1,32,4]{1,2,0:T(4,128)S(1)} copy-done((s32[1,32,4]{1,2,0:T(4,128)S(1)}, s32[1,32,4]{1,2,0:T(4,128)}, u32[]{:S(2)}) %copy-start) | copy-done | bytes 536
  0.7 0.7 %reshape.228 = s32[32,1,128]{2,1,0:T(1,128)} reshape(s32[32,4,32]{2,1,0:T(4,128)S(1)} %broadcast_bitcast_fusion) | data formatting | bytes 32768
  1.4 7.1 %all-to-all-start = ((s32[32,1,128]{2,1,0:T(1,128)}), s32[32,1,128]{2,1,0:T(1,128)S(1)}, u32[]{:S(2)}, u32[]{:S(2)}) async-start(s32[32,1,128]{2,1,0:T(1,128)} %reshape.228), calls=%async_computation | async-start | bytes 32768 | tf_op jit(solution)/shard_map/all_to_all | solution.py:247
  8.5 0.8 %dynamic-slice_bitcast_fusion.3 = (f32[1,7,8]{2,0,1:T(1,128)S(1)}, f32[1,7,8]{2,0,1:T(1,128)S(1)}) fusion(f32[8,2,7,8]{3,0,2,1:T(8,128)} %constant.113.clone, s32[]{:T(128)S(6)} %select_n.64, s32[]{:T(128)S(6)} %add.64), kind=kLoop, calls=%fused_computation.57 | loop fusion | bytes 904 | tf_op jit(solution)/shard_map/slice | solution.py:256
  9.3 0.7 %dynamic-slice_bitcast_fusion = (f32[1,10,32]{2,1,0:T(8,128)S(1)}, f32[1,10,32]{2,1,0:T(8,128)S(1)}) fusion(f32[4,2,10,32]{3,2,1,0:T(8,128)} %constant.114.clone, s32[]{:T(128)S(6)} %select_n.65, s32[]{:T(128)S(6)} %add.64), kind=kLoop, calls=%fused_computation.54 | loop fusion | bytes 5128 | tf_op jit(solution)/shard_map/slice | solution.py:257
  10.1 0.1 broadcast_multiply_fusion
  10.2 0.3 mul.94
  10.5 0.1 copy.32
  10.6 0.1 concatenate.46
  10.8 0.7 %pad_maximum_fusion.1.w_ref = bf16[2,216,256]{2,1,0:T(8,128)(2,1)} fusion(bf16[1,216,256]{2,1,0:T(8,128)(2,1)S(1)} %subtract_convert_fusion, bf16[1,216,256]{2,1,0:T(8,128)(2,1)S(1)} %fusion), kind=kLoop, calls=%fused_computation.2 | loop fusion | flops 110592 | bytes 442368 | tf_op jit(solution)/shard_map/stack | solution.py:80
  11.5 15.5 %shard_map.64 = (f32[12,144,512]{2,1,0:T(8,128)}, f32[12,72,512]{2,1,0:T(8,128)}) custom-call(bf16[12,256,4096]{2,1,0:T(8,128)(2,1)} %bitcast.57, bf16[1024,256]{1,0:T(8,128)(2,1)} %constant.115.clone.main_ref, bf16[256,256]{1,0:T(8,128)(2,1)} %constant.116.clone.halo_ref, bf16[2,216,256]{2,1,0:T(8,128)(2,1)} %pad_maximum_fusion.1.w_ref), custom_call_target="tpu_custom_call" | custom-call | tf_op jit(solution)/shard_map/pallas_call | solution.py:98
  27.0 0.0 all-to-all-done
  27.0 0.5 broadcast.67
  27.5 0.7 %reduce.2 = s32[32,128]{1,0:T(8,128)S(1)} reduce(s32[32,1,128]{2,1,0:T(1,128)S(1)} %all-to-all-done, s32[]{:T(128)} %broadcast.67), dimensions={1}, to_apply=%all_to_all.6.reduce_sub_computation | reduce | bytes 32772 | tf_op jit(solution)/shard_map/all_to_all | solution.py:247
  28.2 0.1 reshape.229
  28.3 0.5 fusion.9
  28.8 0.5 copy.33
  29.4 0.9 %reshape.226.sel_ref = s32[1,4096]{1,0:T(1,128)} reshape(s32[32,32,4]{2,1,0:T(8,128)S(1)} %copy.33) | data formatting | bytes 32768 | tf_op jit(solution)/shard_map/reshape | solution.py:275
  30.3 0.5 copy.30
  30.9 0.9 %reshape.224.idx_ref = s32[4096]{0:T(1024)} reshape(s32[32,32,4]{2,1,0:T(8,128)S(1)} %copy.30) | data formatting | bytes 32768 | tf_op jit(solution)/shard_map/reshape | solution.py:278
  31.7 10.2 %shard_map.65 = f32[32,36,128]{2,1,0:T(8,128)} custom-call(s32[4096]{0:T(1024)} %reshape.224.idx_ref, f32[12,144,512]{2,1,0:T(8,128)} %get-tuple-element.7.xv_ref, f32[12,72,512]{2,1,0:T(8,128)} %get-tuple-element.8.xs_ref, s32[1,4096]{1,0:T(1,128)} %reshape.226.sel_ref), custom_call_target="tpu_custom_call" | custom-call | tf_op jit(solution)/shard_map/pallas_call | solution.py:202
  41.9 5.8 %all-to-all-start.1 = ((f32[32,36,128]{2,1,0:T(8,128)}), f32[32,36,128]{2,1,0:T(8,128)S(1)}, u32[]{:S(2)}, u32[]{:S(2)}) async-start(f32[32,36,128]{2,1,0:T(8,128)} %shard_map.65), calls=%async_computation.1 | async-start | bytes 1310720 | tf_op jit(solution)/shard_map/all_to_all | solution.py:279
  47.8 0.7 %fusion.14 = pred[32,4]{1,0:T(8,128)(4,1)S(1)} fusion(s32[32,32,4]{1,2,0:T(4,128)S(1)} %bitcast.58, s32[]{:T(128)S(6)} %select_n.55), kind=kLoop, calls=%fused_computation.45 | loop fusion | flops 128 | bytes 644 | tf_op jit(solution)/shard_map/ge | solution.py:283
  48.5 0.1 ge.23
  48.6 17.2 %all-to-all-done.1 = f32[32,36,128]{2,1,0:T(8,128)S(1)} async-done(((f32[32,36,128]{2,1,0:T(8,128)}), f32[32,36,128]{2,1,0:T(8,128)S(1)}, u32[]{:S(2)}, u32[]{:S(2)}) %all-to-all-start.1) | async-done | bytes 589856 | tf_op jit(solution)/shard_map/all_to_all | solution.py:279
  65.8 0.1 reduce_sum.72
  66.0 0.1 multiply_reduce_fusion
  66.0 0.2 concatenate.55
  66.2 0.6 multiply_convert_fusion
  (16 shorter events, 0.2 us)
Async XLA Ops:
  0.0 0.7 %copy-start = (s32[1,32,4]{1,2,0:T(4,128)S(1)}, s32[1,32,4]{1,2,0:T(4,128)}, u32[]{:S(2)}) copy-start(s32[1,32,4]{1,2,0:T(4,128)} %param.7) | copy-start | bytes 1540
  1.4 25.6 %all-to-all-start = ((s32[32,1,128]{2,1,0:T(1,128)}), s32[32,1,128]{2,1,0:T(1,128)S(1)}, u32[]{:S(2)}, u32[]{:S(2)}) async-start(s32[32,1,128]{2,1,0:T(1,128)} %reshape.228), calls=%async_computation | async-start | bytes 32768 | tf_op jit(solution)/shard_map/all_to_all | solution.py:247
  41.9 23.9 %all-to-all-start.1 = ((f32[32,36,128]{2,1,0:T(8,128)}), f32[32,36,128]{2,1,0:T(8,128)S(1)}, u32[]{:S(2)}, u32[]{:S(2)}) async-start(f32[32,36,128]{2,1,0:T(8,128)} %shard_map.65), calls=%async_computation.1 | async-start | bytes 1310720 | tf_op jit(solution)/shard_map/all_to_all | solution.py:279
